TPU v7x, 128 devices: a whole 4x4x4 slice. The times are simulated.
128 devices in a mesh: coil: 8 (over y, x_hi), pencil: 16 (over z, x_lo, core).
Axes of the slice: x: 4 (x_hi: 2, x_lo: 2; x = x_hi * 2 + x_lo), y: 4, z: 4, core: 2. Of those that a mesh axis runs over, the one named last changes fastest.
Arguments:
- object_image: bfloat16 [32, 256, 1024], P(None, 'pencil'), may hold values from -6 to 6
- coil_maps: bfloat16 [64, 32, 256, 1024], P('coil', None, 'pencil'), may hold values from -0.75 to 0.75
- sample_mask: int32 [32, 256, 4], replicated, may hold values 0 or 1
Outputs:
- adjoint_image: float32 [32, 256, 1024], P('coil', 'pencil')
Inputs may be any that keep to these rules, and one draw needn't show every extreme that they name: `sample_mask`: 1 where the 128 readout samples of a segment are acquired.
All inputs are finite; a program needn't handle non-finite values.
Results may differ from a plain program's by a relative error of at most 0.01.
Values may be sent and summed in bfloat16 or wider, within the bound.
No kernel may reach another device: no remote copies, remote signals or barrier semaphores. Data moves between devices by JAX's collectives and lax.ppermute only.
A program may use at most 192 MiB of HBM per device.

v0:
```python
import math

import jax
import jax.numpy as jnp
from jax import lax
from jax.sharding import PartitionSpec as P


def dft_tables(length, direction):
    indices = jnp.arange(length, dtype=jnp.int32)
    phases = indices[:, None] * indices[None, :] % length
    angles = phases.astype(jnp.float32) * (2.0 * math.pi / length)
    factor = 1.0 / math.sqrt(length)
    cosine = (jnp.cos(angles) * factor).astype(jnp.bfloat16)
    sine_part = (direction * jnp.sin(angles) * factor).astype(jnp.bfloat16)
    return (cosine, sine_part)


def readout_table(length, direction):
    cosine, sine_part = dft_tables(length, direction)
    upper = jnp.concatenate([cosine, sine_part], axis=1)
    lower = jnp.concatenate([-sine_part, cosine], axis=1)
    return jnp.concatenate([upper, lower], axis=0)


def complex_product(left_side, right_side, readout, conjugate):
    left_full = left_side.astype(jnp.float32)
    right_full = right_side.astype(jnp.float32)
    left_real = left_full[..., :readout]
    left_imag = left_full[..., readout:]
    if conjugate:
        left_imag = -left_imag
    right_real = right_full[..., :readout]
    right_imag = right_full[..., readout:]
    real_part = left_real * right_real - left_imag * right_imag
    imag_part = left_real * right_imag + left_imag * right_real
    return jnp.concatenate([real_part, imag_part], axis=-1)


def transform(volume, tables, formula, readout):
    cosine, sine_part = tables
    direct = jnp.einsum(formula, cosine, volume, preferred_element_type=jnp.float32)
    crossed = jnp.einsum(formula, sine_part, volume, preferred_element_type=jnp.float32)
    turned = jnp.concatenate([-crossed[..., readout:], crossed[..., :readout]], axis=-1)
    return (direct + turned).astype(jnp.bfloat16)


def widen(mask_part, segment):
    flags = jnp.repeat(mask_part, segment, axis=2) > 0
    return jnp.concatenate([flags, flags], axis=2)


def on_device(object_image, coil_maps, sample_mask):
    readout = object_image.shape[2] // 2
    slices = object_image.shape[0]
    row_count = object_image.shape[1]
    pencils = lax.axis_size("pencil")
    depth = slices // pencils
    lines = row_count * pencils
    segment = readout // sample_mask.shape[2]
    position = lax.axis_index("pencil")
    forward_x = readout_table(readout, -1.0)
    inverse_x = readout_table(readout, 1.0)
    forward_z = dft_tables(slices, -1.0)
    inverse_z = dft_tables(slices, 1.0)
    forward_y = dft_tables(lines, -1.0)
    inverse_y = dft_tables(lines, 1.0)
    column_mask = widen(lax.dynamic_slice_in_dim(sample_mask, position * depth, depth, 0), segment)
    nothing = jnp.zeros((), jnp.bfloat16)
    coil_image = complex_product(coil_maps, object_image[None], readout, False).astype(jnp.bfloat16)
    volume = jnp.dot(coil_image, forward_x, preferred_element_type=jnp.float32).astype(jnp.bfloat16)
    volume = transform(volume, forward_z, "kz,czyx->ckyx", readout)
    spectrum = transform(
        lax.all_to_all(volume, "pencil", split_axis=1, concat_axis=2, tiled=True),
        forward_y,
        "ky,czyx->czkx",
        readout,
    )
    spectrum = jnp.where(column_mask, spectrum, nothing)
    spectrum = transform(spectrum, inverse_y, "ky,czyx->czkx", readout)
    coil_block = lax.all_to_all(spectrum, "pencil", split_axis=2, concat_axis=1, tiled=True)
    coil_block = transform(coil_block, inverse_z, "kz,czyx->ckyx", readout)
    returned = jnp.dot(coil_block, inverse_x, preferred_element_type=jnp.float32).astype(
        jnp.bfloat16
    )
    partial_sum = jnp.sum(complex_product(coil_maps, returned, readout, True), axis=0)
    summed = lax.psum(partial_sum.astype(jnp.bfloat16), "coil").astype(jnp.float32)
    share_rows = slices // lax.axis_size("coil")
    return lax.dynamic_slice_in_dim(summed, lax.axis_index("coil") * share_rows, share_rows, 0)


def solution(mesh):
    placed = (P(None, "pencil", None), P("coil", None, "pencil", None), P())
    return jax.shard_map(
        on_device, mesh=mesh, in_specs=placed, out_specs=P("coil", "pencil", None), check_vma=False
    )
```

profile of v0, /device:TPU:0, one launch (start us, length us, event | category | flops | bytes accessed | tf_op | source)
XLA Modules:
  0.0 600.3 jit_solution(16223874633150782746)
XLA Ops:
  14.9 11.5 %convert_element_type.120 = f32[8,32,16,1024]{3,2,1,0:T(8,128)} convert(bf16[8,32,16,1024]{3,2,1,0:T(8,128)(2,1)} %param.4) | non-fusion elementwise | flops 4194304 | bytes 25165824 | tf_op jit(solution)/shard_map/convert_element_type | solution.py:27
  26.9 7.5 %subtract_convert_fusion = (bf16[8,32,16,512]{3,2,1,0:T(8,128)(2,1)S(1)}, bf16[8,32,16,512]{3,2,1,0:T(8,128)(2,1)S(1)}) fusion(f32[8,32,16,1024]{3,2,1,0:T(8,128)} %convert_element_type.120, f32[32,16,512]{2,1,0:T(8,128)S(1)} %get-tuple-element.18, f32[32,16,512]{2,1,0:T(8,128)S(1)} %get-tuple-element.17), kind=kLoop, calls=%fused_computation.27 | loop fusion | flops 16777216 | bytes 27262976 | tf_op jit(solution)/shard_map/convert.1
  34.4 11.5 %fusion.14 = bf16[8,32,16,1024]{3,2,1,0:T(8,128)(2,1)} fusion(bf16[8,32,16,512]{3,2,1,0:T(8,128)(2,1)S(1)} %get-tuple-element.8, bf16[8,32,16,512]{3,2,1,0:T(8,128)(2,1)S(1)} %get-tuple-element.7, bf16[512,512]{1,0:T(8,128)(2,1)S(1)} %get-tuple-element.20, bf16[512,512]{1,0:T(8,128)(2,1)S(1)} %fusion.42, bf16[512,512]{1,0:T(8,128)(2,1)S(1)} %get-tuple-element.19), kind=kOutput, calls=%fused_computation.31 | convolution fusion | flops 8619294720 | bytes 18350080 | tf_op jit(solution)/shard_map/dot_general | solution.py:71
  45.9 15.0 %convolution_bitcast_fusion.1 = f32[8,32,16,1024]{3,1,2,0:T(8,128)S(1)} fusion(bf16[8,32,16,1024]{3,2,1,0:T(8,128)(2,1)} %fusion.14), kind=kOutput, calls=%fused_computation.10 | convolution fusion | flops 268451840 | bytes 25165824 | tf_op jit(solution)/shard_map/kz,czyx->ckyx/dot_general | solution.py:43
  61.0 6.8 %slice_negate_fusion.3 = (f32[8,32,16,512]{3,1,2,0:T(8,128)}, f32[8,32,16,512]{3,1,2,0:T(8,128)}) fusion(f32[8,32,16,1024]{3,1,2,0:T(8,128)S(1)} %convolution_bitcast_fusion.1), kind=kLoop, calls=%fused_computation.16 | loop fusion | flops 2097152 | bytes 33554432 | tf_op jit(solution)/shard_map/neg | solution.py:44
  67.8 26.7 %fusion = bf16[8,32,16,1024]{3,1,2,0:T(8,128)(2,1)} fusion(f32[8,32,16,512]{3,1,2,0:T(8,128)} %get-tuple-element.16, f32[8,32,16,512]{3,1,2,0:T(8,128)} %get-tuple-element.15, bf16[8,32,16,1024]{3,2,1,0:T(8,128)(2,1)} %fusion.14), kind=kOutput, calls=%fused_computation.1 | convolution fusion | flops 281034752 | bytes 33554432 | tf_op jit(solution)/shard_map/kz,czyx->ckyx/dot_general | solution.py:42
  94.5 11.3 %copy.28 = bf16[8,32,16,1024]{3,2,0,1:T(8,128)(2,1)} copy(bf16[8,32,16,1024]{3,1,2,0:T(8,128)(2,1)} %fusion) | data formatting | bytes 16777216 | tf_op jit(solution)/shard_map/convert_element_type | solution.py:45
  105.8 6.9 %all-to-all-start = ((bf16[8,32,16,1024]{3,2,0,1:T(8,128)(2,1)}), bf16[8,32,16,1024]{3,2,0,1:T(8,128)(2,1)}, u32[]{:S(2)}, u32[]{:S(2)}) async-start(bf16[8,32,16,1024]{3,2,0,1:T(8,128)(2,1)} %copy.28), calls=%async_computation | async-start | bytes 16777216 | tf_op jit(solution)/shard_map/all_to_all | solution.py:74
  113.6 94.4 %all-to-all-done = bf16[8,32,16,1024]{3,2,0,1:T(8,128)(2,1)} async-done(((bf16[8,32,16,1024]{3,2,0,1:T(8,128)(2,1)}), bf16[8,32,16,1024]{3,2,0,1:T(8,128)(2,1)}, u32[]{:S(2)}, u32[]{:S(2)}) %all-to-all-start) | async-done | bytes 8388640 | tf_op jit(solution)/shard_map/all_to_all | solution.py:74
  208.0 8.5 %copy.30 = bf16[8,2,16,16,1024]{4,3,2,1,0:T(8,128)(2,1)} copy(bf16[8,2,16,16,1024]{4,3,0,1,2:T(8,128)(2,1)} %bitcast.15) | data formatting | bytes 16777216 | tf_op jit(solution)/shard_map/all_to_all | solution.py:74
  229.6 13.8 %fusion.1 = bf16[8,2,256,1024]{2,3,1,0:T(8,128)(2,1)} fusion(f32[8,2,256,512]{2,3,1,0:T(8,128)} %get-tuple-element.14, f32[8,2,256,512]{2,3,1,0:T(8,128)} %get-tuple-element.13, bf16[8,2,256,1024]{3,2,1,0:T(8,128)(2,1)} %bitcast.80), kind=kOutput, calls=%fused_computation.3 | convolution fusion | flops 2161115136 | bytes 33554432 | tf_op jit(solution)/shard_map/ky,czyx->czkx/dot_general | solution.py:42
  250.0 6.9 %slice_negate_fusion.1 = (f32[8,2,256,512]{2,3,1,0:T(8,128)}, f32[8,2,256,512]{2,3,1,0:T(8,128)}) fusion(f32[8,2,256,1024]{2,3,1,0:T(8,128)S(1)} %convolution_bitcast_fusion.2), kind=kLoop, calls=%fused_computation.14 | loop fusion | flops 2097152 | bytes 33554432 | tf_op jit(solution)/shard_map/neg | solution.py:44
  256.9 13.7 %fusion.2 = bf16[8,2,256,1024]{2,3,1,0:T(8,128)(2,1)} fusion(f32[8,2,256,512]{2,3,1,0:T(8,128)} %get-tuple-element.12, f32[8,2,256,512]{2,3,1,0:T(8,128)} %get-tuple-element.11, bf16[8,2,256,1024]{2,3,1,0:T(8,128)(2,1)} %fusion.1, pred[2,256,1024]{1,2,0:T(8,128)(4,1)S(1)} %pad_add_fusion), kind=kOutput, calls=%fused_computation.5 | convolution fusion | flops 2165309440 | bytes 34078720 | tf_op jit(solution)/shard_map/ky,czyx->czkx/dot_general | solution.py:42
  270.6 21.2 %copy.33 = bf16[8,2,256,1024]{3,1,0,2:T(2,128)(2,1)} copy(bf16[8,2,256,1024]{2,3,1,0:T(8,128)(2,1)} %fusion.2) | data formatting | bytes 16777216 | tf_op jit(solution)/shard_map/convert_element_type | solution.py:45
  304.6 87.2 %all-to-all-done.1 = bf16[8,2,256,1024]{3,1,0,2:T(2,128)(2,1)} async-done(((bf16[8,2,256,1024]{3,1,0,2:T(2,128)(2,1)}), bf16[8,2,256,1024]{3,1,0,2:T(2,128)(2,1)}, u32[]{:S(2)}, u32[]{:S(2)}) %all-to-all-start.1) | async-done | bytes 8388640 | tf_op jit(solution)/shard_map/all_to_all | solution.py:81
  391.8 11.3 %copy.34 = bf16[8,2,256,1024]{3,2,1,0:T(8,128)(2,1)} copy(bf16[8,2,256,1024]{3,1,0,2:T(2,128)(2,1)} %all-to-all-done.1) | data formatting | bytes 16777216 | tf_op jit(solution)/shard_map/all_to_all | solution.py:81
  403.1 16.3 %copy.35 = bf16[8,16,2,16,1024]{4,2,1,3,0:T(2,128)(2,1)} copy(bf16[8,16,2,16,1024]{4,3,1,2,0:T(8,128)(2,1)} %bitcast.81) | data formatting | bytes 16777216 | tf_op jit(solution)/shard_map/all_to_all | solution.py:81
  419.5 13.2 %all_to_all.33 = bf16[8,32,16,1024]{3,1,2,0:T(8,128)(2,1)} reshape(bf16[8,16,2,16,1024]{4,2,1,3,0:T(2,128)(2,1)} %copy.35) | data formatting | bytes 16777216 | tf_op jit(solution)/shard_map/all_to_all | solution.py:81
  438.4 6.8 %slice_negate_fusion = (f32[8,32,16,512]{3,1,2,0:T(8,128)}, f32[8,32,16,512]{3,1,2,0:T(8,128)}) fusion(f32[8,32,16,1024]{3,1,2,0:T(8,128)S(1)} %convolution_bitcast_fusion), kind=kLoop, calls=%fused_computation.13 | loop fusion | flops 2097152 | bytes 33554432 | tf_op jit(solution)/shard_map/neg | solution.py:44
  445.2 12.0 %fusion.3 = bf16[8,32,16,1024]{3,1,2,0:T(8,128)(2,1)} fusion(f32[8,32,16,512]{3,1,2,0:T(8,128)} %get-tuple-element.10, f32[8,32,16,512]{3,1,2,0:T(8,128)} %get-tuple-element.9, bf16[8,32,16,1024]{3,1,2,0:T(8,128)(2,1)} %all_to_all.33), kind=kOutput, calls=%fused_computation.7 | convolution fusion | flops 281034752 | bytes 33554432 | tf_op jit(solution)/shard_map/kz,czyx->ckyx/dot_general | solution.py:42
  457.3 17.3 %convert_convert_fusion = f32[8,32,16,1024]{3,2,1,0:T(8,128)} fusion(bf16[8,32,16,1024]{3,1,2,0:T(8,128)(2,1)} %fusion.3, bf16[512,512]{1,0:T(8,128)(2,1)S(1)} %get-tuple-element.20, bf16[512,512]{1,0:T(8,128)(2,1)S(1)} %fusion.43, bf16[512,512]{1,0:T(8,128)(2,1)S(1)} %multiply_convert_fusion), kind=kOutput, calls=%fused_computation.25 | convolution fusion | flops 8606711808 | bytes 26738688 | tf_op jit(solution)/shard_map/dot_general | solution.py:83
  474.6 18.5 %multiply_subtract_fusion = (f32[8,32,16,512]{3,2,1,0:T(8,128)}, f32[8,32,16,512]{3,2,1,0:T(8,128)}) fusion(f32[8,32,16,1024]{3,2,1,0:T(8,128)} %convert_convert_fusion, f32[8,32,16,1024]{3,2,1,0:T(8,128)} %convert_element_type.120), kind=kLoop, calls=%fused_computation.24 | loop fusion | flops 14680064 | bytes 50331648 | tf_op jit(solution)/shard_map/sub | solution.py:35
  493.0 7.9 %maximum_reduce_fusion = bf16[32,16,1024]{2,1,0:T(8,128)(2,1)} fusion(f32[8,32,16,512]{3,2,1,0:T(8,128)} %get-tuple-element.6, f32[8,32,16,512]{3,2,1,0:T(8,128)} %get-tuple-element.5), kind=kLoop, calls=%fused_computation.8 | loop fusion | flops 7864320 | bytes 17825792 | tf_op jit(solution)/shard_map/reduce_sum | solution.py:86
  501.0 90.6 %all-reduce.2.cloned.1.call-done = bf16[32,16,1024]{2,1,0:T(8,128)(2,1)} async-done(((bf16[32,16,1024]{2,1,0:T(8,128)(2,1)}), bf16[32,16,1024]{2,1,0:T(8,128)(2,1)}) %all-reduce.2.cloned.1.call-update) | async-done | bytes 1048592 | tf_op jit(solution)/shard_map/psum | solution.py:87
  (19 shorter events, 49.7 us)
Async XLA Ops:
  14.9 11.5 %copy-start = (bf16[32,16,1024]{2,1,0:T(8,128)(2,1)S(1)}, bf16[32,16,1024]{2,1,0:T(8,128)(2,1)}, u32[]{:S(2)}) copy-start(bf16[32,16,1024]{2,1,0:T(8,128)(2,1)} %param.3) | copy-start | bytes 3145732
  105.8 102.2 %all-to-all-start = ((bf16[8,32,16,1024]{3,2,0,1:T(8,128)(2,1)}), bf16[8,32,16,1024]{3,2,0,1:T(8,128)(2,1)}, u32[]{:S(2)}, u32[]{:S(2)}) async-start(bf16[8,32,16,1024]{3,2,0,1:T(8,128)(2,1)} %copy.28), calls=%async_computation | async-start | bytes 16777216 | tf_op jit(solution)/shard_map/all_to_all | solution.py:74
  291.8 100.1 %all-to-all-start.1 = ((bf16[8,2,256,1024]{3,1,0,2:T(2,128)(2,1)}), bf16[8,2,256,1024]{3,1,0,2:T(2,128)(2,1)}, u32[]{:S(2)}, u32[]{:S(2)}) async-start(bf16[8,2,256,1024]{3,1,0,2:T(2,128)(2,1)} %copy.33), calls=%async_computation.1 | async-start | bytes 16777216 | tf_op jit(solution)/shard_map/all_to_all | solution.py:81
  296.5 295.1 %all-reduce.2.cloned.1.call-start = ((), (), s32[]{:S(2)}) async-start(), calls=%async_computation.2 | async-start | bytes 2097152 | tf_op jit(solution)/shard_map/psum | solution.py:87
Sparse Core Ops, SparseCore 0:
  501.1 90.4 all-reduce.1
where the time goes:
time: 608 us; the launch traced here: 600 us
  waiting for transfers between devices  272 us (45%)
  matrix products  129 us (21%)
  other arithmetic  91.2 us (15%)
  local copies, waits for them, and re-layouts  82.2 us (14%)
  between operations  13.8 us (2%)
  starting transfers between devices  11.7 us (2%)
    all_to_all x1, waiting for transfers between devices, on_device(): lax.all_to_all(volume, 'pencil', split_axis=1, concat_axis=2, tiled=True)  94.4 us
    psum x1, waiting for transfers between devices, on_device(): lax.psum(partial_sum.astype(jnp.bfloat16), 'coil').astype(jnp.float32)  90.6 us
    all_to_all x1, waiting for transfers between devices, on_device(): lax.all_to_all(spectrum, 'pencil', split_axis=2, concat_axis=1, tiled=True)  87.2 us
    dot_general x4, matrix products, transform(): jnp.einsum(formula, cosine, volume, preferred_element_type=jnp.float32)  66.2 us
    all_to_all x3, local copies, waits for them, and re-layouts, on_device(): lax.all_to_all(spectrum, 'pencil', split_axis=2, concat_axis=1, tiled=True)  40.8 us
    dot_general x4, matrix products, transform(): jnp.einsum(formula, sine_part, volume, preferred_element_type=jnp.float32)  34.2 us
    convert_element_type x2, local copies, waits for them, and re-layouts, transform(): return (direct + turned).astype(jnp.bfloat16)  32.5 us
    neg x4, other arithmetic, transform(): -crossed[..., readout:]  26.8 us
  transfers between devices with their start and end apart: 3, of which 3 were waited for; matrix products, arithmetic and copies ran while one was open for 1% of the time, Pallas kernels for 0%

commit v1 on v0

v1 whole, which is shorter than its diff:
```python
import math

import jax
import jax.numpy as jnp
from jax import lax
from jax.experimental import pallas as pl
from jax.experimental.pallas import tpu as pltpu
from jax.sharding import PartitionSpec as P


def dft_tables(length, direction):
    indices = jnp.arange(length, dtype=jnp.int32)
    phases = indices[:, None] * indices[None, :] % length
    angles = phases.astype(jnp.float32) * (2.0 * math.pi / length)
    factor = 1.0 / math.sqrt(length)
    cosine = (jnp.cos(angles) * factor).astype(jnp.bfloat16)
    sine_part = (direction * jnp.sin(angles) * factor).astype(jnp.bfloat16)
    return (cosine, sine_part)


def readout_table(length, direction):
    cosine, sine_part = dft_tables(length, direction)
    upper = jnp.concatenate([cosine, sine_part], axis=1)
    lower = jnp.concatenate([-sine_part, cosine], axis=1)
    return jnp.concatenate([upper, lower], axis=0)


def block_table(length, direction):
    cosine, sine_part = dft_tables(length, direction)
    upper = jnp.concatenate([cosine, -sine_part], axis=1)
    lower = jnp.concatenate([sine_part, cosine], axis=1)
    return jnp.concatenate([upper, lower], axis=0)


def slice_tables(length, direction, rows):
    cosine, sine_part = dft_tables(length, direction)
    eye = jnp.eye(rows, dtype=jnp.bfloat16)
    return jnp.kron(cosine, eye), jnp.kron(sine_part, eye)


def turn_add(direct, crossed, half):
    return jnp.concatenate(
        [direct[:, :half] - crossed[:, half:], direct[:, half:] + crossed[:, :half]], axis=1
    )


def dot32(a, b):
    return jnp.dot(a, b, preferred_element_type=jnp.float32)


PARAMS = pltpu.CompilerParams(vmem_limit_bytes=60 * 1024 * 1024)


def forward_kernel(map_ref, obj_ref, fx_ref, kc_ref, ks_ref, out_ref):
    depth, rows, width = map_ref.shape
    half = width // 2
    maps = map_ref[...].reshape(depth * rows, width).astype(jnp.float32)
    obj = obj_ref[...].reshape(depth * rows, width).astype(jnp.float32)
    m_re, m_im = maps[:, :half], maps[:, half:]
    o_re, o_im = obj[:, :half], obj[:, half:]
    image = jnp.concatenate([m_re * o_re - m_im * o_im, m_re * o_im + m_im * o_re], axis=1)
    image = image.astype(jnp.bfloat16)
    along_x = dot32(image, fx_ref[...]).astype(jnp.bfloat16)
    direct = dot32(kc_ref[...], along_x)
    crossed = dot32(ks_ref[...], along_x)
    along_z = turn_add(direct, crossed, half).astype(jnp.bfloat16)
    out_ref[...] = along_z.reshape(out_ref.shape)


def line_kernel(in_ref, mask_ref, wf_ref, wi_ref, out_ref):
    groups, rows, width = in_ref.shape
    half = width // 2
    lines = groups * rows
    volume = in_ref[...].reshape(lines, width)
    stacked = jnp.concatenate([volume[:, :half], volume[:, half:]], axis=0)
    spectrum = dot32(wf_ref[...], stacked).astype(jnp.bfloat16)
    keep = mask_ref[...] > 0
    keep = jnp.concatenate([keep, keep], axis=0)
    sampled = jnp.where(keep, spectrum, jnp.zeros_like(spectrum))
    back = dot32(wi_ref[...], sampled).astype(jnp.bfloat16)
    result = jnp.concatenate([back[:lines], back[lines:]], axis=1)
    out_ref[...] = result.reshape(out_ref.shape)


def backward_kernel(in_ref, map_ref, kc_ref, ks_ref, fx_ref, acc_ref, out_ref):
    depth, rows, width = map_ref.shape
    half = width // 2
    volume = in_ref[...].reshape(depth * rows, width)
    direct = dot32(kc_ref[...], volume)
    crossed = dot32(ks_ref[...], volume)
    back_z = turn_add(direct, crossed, half).astype(jnp.bfloat16)
    back_x = dot32(back_z, fx_ref[...]).astype(jnp.bfloat16).astype(jnp.float32)
    maps = map_ref[...].reshape(depth * rows, width).astype(jnp.float32)
    m_re, m_im = maps[:, :half], maps[:, half:]
    b_re, b_im = back_x[:, :half], back_x[:, half:]
    product = jnp.concatenate([m_re * b_re + m_im * b_im, m_re * b_im - m_im * b_re], axis=1)

    @pl.when(pl.program_id(0) == 0)
    def _():
        out_ref[...] = acc_ref[...]

    out_ref[...] += product.reshape(out_ref.shape)


def on_device(object_image, coil_maps, sample_mask):
    width = object_image.shape[2]
    readout = width // 2
    slices, rows = object_image.shape[0], object_image.shape[1]
    coils = coil_maps.shape[0]
    pencils = lax.axis_size("pencil")
    depth = slices // pencils
    lines = rows * pencils
    segment = readout // sample_mask.shape[2]
    position = lax.axis_index("pencil")

    forward_x = readout_table(readout, -1.0)
    inverse_x = readout_table(readout, 1.0)
    kc_f, ks_f = slice_tables(slices, -1.0, rows)
    kc_i, ks_i = slice_tables(slices, 1.0, rows)
    wf = block_table(lines, -1.0)
    wi = block_table(lines, 1.0)
    mask = lax.dynamic_slice_in_dim(sample_mask, position * depth, depth, 0)
    mask = jnp.repeat(mask, segment, axis=2)

    chunks = 2 if coils % 2 == 0 else 1
    per = coils // chunks
    const2 = lambda c: (0, 0)
    const3 = lambda c: (0, 0, 0)
    acc = jnp.zeros((slices, rows, width), jnp.float32)
    for chunk in range(chunks):
        start = chunk * per
        map_spec = pl.BlockSpec((None, slices, rows, width), lambda c, s=start: (c + s, 0, 0, 0))
        split = pl.pallas_call(
            forward_kernel,
            grid=(per,),
            in_specs=[
                map_spec,
                pl.BlockSpec((slices, rows, width), const3),
                pl.BlockSpec((width, width), const2),
                pl.BlockSpec((slices * rows, slices * rows), const2),
                pl.BlockSpec((slices * rows, slices * rows), const2),
            ],
            out_specs=pl.BlockSpec(
                (pencils, None, depth, rows, width), lambda c: (0, c, 0, 0, 0)
            ),
            out_shape=jax.ShapeDtypeStruct((pencils, per, depth, rows, width), jnp.bfloat16),
            compiler_params=PARAMS,
        )(coil_maps, object_image, forward_x, kc_f, ks_f)
        gathered = lax.all_to_all(split, "pencil", 0, 0, tiled=True)
        lined = pl.pallas_call(
            line_kernel,
            grid=(per, depth),
            in_specs=[
                pl.BlockSpec((pencils, None, None, rows, width), lambda c, k: (0, c, k, 0, 0)),
                pl.BlockSpec((None, lines, readout), lambda c, k: (k, 0, 0)),
                pl.BlockSpec((2 * lines, 2 * lines), lambda c, k: (0, 0)),
                pl.BlockSpec((2 * lines, 2 * lines), lambda c, k: (0, 0)),
            ],
            out_specs=pl.BlockSpec(
                (pencils, None, None, rows, width), lambda c, k: (0, c, k, 0, 0)
            ),
            out_shape=jax.ShapeDtypeStruct((pencils, per, depth, rows, width), jnp.bfloat16),
            compiler_params=PARAMS,
        )(gathered, mask, wf, wi)
        returned = lax.all_to_all(lined, "pencil", 0, 0, tiled=True)
        acc = pl.pallas_call(
            backward_kernel,
            grid=(per,),
            in_specs=[
                pl.BlockSpec((pencils, None, depth, rows, width), lambda c: (0, c, 0, 0, 0)),
                map_spec,
                pl.BlockSpec((slices * rows, slices * rows), const2),
                pl.BlockSpec((slices * rows, slices * rows), const2),
                pl.BlockSpec((width, width), const2),
                pl.BlockSpec((slices, rows, width), const3),
            ],
            out_specs=pl.BlockSpec((slices, rows, width), const3),
            out_shape=jax.ShapeDtypeStruct((slices, rows, width), jnp.float32),
            input_output_aliases={5: 0},
            compiler_params=pltpu.CompilerParams(
                vmem_limit_bytes=60 * 1024 * 1024, dimension_semantics=("arbitrary",)
            ),
        )(returned, coil_maps, kc_i, ks_i, inverse_x, acc)
    summed = lax.psum_scatter(acc.astype(jnp.bfloat16), "coil", scatter_dimension=0, tiled=True)
    return summed.astype(jnp.float32)


def solution(mesh):
    placed = (P(None, "pencil", None), P("coil", None, "pencil", None), P())
    return jax.shard_map(
        on_device, mesh=mesh, in_specs=placed, out_specs=P("coil", "pencil", None), check_vma=False
    )
```

time: 608 us -> 384 us (0.63); the launches traced: 600 us -> 384 us
  matrix products: 129 us -> 0 us
  Pallas kernels: 0 us -> 79.4 us
  waiting for transfers between devices: 272 us -> 205 us
  other arithmetic: 91.2 us -> 35.6 us
  local copies, waits for them, and re-layouts: 82.2 us -> 29.5 us
  starting transfers between devices: 11.7 us -> 20.4 us
    dot_general x10 -> x0, matrix products: 129 us -> none  [the longest x4 66.2 us: transform(): jnp.einsum(formula, cosine, volume, preferred_element_type=jnp.float32)]
    psum x1 -> x0, waiting for transfers between devices: 90.6 us -> none  [on_device(): lax.psum(partial_sum.astype(jnp.bfloat16), 'coil').astype(jnp.float32)]
    pallas_call x0 -> x6, Pallas kernels: none -> 79.4 us  [the longest x2 31.6 us: on_device(): pl.pallas_call(backward_kernel, grid=(per,), in_specs=[pl.BlockSpec((penc...]
    reduce_scatter x0 -> x1, waiting for transfers between devices: none -> 71.3 us  [on_device(): lax.psum_scatter(acc.astype(jnp.bfloat16), 'coil', scatter_dimension=0, t...]
    all_to_all x4 -> x0, local copies, waits for them, and re-layouts: 49.3 us -> none  [the longest x3 40.8 us: on_device(): lax.all_to_all(spectrum, 'pencil', split_axis=2, concat_axis=1, tiled=True)]
    all_to_all x2 -> x4, waiting for transfers between devices: 182 us -> 134 us  [the longest x2 70.2 us: on_device(): gathered = lax.all_to_all(split, 'pencil', 0, 0, tiled=True)]
    convert_element_type x2 -> x0, local copies, waits for them, and re-layouts: 32.5 us -> none  [transform(): return (direct + turned).astype(jnp.bfloat16)]
    neg x4 -> x1, other arithmetic: 26.8 us -> 1 us  [block_table(): upper = jnp.concatenate([cosine, -sine_part], axis=1)]
  transfers between devices with their start and end apart: 3 -> 5, of which waited for: 3 -> 5; matrix products, arithmetic and copies ran while one was open for 1% -> 4% of each run, Pallas kernels for 0% -> 13%
where the time goes in v1:
time: 384 us
  waiting for transfers between devices  205 us (53%)
  Pallas kernels  79.4 us (21%)
  other arithmetic  35.6 us (9%)
  local copies, waits for them, and re-layouts  29.5 us (8%)
  starting transfers between devices  20.4 us (5%)
  between operations  13.5 us (4%)
    reduce_scatter x1, waiting for transfers between devices, on_device(): lax.psum_scatter(acc.astype(jnp.bfloat16), 'coil', scatter_dimension=0, t...  71.3 us
    all_to_all x2, waiting for transfers between devices, on_device(): gathered = lax.all_to_all(split, 'pencil', 0, 0, tiled=True)  70.2 us
    all_to_all x2, waiting for transfers between devices, on_device(): returned = lax.all_to_all(lined, 'pencil', 0, 0, tiled=True)  63.8 us
    pallas_call x2, Pallas kernels, on_device(): pl.pallas_call(backward_kernel, grid=(per,), in_specs=[pl.BlockSpec((penc...  31.6 us
    pallas_call x2, Pallas kernels, on_device(): pl.pallas_call(forward_kernel, grid=(per,), in_specs=[map_spec, pl.BlockS...  26.1 us
    mul x3, local copies, waits for them, and re-layouts, slice_tables(): return (jnp.kron(cosine, eye), jnp.kron(sine_part, eye))  25.5 us
    pallas_call x2, Pallas kernels, on_device(): pl.pallas_call(line_kernel, grid=(per, depth), in_specs=[pl.BlockSpec((pe...  21.7 us
    all_to_all x2, starting transfers between devices, on_device(): gathered = lax.all_to_all(split, 'pencil', 0, 0, tiled=True)  11.3 us
  transfers between devices with their start and end apart: 5, of which 5 were waited for; matrix products, arithmetic and copies ran while one was open for 4% of the time, Pallas kernels for 13%

profile of v1, /device:TPU:0, one launch (start us, length us, event | category | flops | bytes accessed | tf_op | source)
XLA Modules:
  0.0 383.6 jit_solution(10599404449357169759)
XLA Ops:
  6.7 4.0 %multiply_convert_fusion = (bf16[512,512]{1,0:T(8,128)(2,1)S(1)}, bf16[512,512]{1,0:T(8,128)(2,1)S(1)}) fusion(), kind=kLoop, calls=%fused_computation.15 | loop fusion | flops 4718592 | bytes 1048576 | tf_op jit(solution)/shard_map/convert_element_type | solution.py:17
  10.8 4.0 %fusion.17 = (bf16[512,512]{1,0:T(8,128)(2,1)S(1)}, bf16[512,512]{1,0:T(8,128)(2,1)S(1)}) fusion(), kind=kLoop, calls=%fused_computation.40 | loop fusion | flops 6291456 | bytes 1048576 | tf_op jit(solution)/shard_map/neg | solution.py:24
  14.8 4.0 %multiply_convert_fusion.2 = bf16[512,512]{1,0:T(8,128)(2,1)S(1)} fusion(), kind=kLoop, calls=%fused_computation.17 | loop fusion | flops 4194304 | bytes 524288 | tf_op jit(solution)/shard_map/convert_element_type | solution.py:16
  18.8 4.9 %broadcast_multiply_fusion = (bf16[32,16,32,16]{3,2,1,0:T(8,128)(2,1)}, bf16[32,16,32,16]{3,2,1,0:T(8,128)(2,1)}, bf16[32,16,32,16]{3,2,1,0:T(8,128)(2,1)}) fusion(bf16[32,32]{1,0:T(8,128)(2,1)S(1)} %get-tuple-element.16, bf16[16,16]{1,0:T(8,128)(2,1)S(1)} %fusion.29, bf16[32,32]{1,0:T(8,128)(2,1)S(1)} %get-tuple-element.17, ...), kind=kLoop, calls=%fused_computation.6 | loop fusion | flops 786432 | bytes 1579520 | tf_op jit(solution)/shard_map/jit(kron)/mul | solution.py:38
  23.7 8.4 %mul.467.kc_ref = bf16[512,512]{1,0:T(8,128)(2,1)} reshape(bf16[32,16,32,16]{3,2,1,0:T(8,128)(2,1)} %get-tuple-element.11) | data formatting | bytes 1048576 | tf_op jit(solution)/shard_map/jit(kron)/mul | solution.py:38
  32.1 8.4 %mul.472.ks_ref = bf16[512,512]{1,0:T(8,128)(2,1)} reshape(bf16[32,16,32,16]{3,2,1,0:T(8,128)(2,1)} %get-tuple-element.10) | data formatting | bytes 1048576 | tf_op jit(solution)/shard_map/jit(kron)/mul | solution.py:38
  40.5 10.0 %fusion.1 = (bf16[1024,1024]{1,0:T(8,128)(2,1)}, bf16[1024,1024]{1,0:T(8,128)(2,1)}) fusion(bf16[512,512]{1,0:T(8,128)(2,1)S(1)} %multiply_convert_fusion.2, bf16[512,512]{1,0:T(8,128)(2,1)S(1)} %get-tuple-element.15, bf16[512,512]{1,0:T(8,128)(2,1)S(1)} %get-tuple-element.12, bf16[512,512]{1,0:T(8,128)(2,1)S(1)} %get-tuple-element.14, ...), kind=kLoop, calls=%fused_computation.5 | loop fusion | flops 14680064 | bytes 6815744 | tf_op jit(solution)/shard_map/concatenate | solution.py:25
  50.5 13.1 %shard_map.39 = bf16[16,4,2,16,1024]{4,3,2,1,0:T(8,128)(2,1)} custom-call(bf16[8,32,16,1024]{3,2,1,0:T(8,128)(2,1)} %map_ref.7, bf16[32,16,1024]{2,1,0:T(8,128)(2,1)} %obj_ref.3, bf16[1024,1024]{1,0:T(8,128)(2,1)} %get-tuple-element.6.fx_ref, bf16[512,512]{1,0:T(8,128)(2,1)} %mul.467.kc_ref, bf16[512,512]{1,0:T(8,128)(2,1)} %mul.472.ks_ref), custom_call_target="tpu_custom_call" | custom-call | tf_op jit(solution)/shard_map/pallas_call | solution.py:133
  63.6 6.5 %all-to-all-start.2 = ((bf16[16,4,2,16,1024]{4,3,2,1,0:T(8,128)(2,1)}), bf16[16,4,2,16,1024]{4,3,2,1,0:T(8,128)(2,1)}, u32[]{:S(2)}, u32[]{:S(2)}) async-start(bf16[16,4,2,16,1024]{4,3,2,1,0:T(8,128)(2,1)} %shard_map.39), calls=%async_computation.2 | async-start | bytes 8388608 | tf_op jit(solution)/shard_map/all_to_all | solution.py:149
  70.1 13.0 %shard_map.37 = bf16[16,4,2,16,1024]{4,3,2,1,0:T(8,128)(2,1)} custom-call(bf16[8,32,16,1024]{3,2,1,0:T(8,128)(2,1)} %map_ref.7, bf16[32,16,1024]{2,1,0:T(8,128)(2,1)} %obj_ref.3, bf16[1024,1024]{1,0:T(8,128)(2,1)} %get-tuple-element.6.fx_ref, bf16[512,512]{1,0:T(8,128)(2,1)} %mul.467.kc_ref, bf16[512,512]{1,0:T(8,128)(2,1)} %mul.472.ks_ref), custom_call_target="tpu_custom_call" | custom-call | tf_op jit(solution)/shard_map/pallas_call | solution.py:133
  83.1 37.4 %all-to-all-done.2.in_ref = bf16[16,4,2,16,1024]{4,3,2,1,0:T(8,128)(2,1)} async-done(((bf16[16,4,2,16,1024]{4,3,2,1,0:T(8,128)(2,1)}), bf16[16,4,2,16,1024]{4,3,2,1,0:T(8,128)(2,1)}, u32[]{:S(2)}, u32[]{:S(2)}) %all-to-all-start.2) | async-done | bytes 4194336 | tf_op jit(solution)/shard_map/all_to_all | solution.py:149
  120.5 4.8 %all-to-all-start = ((bf16[16,4,2,16,1024]{4,3,2,1,0:T(8,128)(2,1)}), bf16[16,4,2,16,1024]{4,3,2,1,0:T(8,128)(2,1)}, u32[]{:S(2)}, u32[]{:S(2)}) async-start(bf16[16,4,2,16,1024]{4,3,2,1,0:T(8,128)(2,1)} %shard_map.37), calls=%async_computation | async-start | bytes 8388608 | tf_op jit(solution)/shard_map/all_to_all | solution.py:149
  131.8 10.8 %shard_map.40 = bf16[16,4,2,16,1024]{4,3,2,1,0:T(8,128)(2,1)} custom-call(bf16[16,4,2,16,1024]{4,3,2,1,0:T(8,128)(2,1)} %all-to-all-done.2.in_ref, s32[2,256,512]{2,1,0:T(8,128)} %reshape.76.mask_ref, bf16[512,512]{1,0:T(8,128)(2,1)} %get-tuple-element.8.wf_ref, bf16[512,512]{1,0:T(8,128)(2,1)} %get-tuple-element.7.wi_ref), custom_call_target="tpu_custom_call" | custom-call | tf_op jit(solution)/shard_map/pallas_call | solution.py:150
  142.6 32.8 %all-to-all-done.in_ref = bf16[16,4,2,16,1024]{4,3,2,1,0:T(8,128)(2,1)} async-done(((bf16[16,4,2,16,1024]{4,3,2,1,0:T(8,128)(2,1)}), bf16[16,4,2,16,1024]{4,3,2,1,0:T(8,128)(2,1)}, u32[]{:S(2)}, u32[]{:S(2)}) %all-to-all-start) | async-done | bytes 4194336 | tf_op jit(solution)/shard_map/all_to_all | solution.py:149
  175.4 4.6 %all-to-all-start.3 = ((bf16[16,4,2,16,1024]{4,3,2,1,0:T(8,128)(2,1)}), bf16[16,4,2,16,1024]{4,3,2,1,0:T(8,128)(2,1)}, u32[]{:S(2)}, u32[]{:S(2)}) async-start(bf16[16,4,2,16,1024]{4,3,2,1,0:T(8,128)(2,1)} %shard_map.40), calls=%async_computation.3 | async-start | bytes 8388608 | tf_op jit(solution)/shard_map/all_to_all | solution.py:165
  180.0 10.9 %shard_map.38 = bf16[16,4,2,16,1024]{4,3,2,1,0:T(8,128)(2,1)} custom-call(bf16[16,4,2,16,1024]{4,3,2,1,0:T(8,128)(2,1)} %all-to-all-done.in_ref, s32[2,256,512]{2,1,0:T(8,128)} %reshape.76.mask_ref, bf16[512,512]{1,0:T(8,128)(2,1)} %get-tuple-element.8.wf_ref, bf16[512,512]{1,0:T(8,128)(2,1)} %get-tuple-element.7.wi_ref), custom_call_target="tpu_custom_call" | custom-call | tf_op jit(solution)/shard_map/pallas_call | solution.py:150
  190.8 39.5 %all-to-all-done.3.in_ref = bf16[16,4,2,16,1024]{4,3,2,1,0:T(8,128)(2,1)} async-done(((bf16[16,4,2,16,1024]{4,3,2,1,0:T(8,128)(2,1)}), bf16[16,4,2,16,1024]{4,3,2,1,0:T(8,128)(2,1)}, u32[]{:S(2)}, u32[]{:S(2)}) %all-to-all-start.3) | async-done | bytes 4194336 | tf_op jit(solution)/shard_map/all_to_all | solution.py:165
  230.3 4.6 %all-to-all-start.1 = ((bf16[16,4,2,16,1024]{4,3,2,1,0:T(8,128)(2,1)}), bf16[16,4,2,16,1024]{4,3,2,1,0:T(8,128)(2,1)}, u32[]{:S(2)}, u32[]{:S(2)}) async-start(bf16[16,4,2,16,1024]{4,3,2,1,0:T(8,128)(2,1)} %shard_map.38), calls=%async_computation.1 | async-start | bytes 8388608 | tf_op jit(solution)/shard_map/all_to_all | solution.py:165
  234.9 8.7 %mul.485.ks_ref = bf16[512,512]{1,0:T(8,128)(2,1)} reshape(bf16[32,16,32,16]{3,2,1,0:T(8,128)(2,1)} %get-tuple-element.9) | data formatting | bytes 1048576 | tf_op jit(solution)/shard_map/jit(kron)/mul | solution.py:38
  245.2 15.8 %shard_map.41.acc_ref = f32[32,16,1024]{2,1,0:T(8,128)} custom-call(bf16[16,4,2,16,1024]{4,3,2,1,0:T(8,128)(2,1)} %all-to-all-done.3.in_ref, bf16[8,32,16,1024]{3,2,1,0:T(8,128)(2,1)} %map_ref.7, bf16[512,512]{1,0:T(8,128)(2,1)} %mul.467.kc_ref, bf16[512,512]{1,0:T(8,128)(2,1)} %mul.485.ks_ref, ...), custom_call_target="tpu_custom_call", output_to_operand_aliasing={{}: (5, {})} | custom-call | tf_op jit(solution)/shard_map/pallas_call | solution.py:166
  261.0 24.3 %all-to-all-done.1.in_ref = bf16[16,4,2,16,1024]{4,3,2,1,0:T(8,128)(2,1)} async-done(((bf16[16,4,2,16,1024]{4,3,2,1,0:T(8,128)(2,1)}), bf16[16,4,2,16,1024]{4,3,2,1,0:T(8,128)(2,1)}, u32[]{:S(2)}, u32[]{:S(2)}) %all-to-all-start.1) | async-done | bytes 4194336 | tf_op jit(solution)/shard_map/all_to_all | solution.py:165
  285.3 15.8 %shard_map.42 = f32[32,16,1024]{2,1,0:T(8,128)} custom-call(bf16[16,4,2,16,1024]{4,3,2,1,0:T(8,128)(2,1)} %all-to-all-done.1.in_ref, bf16[8,32,16,1024]{3,2,1,0:T(8,128)(2,1)} %map_ref.7, bf16[512,512]{1,0:T(8,128)(2,1)} %mul.467.kc_ref, bf16[512,512]{1,0:T(8,128)(2,1)} %mul.485.ks_ref, ...), custom_call_target="tpu_custom_call", output_to_operand_aliasing={{}: (5, {})} | custom-call | tf_op jit(solution)/shard_map/pallas_call | solution.py:166
  301.1 2.7 convert_element_type.177
  303.8 71.3 %reduce-scatter.2.cloned.1.call-done = bf16[4,16,1024]{2,1,0:T(8,128)(2,1)} async-done(((bf16[32,16,1024]{2,1,0:T(8,128)(2,1)}), bf16[4,16,1024]{2,1,0:T(8,128)(2,1)}) %reduce-scatter.2.cloned.1.call-update) | async-done | bytes 131088 | tf_op jit(solution)/shard_map/reduce_scatter | solution.py:184
  (19 shorter events, 9.9 us)
Async XLA Ops:
  6.5 118.7 %copy-start = (s32[32,256,4]{1,2,0:T(4,128)S(1)}, s32[32,256,4]{1,2,0:T(4,128)}, u32[]{:S(2)}) copy-start(s32[32,256,4]{1,2,0:T(4,128)} %param.5) | copy-start | bytes 393220
  63.6 56.9 %all-to-all-start.2 = ((bf16[16,4,2,16,1024]{4,3,2,1,0:T(8,128)(2,1)}), bf16[16,4,2,16,1024]{4,3,2,1,0:T(8,128)(2,1)}, u32[]{:S(2)}, u32[]{:S(2)}) async-start(bf16[16,4,2,16,1024]{4,3,2,1,0:T(8,128)(2,1)} %shard_map.39), calls=%async_computation.2 | async-start | bytes 8388608 | tf_op jit(solution)/shard_map/all_to_all | solution.py:149
  120.5 54.9 %all-to-all-start = ((bf16[16,4,2,16,1024]{4,3,2,1,0:T(8,128)(2,1)}), bf16[16,4,2,16,1024]{4,3,2,1,0:T(8,128)(2,1)}, u32[]{:S(2)}, u32[]{:S(2)}) async-start(bf16[16,4,2,16,1024]{4,3,2,1,0:T(8,128)(2,1)} %shard_map.37), calls=%async_computation | async-start | bytes 8388608 | tf_op jit(solution)/shard_map/all_to_all | solution.py:149
  175.4 54.9 %all-to-all-start.3 = ((bf16[16,4,2,16,1024]{4,3,2,1,0:T(8,128)(2,1)}), bf16[16,4,2,16,1024]{4,3,2,1,0:T(8,128)(2,1)}, u32[]{:S(2)}, u32[]{:S(2)}) async-start(bf16[16,4,2,16,1024]{4,3,2,1,0:T(8,128)(2,1)} %shard_map.40), calls=%async_computation.3 | async-start | bytes 8388608 | tf_op jit(solution)/shard_map/all_to_all | solution.py:165
  230.3 54.9 %all-to-all-start.1 = ((bf16[16,4,2,16,1024]{4,3,2,1,0:T(8,128)(2,1)}), bf16[16,4,2,16,1024]{4,3,2,1,0:T(8,128)(2,1)}, u32[]{:S(2)}, u32[]{:S(2)}) async-start(bf16[16,4,2,16,1024]{4,3,2,1,0:T(8,128)(2,1)} %shard_map.38), calls=%async_computation.1 | async-start | bytes 8388608 | tf_op jit(solution)/shard_map/all_to_all | solution.py:165
  234.9 140.3 %reduce-scatter.2.cloned.1.call-start = ((), (), s32[]{:S(2)}) async-start(), calls=%async_computation.5 | async-start | bytes 1179648 | tf_op jit(solution)/shard_map/reduce_scatter | solution.py:184
  285.3 91.5 %copy-start.1 = (s32[32,256,4]{1,2,0:T(4,128)S(1)}, s32[32,256,4]{1,2,0:T(4,128)}, u32[]{:S(2)}) copy-start(s32[32,256,4]{1,2,0:T(4,128)} %param.5) | copy-start | bytes 393220
Sparse Core Ops, SparseCore 0:
  304.0 71.1 reduce-scatter.1

commit v2 on v1

--- a/solution.py
+++ b/solution.py
@@ -1,6 +1,8 @@
 import math
 
 import jax
+import ml_dtypes
+import numpy as np
 import jax.numpy as jnp
 from jax import lax
 from jax.experimental import pallas as pl
@@ -9,33 +11,34 @@
 
 
 def dft_tables(length, direction):
-    indices = jnp.arange(length, dtype=jnp.int32)
+    indices = np.arange(length, dtype=np.int32)
     phases = indices[:, None] * indices[None, :] % length
-    angles = phases.astype(jnp.float32) * (2.0 * math.pi / length)
-    factor = 1.0 / math.sqrt(length)
-    cosine = (jnp.cos(angles) * factor).astype(jnp.bfloat16)
-    sine_part = (direction * jnp.sin(angles) * factor).astype(jnp.bfloat16)
+    angles = phases.astype(np.float32) * np.float32(2.0 * math.pi / length)
+    factor = np.float32(1.0 / math.sqrt(length))
+    cosine = (np.cos(angles) * factor).astype(ml_dtypes.bfloat16)
+    sine_part = (np.float32(direction) * np.sin(angles) * factor).astype(ml_dtypes.bfloat16)
     return (cosine, sine_part)
 
 
 def readout_table(length, direction):
     cosine, sine_part = dft_tables(length, direction)
-    upper = jnp.concatenate([cosine, sine_part], axis=1)
-    lower = jnp.concatenate([-sine_part, cosine], axis=1)
-    return jnp.concatenate([upper, lower], axis=0)
+    upper = np.concatenate([cosine, sine_part], axis=1)
+    lower = np.concatenate([-sine_part, cosine], axis=1)
+    return jnp.asarray(np.concatenate([upper, lower], axis=0))
 
 
 def block_table(length, direction):
     cosine, sine_part = dft_tables(length, direction)
-    upper = jnp.concatenate([cosine, -sine_part], axis=1)
-    lower = jnp.concatenate([sine_part, cosine], axis=1)
-    return jnp.concatenate([upper, lower], axis=0)
+    upper = np.concatenate([cosine, -sine_part], axis=1)
+    lower = np.concatenate([sine_part, cosine], axis=1)
+    return jnp.asarray(np.concatenate([upper, lower], axis=0))
 
 
 def slice_tables(length, direction, rows):
     cosine, sine_part = dft_tables(length, direction)
-    eye = jnp.eye(rows, dtype=jnp.bfloat16)
-    return jnp.kron(cosine, eye), jnp.kron(sine_part, eye)
+    eye = np.eye(rows, dtype=np.float32)
+    kron = lambda t: jnp.asarray(np.kron(t.astype(np.float32), eye).astype(ml_dtypes.bfloat16))
+    return kron(cosine), kron(sine_part)
 
 
 def turn_add(direct, crossed, half):
@@ -181,8 +184,10 @@
                 vmem_limit_bytes=60 * 1024 * 1024, dimension_semantics=("arbitrary",)
             ),
         )(returned, coil_maps, kc_i, ks_i, inverse_x, acc)
-    summed = lax.psum_scatter(acc.astype(jnp.bfloat16), "coil", scatter_dimension=0, tiled=True)
-    return summed.astype(jnp.float32)
+    groups = lax.axis_size("coil")
+    parts = acc.astype(jnp.bfloat16).reshape(groups, slices // groups, rows, width)
+    parts = lax.all_to_all(parts, "coil", 0, 0, tiled=True)
+    return jnp.sum(parts.astype(jnp.float32), axis=0)
 
 
 def solution(mesh):

time: 384 us -> 277 us (0.72)
  waiting for transfers between devices: 205 us -> 147 us
  other arithmetic: 35.6 us -> 2.62 us
  local copies, waits for them, and re-layouts: 29.5 us -> 3.95 us
  blocking collectives: 0 us -> 23.4 us
  between operations: 13.5 us -> 0.08 us
    reduce_scatter x1 -> x0, waiting for transfers between devices: 71.3 us -> none  [on_device(): lax.psum_scatter(acc.astype(jnp.bfloat16), 'coil', scatter_dimension=0, t...]
    mul x3 -> x0, local copies, waits for them, and re-layouts: 25.5 us -> none  [slice_tables(): return (jnp.kron(cosine, eye), jnp.kron(sine_part, eye))]
    all_to_all x0 -> x1, blocking collectives: none -> 23.4 us  [on_device(): parts = lax.all_to_all(parts, 'coil', 0, 0, tiled=True)]
    convert_element_type x9 -> x1, other arithmetic: 14.5 us -> 1.74 us  [on_device(): acc.astype(jnp.bfloat16).reshape(groups, slices // groups, rows, width)]
    concatenate x2 -> x0, other arithmetic: 11.1 us -> none  [the longest x1 9.99 us: readout_table(): return jnp.concatenate([upper, lower], axis=0)]
    all_to_all x2, waiting for transfers between devices: 63.8 us -> 72.5 us  [on_device(): returned = lax.all_to_all(lined, 'pencil', 0, 0, tiled=True)]
    neg x2 -> x0, other arithmetic: 5.05 us -> none  [the longest x1 4.05 us: readout_table(): lower = jnp.concatenate([-sine_part, cosine], axis=1)]
    mul x1 -> x0, other arithmetic: 4.87 us -> none  [slice_tables(): return (jnp.kron(cosine, eye), jnp.kron(sine_part, eye))]
  transfers between devices with their start and end apart: 5 -> 4, of which waited for: 5 -> 4; matrix products, arithmetic and copies ran while one was open for 4% -> 1% of each run, Pallas kernels for 13% -> 18%
where the time goes in v2:
time: 277 us
  waiting for transfers between devices  147 us (53%)
  Pallas kernels  79.4 us (29%)
  blocking collectives  23.4 us (8%)
  starting transfers between devices  20.2 us (7%)
  local copies, waits for them, and re-layouts  3.95 us (1%)
    all_to_all x2, waiting for transfers between devices, on_device(): gathered = lax.all_to_all(split, 'pencil', 0, 0, tiled=True)  74.4 us
    all_to_all x2, waiting for transfers between devices, on_device(): returned = lax.all_to_all(lined, 'pencil', 0, 0, tiled=True)  72.5 us
    pallas_call x2, Pallas kernels, on_device(): pl.pallas_call(backward_kernel, grid=(per,), in_specs=[pl.BlockSpec((penc...  31.5 us
    pallas_call x2, Pallas kernels, on_device(): pl.pallas_call(forward_kernel, grid=(per,), in_specs=[map_spec, pl.BlockS...  26.2 us
    all_to_all x1, blocking collectives, on_device(): parts = lax.all_to_all(parts, 'coil', 0, 0, tiled=True)  23.4 us
    pallas_call x2, Pallas kernels, on_device(): pl.pallas_call(line_kernel, grid=(per, depth), in_specs=[pl.BlockSpec((pe...  21.7 us
    all_to_all x2, starting transfers between devices, on_device(): gathered = lax.all_to_all(split, 'pencil', 0, 0, tiled=True)  11.1 us
    all_to_all x2, starting transfers between devices, on_device(): returned = lax.all_to_all(lined, 'pencil', 0, 0, tiled=True)  9.12 us
  transfers between devices with their start and end apart: 4, of which 4 were waited for; matrix products, arithmetic and copies ran while one was open for 1% of the time, Pallas kernels for 18%

profile of v2, /device:TPU:0, one launch (start us, length us, event | category | flops | bytes accessed | tf_op | source)
XLA Modules:
  0.0 276.6 jit_solution(638689880753511743)
XLA Ops:
  0.0 0.0 copy-start
  0.0 13.1 %shard_map.111 = bf16[16,4,2,16,1024]{4,3,2,1,0:T(8,128)(2,1)} custom-call(bf16[8,32,16,1024]{3,2,1,0:T(8,128)(2,1)} %map_ref.7, bf16[32,16,1024]{2,1,0:T(8,128)(2,1)} %obj_ref.3, bf16[1024,1024]{1,0:T(8,128)(2,1)} %constant.11.clone.fx_ref, bf16[512,512]{1,0:T(8,128)(2,1)} %constant.29.clone.kc_ref, bf16[512,512]{1,0:T(8,128)(2,1)} %constant.30.clone.ks_ref), custom_call_target="tpu_custom_call" | custom-call | tf_op jit(solution)/shard_map/pallas_call | solution.py:136
  13.1 6.5 %all-to-all-start.2 = ((bf16[16,4,2,16,1024]{4,3,2,1,0:T(8,128)(2,1)}), bf16[16,4,2,16,1024]{4,3,2,1,0:T(8,128)(2,1)}, u32[]{:S(2)}, u32[]{:S(2)}) async-start(bf16[16,4,2,16,1024]{4,3,2,1,0:T(8,128)(2,1)} %shard_map.111), calls=%async_computation.2 | async-start | bytes 8388608 | tf_op jit(solution)/shard_map/all_to_all | solution.py:152
  19.6 13.1 %shard_map.109 = bf16[16,4,2,16,1024]{4,3,2,1,0:T(8,128)(2,1)} custom-call(bf16[8,32,16,1024]{3,2,1,0:T(8,128)(2,1)} %map_ref.7, bf16[32,16,1024]{2,1,0:T(8,128)(2,1)} %obj_ref.3, bf16[1024,1024]{1,0:T(8,128)(2,1)} %constant.11.clone.fx_ref, bf16[512,512]{1,0:T(8,128)(2,1)} %constant.29.clone.kc_ref, bf16[512,512]{1,0:T(8,128)(2,1)} %constant.30.clone.ks_ref), custom_call_target="tpu_custom_call" | custom-call | tf_op jit(solution)/shard_map/pallas_call | solution.py:136
  32.7 37.3 %all-to-all-done.2.in_ref = bf16[16,4,2,16,1024]{4,3,2,1,0:T(8,128)(2,1)} async-done(((bf16[16,4,2,16,1024]{4,3,2,1,0:T(8,128)(2,1)}), bf16[16,4,2,16,1024]{4,3,2,1,0:T(8,128)(2,1)}, u32[]{:S(2)}, u32[]{:S(2)}) %all-to-all-start.2) | async-done | bytes 4194336 | tf_op jit(solution)/shard_map/all_to_all | solution.py:152
  70.0 4.6 %all-to-all-start = ((bf16[16,4,2,16,1024]{4,3,2,1,0:T(8,128)(2,1)}), bf16[16,4,2,16,1024]{4,3,2,1,0:T(8,128)(2,1)}, u32[]{:S(2)}, u32[]{:S(2)}) async-start(bf16[16,4,2,16,1024]{4,3,2,1,0:T(8,128)(2,1)} %shard_map.109), calls=%async_computation | async-start | bytes 8388608 | tf_op jit(solution)/shard_map/all_to_all | solution.py:152
  74.6 0.0 copy-done
  74.6 0.1 copy.14
  74.7 0.8 broadcast_in_dim.6
  75.5 1.4 reshape.6.mask_ref
  77.0 10.8 %shard_map.112 = bf16[16,4,2,16,1024]{4,3,2,1,0:T(8,128)(2,1)} custom-call(bf16[16,4,2,16,1024]{4,3,2,1,0:T(8,128)(2,1)} %all-to-all-done.2.in_ref, s32[2,256,512]{2,1,0:T(8,128)} %reshape.6.mask_ref, bf16[512,512]{1,0:T(8,128)(2,1)} %constant.32.clone.wf_ref, bf16[512,512]{1,0:T(8,128)(2,1)} %constant.33.clone.wi_ref), custom_call_target="tpu_custom_call" | custom-call | tf_op jit(solution)/shard_map/pallas_call | solution.py:153
  87.8 37.1 %all-to-all-done.in_ref = bf16[16,4,2,16,1024]{4,3,2,1,0:T(8,128)(2,1)} async-done(((bf16[16,4,2,16,1024]{4,3,2,1,0:T(8,128)(2,1)}), bf16[16,4,2,16,1024]{4,3,2,1,0:T(8,128)(2,1)}, u32[]{:S(2)}, u32[]{:S(2)}) %all-to-all-start) | async-done | bytes 4194336 | tf_op jit(solution)/shard_map/all_to_all | solution.py:152
  124.9 4.5 %all-to-all-start.3 = ((bf16[16,4,2,16,1024]{4,3,2,1,0:T(8,128)(2,1)}), bf16[16,4,2,16,1024]{4,3,2,1,0:T(8,128)(2,1)}, u32[]{:S(2)}, u32[]{:S(2)}) async-start(bf16[16,4,2,16,1024]{4,3,2,1,0:T(8,128)(2,1)} %shard_map.112), calls=%async_computation.3 | async-start | bytes 8388608 | tf_op jit(solution)/shard_map/all_to_all | solution.py:168
  129.5 10.8 %shard_map.110 = bf16[16,4,2,16,1024]{4,3,2,1,0:T(8,128)(2,1)} custom-call(bf16[16,4,2,16,1024]{4,3,2,1,0:T(8,128)(2,1)} %all-to-all-done.in_ref, s32[2,256,512]{2,1,0:T(8,128)} %reshape.6.mask_ref, bf16[512,512]{1,0:T(8,128)(2,1)} %constant.32.clone.wf_ref, bf16[512,512]{1,0:T(8,128)(2,1)} %constant.33.clone.wi_ref), custom_call_target="tpu_custom_call" | custom-call | tf_op jit(solution)/shard_map/pallas_call | solution.py:153
  140.3 39.5 %all-to-all-done.3.in_ref = bf16[16,4,2,16,1024]{4,3,2,1,0:T(8,128)(2,1)} async-done(((bf16[16,4,2,16,1024]{4,3,2,1,0:T(8,128)(2,1)}), bf16[16,4,2,16,1024]{4,3,2,1,0:T(8,128)(2,1)}, u32[]{:S(2)}, u32[]{:S(2)}) %all-to-all-start.3) | async-done | bytes 4194336 | tf_op jit(solution)/shard_map/all_to_all | solution.py:168
  179.9 4.6 %all-to-all-start.1 = ((bf16[16,4,2,16,1024]{4,3,2,1,0:T(8,128)(2,1)}), bf16[16,4,2,16,1024]{4,3,2,1,0:T(8,128)(2,1)}, u32[]{:S(2)}, u32[]{:S(2)}) async-start(bf16[16,4,2,16,1024]{4,3,2,1,0:T(8,128)(2,1)} %shard_map.110), calls=%async_computation.1 | async-start | bytes 8388608 | tf_op jit(solution)/shard_map/all_to_all | solution.py:168
  184.4 1.6 broadcast_in_dim.7.acc_ref
  186.0 15.8 %shard_map.113.acc_ref = f32[32,16,1024]{2,1,0:T(8,128)} custom-call(bf16[16,4,2,16,1024]{4,3,2,1,0:T(8,128)(2,1)} %all-to-all-done.3.in_ref, bf16[8,32,16,1024]{3,2,1,0:T(8,128)(2,1)} %map_ref.7, bf16[512,512]{1,0:T(8,128)(2,1)} %constant.29.clone.kc_ref, bf16[512,512]{1,0:T(8,128)(2,1)} %constant.31.clone.ks_ref, ...), custom_call_target="tpu_custom_call", output_to_operand_aliasing={{}: (5, {})} | custom-call | tf_op jit(solution)/shard_map/pallas_call | solution.py:169
  201.8 33.0 %all-to-all-done.1.in_ref = bf16[16,4,2,16,1024]{4,3,2,1,0:T(8,128)(2,1)} async-done(((bf16[16,4,2,16,1024]{4,3,2,1,0:T(8,128)(2,1)}), bf16[16,4,2,16,1024]{4,3,2,1,0:T(8,128)(2,1)}, u32[]{:S(2)}, u32[]{:S(2)}) %all-to-all-start.1) | async-done | bytes 4194336 | tf_op jit(solution)/shard_map/all_to_all | solution.py:168
  234.8 15.8 %shard_map.114 = f32[32,16,1024]{2,1,0:T(8,128)} custom-call(bf16[16,4,2,16,1024]{4,3,2,1,0:T(8,128)(2,1)} %all-to-all-done.1.in_ref, bf16[8,32,16,1024]{3,2,1,0:T(8,128)(2,1)} %map_ref.7, bf16[512,512]{1,0:T(8,128)(2,1)} %constant.29.clone.kc_ref, bf16[512,512]{1,0:T(8,128)(2,1)} %constant.31.clone.ks_ref, ...), custom_call_target="tpu_custom_call", output_to_operand_aliasing={{}: (5, {})} | custom-call | tf_op jit(solution)/shard_map/pallas_call | solution.py:169
  250.6 1.7 convert_element_type.6
  252.3 23.4 %all_to_all.25 = bf16[8,4,16,1024]{3,2,1,0:T(8,128)(2,1)S(1)} all-to-all(bf16[8,4,16,1024]{3,2,1,0:T(8,128)(2,1)S(1)} %bitcast.1), channel_id=1, replica_groups=mesh['coil'=8,'pencil'=16] {'coil'}, dimensions={0} | all-to-all | bytes 2097152 | tf_op jit(solution)/shard_map/all_to_all | solution.py:189
  275.8 0.9 convert_reduce_fusion
  (1 shorter events, 0.0 us)
Async XLA Ops:
  0.0 74.6 %copy-start = (s32[32,256,4]{1,2,0:T(4,128)S(1)}, s32[32,256,4]{1,2,0:T(4,128)}, u32[]{:S(2)}) copy-start(s32[32,256,4]{1,2,0:T(4,128)} %param.13) | copy-start | bytes 393220
  13.1 56.9 %all-to-all-start.2 = ((bf16[16,4,2,16,1024]{4,3,2,1,0:T(8,128)(2,1)}), bf16[16,4,2,16,1024]{4,3,2,1,0:T(8,128)(2,1)}, u32[]{:S(2)}, u32[]{:S(2)}) async-start(bf16[16,4,2,16,1024]{4,3,2,1,0:T(8,128)(2,1)} %shard_map.111), calls=%async_computation.2 | async-start | bytes 8388608 | tf_op jit(solution)/shard_map/all_to_all | solution.py:152
  70.0 54.9 %all-to-all-start = ((bf16[16,4,2,16,1024]{4,3,2,1,0:T(8,128)(2,1)}), bf16[16,4,2,16,1024]{4,3,2,1,0:T(8,128)(2,1)}, u32[]{:S(2)}, u32[]{:S(2)}) async-start(bf16[16,4,2,16,1024]{4,3,2,1,0:T(8,128)(2,1)} %shard_map.109), calls=%async_computation | async-start | bytes 8388608 | tf_op jit(solution)/shard_map/all_to_all | solution.py:152
  124.9 54.9 %all-to-all-start.3 = ((bf16[16,4,2,16,1024]{4,3,2,1,0:T(8,128)(2,1)}), bf16[16,4,2,16,1024]{4,3,2,1,0:T(8,128)(2,1)}, u32[]{:S(2)}, u32[]{:S(2)}) async-start(bf16[16,4,2,16,1024]{4,3,2,1,0:T(8,128)(2,1)} %shard_map.112), calls=%async_computation.3 | async-start | bytes 8388608 | tf_op jit(solution)/shard_map/all_to_all | solution.py:168
  179.9 54.9 %all-to-all-start.1 = ((bf16[16,4,2,16,1024]{4,3,2,1,0:T(8,128)(2,1)}), bf16[16,4,2,16,1024]{4,3,2,1,0:T(8,128)(2,1)}, u32[]{:S(2)}, u32[]{:S(2)}) async-start(bf16[16,4,2,16,1024]{4,3,2,1,0:T(8,128)(2,1)} %shard_map.110), calls=%async_computation.1 | async-start | bytes 8388608 | tf_op jit(solution)/shard_map/all_to_all | solution.py:168

commit v3 on v2

--- a/solution.py
+++ b/solution.py
@@ -125,7 +125,7 @@
     mask = lax.dynamic_slice_in_dim(sample_mask, position * depth, depth, 0)
     mask = jnp.repeat(mask, segment, axis=2)
 
-    chunks = 2 if coils % 2 == 0 else 1
+    chunks = 4 if coils % 4 == 0 else 1
     per = coils // chunks
     const2 = lambda c: (0, 0)
     const3 = lambda c: (0, 0, 0)

time: 277 us -> 316 us (1.14)
  Pallas kernels: 79.4 us -> 99 us
  starting transfers between devices: 20.2 us -> 34.1 us
  local copies, waits for them, and re-layouts: 3.95 us -> 12.1 us
  waiting for transfers between devices: 147 us -> 143 us
    pallas_call x2 -> x4, Pallas kernels: 31.5 us -> 40.9 us  [on_device(): pl.pallas_call(backward_kernel, grid=(per,), in_specs=[pl.BlockSpec((penc...]
    unnamed x2 -> x14, local copies, waits for them, and re-layouts: 0.01 us -> 8.08 us
    all_to_all x2 -> x4, waiting for transfers between devices: 72.5 us -> 64.8 us  [on_device(): returned = lax.all_to_all(lined, 'pencil', 0, 0, tiled=True)]
    all_to_all x2 -> x4, starting transfers between devices: 9.12 us -> 16.5 us  [on_device(): returned = lax.all_to_all(lined, 'pencil', 0, 0, tiled=True)]
    pallas_call x2 -> x4, Pallas kernels: 26.2 us -> 33 us  [on_device(): pl.pallas_call(forward_kernel, grid=(per,), in_specs=[map_spec, pl.BlockS...]
    all_to_all x2 -> x4, starting transfers between devices: 11.1 us -> 17.6 us  [on_device(): gathered = lax.all_to_all(split, 'pencil', 0, 0, tiled=True)]
    all_to_all x2 -> x4, waiting for transfers between devices: 74.4 us -> 78.1 us  [on_device(): gathered = lax.all_to_all(split, 'pencil', 0, 0, tiled=True)]
    pallas_call x2 -> x4, Pallas kernels: 21.7 us -> 25.1 us  [on_device(): pl.pallas_call(line_kernel, grid=(per, depth), in_specs=[pl.BlockSpec((pe...]
  transfers between devices with their start and end apart: 4 -> 8, of which waited for: 4 -> 7; matrix products, arithmetic and copies ran while one was open for 1% -> 1% of each run, Pallas kernels for 18% -> 26%
where the time goes in v3:
time: 316 us; the launch traced here: 315 us
  waiting for transfers between devices  143 us (45%)
  Pallas kernels  99 us (31%)
  starting transfers between devices  34.1 us (11%)
  blocking collectives  24.1 us (8%)
  local copies, waits for them, and re-layouts  12.1 us (4%)
    all_to_all x4, waiting for transfers between devices, on_device(): gathered = lax.all_to_all(split, 'pencil', 0, 0, tiled=True)  78.1 us
    all_to_all x4, waiting for transfers between devices, on_device(): returned = lax.all_to_all(lined, 'pencil', 0, 0, tiled=True)  64.8 us
    pallas_call x4, Pallas kernels, on_device(): pl.pallas_call(backward_kernel, grid=(per,), in_specs=[pl.BlockSpec((penc...  40.9 us
    pallas_call x4, Pallas kernels, on_device(): pl.pallas_call(forward_kernel, grid=(per,), in_specs=[map_spec, pl.BlockS...  33 us
    pallas_call x4, Pallas kernels, on_device(): pl.pallas_call(line_kernel, grid=(per, depth), in_specs=[pl.BlockSpec((pe...  25.1 us
    all_to_all x1, blocking collectives, on_device(): parts = lax.all_to_all(parts, 'coil', 0, 0, tiled=True)  24.1 us
    all_to_all x4, starting transfers between devices, on_device(): gathered = lax.all_to_all(split, 'pencil', 0, 0, tiled=True)  17.6 us
    all_to_all x4, starting transfers between devices, on_device(): returned = lax.all_to_all(lined, 'pencil', 0, 0, tiled=True)  16.5 us
  transfers between devices with their start and end apart: 8, of which 7 were waited for; matrix products, arithmetic and copies ran while one was open for 1% of the time, Pallas kernels for 26%

profile of v3, /device:TPU:0, one launch (start us, length us, event | category | flops | bytes accessed | tf_op | source)
XLA Modules:
  0.0 314.9 jit_solution(4221230828679034026)
XLA Ops:
  0.0 8.3 %shard_map.115 = bf16[16,2,2,16,1024]{4,3,2,1,0:T(8,128)(2,1)} custom-call(bf16[8,32,16,1024]{3,2,1,0:T(8,128)(2,1)} %map_ref.15, bf16[32,16,1024]{2,1,0:T(8,128)(2,1)} %obj_ref.7, bf16[1024,1024]{1,0:T(8,128)(2,1)} %constant.11.clone.fx_ref, bf16[512,512]{1,0:T(8,128)(2,1)} %constant.29.clone.kc_ref, bf16[512,512]{1,0:T(8,128)(2,1)} %constant.30.clone.ks_ref), custom_call_target="tpu_custom_call" | custom-call | tf_op jit(solution)/shard_map/pallas_call | solution.py:136
  8.3 6.4 %all-to-all-start.6 = ((bf16[16,2,2,16,1024]{4,3,2,1,0:T(8,128)(2,1)}), bf16[16,2,2,16,1024]{4,3,2,1,0:T(8,128)(2,1)S(1)}, u32[]{:S(2)}, u32[]{:S(2)}) async-start(bf16[16,2,2,16,1024]{4,3,2,1,0:T(8,128)(2,1)} %shard_map.115), calls=%async_computation.6 | async-start | bytes 4194304 | tf_op jit(solution)/shard_map/all_to_all | solution.py:152
  14.7 8.3 %shard_map.113 = bf16[16,2,2,16,1024]{4,3,2,1,0:T(8,128)(2,1)} custom-call(bf16[8,32,16,1024]{3,2,1,0:T(8,128)(2,1)} %map_ref.15, bf16[32,16,1024]{2,1,0:T(8,128)(2,1)} %obj_ref.7, bf16[1024,1024]{1,0:T(8,128)(2,1)} %constant.11.clone.fx_ref, bf16[512,512]{1,0:T(8,128)(2,1)} %constant.29.clone.kc_ref, bf16[512,512]{1,0:T(8,128)(2,1)} %constant.30.clone.ks_ref), custom_call_target="tpu_custom_call" | custom-call | tf_op jit(solution)/shard_map/pallas_call | solution.py:136
  23.0 19.6 %all-to-all-done.6.in_ref = bf16[16,2,2,16,1024]{4,3,2,1,0:T(8,128)(2,1)S(1)} async-done(((bf16[16,2,2,16,1024]{4,3,2,1,0:T(8,128)(2,1)}), bf16[16,2,2,16,1024]{4,3,2,1,0:T(8,128)(2,1)S(1)}, u32[]{:S(2)}, u32[]{:S(2)}) %all-to-all-start.6) | async-done | bytes 2097184 | tf_op jit(solution)/shard_map/all_to_all | solution.py:152
  47.7 8.2 %shard_map.111 = bf16[16,2,2,16,1024]{4,3,2,1,0:T(8,128)(2,1)} custom-call(bf16[8,32,16,1024]{3,2,1,0:T(8,128)(2,1)} %map_ref.15, bf16[32,16,1024]{2,1,0:T(8,128)(2,1)} %obj_ref.7, bf16[1024,1024]{1,0:T(8,128)(2,1)} %constant.11.clone.fx_ref, bf16[512,512]{1,0:T(8,128)(2,1)} %constant.29.clone.kc_ref, bf16[512,512]{1,0:T(8,128)(2,1)} %constant.30.clone.ks_ref), custom_call_target="tpu_custom_call" | custom-call | tf_op jit(solution)/shard_map/pallas_call | solution.py:136
  55.9 19.6 %all-to-all-done.4.in_ref = bf16[16,2,2,16,1024]{4,3,2,1,0:T(8,128)(2,1)S(1)} async-done(((bf16[16,2,2,16,1024]{4,3,2,1,0:T(8,128)(2,1)}), bf16[16,2,2,16,1024]{4,3,2,1,0:T(8,128)(2,1)S(1)}, u32[]{:S(2)}, u32[]{:S(2)}) %all-to-all-start.4) | async-done | bytes 2097184 | tf_op jit(solution)/shard_map/all_to_all | solution.py:152
  80.6 8.2 %shard_map.109 = bf16[16,2,2,16,1024]{4,3,2,1,0:T(8,128)(2,1)} custom-call(bf16[8,32,16,1024]{3,2,1,0:T(8,128)(2,1)} %map_ref.15, bf16[32,16,1024]{2,1,0:T(8,128)(2,1)} %obj_ref.7, bf16[1024,1024]{1,0:T(8,128)(2,1)} %constant.11.clone.fx_ref, bf16[512,512]{1,0:T(8,128)(2,1)} %constant.29.clone.kc_ref, bf16[512,512]{1,0:T(8,128)(2,1)} %constant.30.clone.ks_ref), custom_call_target="tpu_custom_call" | custom-call | tf_op jit(solution)/shard_map/pallas_call | solution.py:136
  88.8 19.6 %all-to-all-done.2.in_ref = bf16[16,2,2,16,1024]{4,3,2,1,0:T(8,128)(2,1)S(1)} async-done(((bf16[16,2,2,16,1024]{4,3,2,1,0:T(8,128)(2,1)}), bf16[16,2,2,16,1024]{4,3,2,1,0:T(8,128)(2,1)S(1)}, u32[]{:S(2)}, u32[]{:S(2)}) %all-to-all-start.2) | async-done | bytes 2097184 | tf_op jit(solution)/shard_map/all_to_all | solution.py:152
  115.9 6.2 %shard_map.116 = bf16[16,2,2,16,1024]{4,3,2,1,0:T(8,128)(2,1)} custom-call(bf16[16,2,2,16,1024]{4,3,2,1,0:T(8,128)(2,1)} %copy-done.4, s32[2,256,512]{2,1,0:T(8,128)} %reshape.6.mask_ref, bf16[512,512]{1,0:T(8,128)(2,1)} %constant.32.clone.wf_ref, bf16[512,512]{1,0:T(8,128)(2,1)} %constant.33.clone.wi_ref), custom_call_target="tpu_custom_call" | custom-call | tf_op jit(solution)/shard_map/pallas_call | solution.py:153
  122.2 19.2 %all-to-all-done.in_ref = bf16[16,2,2,16,1024]{4,3,2,1,0:T(8,128)(2,1)S(1)} async-done(((bf16[16,2,2,16,1024]{4,3,2,1,0:T(8,128)(2,1)}), bf16[16,2,2,16,1024]{4,3,2,1,0:T(8,128)(2,1)S(1)}, u32[]{:S(2)}, u32[]{:S(2)}) %all-to-all-start) | async-done | bytes 2097184 | tf_op jit(solution)/shard_map/all_to_all | solution.py:152
  142.7 4.4 %all-to-all-start.7 = ((bf16[16,2,2,16,1024]{4,3,2,1,0:T(8,128)(2,1)}), bf16[16,2,2,16,1024]{4,3,2,1,0:T(8,128)(2,1)}, u32[]{:S(2)}, u32[]{:S(2)}) async-start(bf16[16,2,2,16,1024]{4,3,2,1,0:T(8,128)(2,1)} %shard_map.116), calls=%async_computation.7 | async-start | bytes 4194304 | tf_op jit(solution)/shard_map/all_to_all | solution.py:168
  147.2 6.3 %shard_map.114 = bf16[16,2,2,16,1024]{4,3,2,1,0:T(8,128)(2,1)} custom-call(bf16[16,2,2,16,1024]{4,3,2,1,0:T(8,128)(2,1)} %copy-done.3, s32[2,256,512]{2,1,0:T(8,128)} %reshape.6.mask_ref, bf16[512,512]{1,0:T(8,128)(2,1)} %constant.32.clone.wf_ref, bf16[512,512]{1,0:T(8,128)(2,1)} %constant.33.clone.wi_ref), custom_call_target="tpu_custom_call" | custom-call | tf_op jit(solution)/shard_map/pallas_call | solution.py:153
  153.5 21.6 %all-to-all-done.7.in_ref = bf16[16,2,2,16,1024]{4,3,2,1,0:T(8,128)(2,1)} async-done(((bf16[16,2,2,16,1024]{4,3,2,1,0:T(8,128)(2,1)}), bf16[16,2,2,16,1024]{4,3,2,1,0:T(8,128)(2,1)}, u32[]{:S(2)}, u32[]{:S(2)}) %all-to-all-start.7) | async-done | bytes 2097184 | tf_op jit(solution)/shard_map/all_to_all | solution.py:168
  175.1 3.7 %all-to-all-start.5 = ((bf16[16,2,2,16,1024]{4,3,2,1,0:T(8,128)(2,1)}), bf16[16,2,2,16,1024]{4,3,2,1,0:T(8,128)(2,1)S(1)}, u32[]{:S(2)}, u32[]{:S(2)}) async-start(bf16[16,2,2,16,1024]{4,3,2,1,0:T(8,128)(2,1)} %shard_map.114), calls=%async_computation.5 | async-start | bytes 4194304 | tf_op jit(solution)/shard_map/all_to_all | solution.py:168
  178.8 6.3 %shard_map.112 = bf16[16,2,2,16,1024]{4,3,2,1,0:T(8,128)(2,1)} custom-call(bf16[16,2,2,16,1024]{4,3,2,1,0:T(8,128)(2,1)} %copy-done.2, s32[2,256,512]{2,1,0:T(8,128)} %reshape.6.mask_ref, bf16[512,512]{1,0:T(8,128)(2,1)} %constant.32.clone.wf_ref, bf16[512,512]{1,0:T(8,128)(2,1)} %constant.33.clone.wi_ref), custom_call_target="tpu_custom_call" | custom-call | tf_op jit(solution)/shard_map/pallas_call | solution.py:153
  185.1 21.6 %all-to-all-done.5.in_ref = bf16[16,2,2,16,1024]{4,3,2,1,0:T(8,128)(2,1)S(1)} async-done(((bf16[16,2,2,16,1024]{4,3,2,1,0:T(8,128)(2,1)}), bf16[16,2,2,16,1024]{4,3,2,1,0:T(8,128)(2,1)S(1)}, u32[]{:S(2)}, u32[]{:S(2)}) %all-to-all-start.5) | async-done | bytes 2097184 | tf_op jit(solution)/shard_map/all_to_all | solution.py:168
  208.0 4.6 %all-to-all-start.3 = ((bf16[16,2,2,16,1024]{4,3,2,1,0:T(8,128)(2,1)}), bf16[16,2,2,16,1024]{4,3,2,1,0:T(8,128)(2,1)}, u32[]{:S(2)}, u32[]{:S(2)}) async-start(bf16[16,2,2,16,1024]{4,3,2,1,0:T(8,128)(2,1)} %shard_map.112), calls=%async_computation.3 | async-start | bytes 4194304 | tf_op jit(solution)/shard_map/all_to_all | solution.py:168
  212.7 6.3 %shard_map.110 = bf16[16,2,2,16,1024]{4,3,2,1,0:T(8,128)(2,1)} custom-call(bf16[16,2,2,16,1024]{4,3,2,1,0:T(8,128)(2,1)} %copy-done.1, s32[2,256,512]{2,1,0:T(8,128)} %reshape.6.mask_ref, bf16[512,512]{1,0:T(8,128)(2,1)} %constant.32.clone.wf_ref, bf16[512,512]{1,0:T(8,128)(2,1)} %constant.33.clone.wi_ref), custom_call_target="tpu_custom_call" | custom-call | tf_op jit(solution)/shard_map/pallas_call | solution.py:153
  219.0 21.6 %all-to-all-done.3.in_ref = bf16[16,2,2,16,1024]{4,3,2,1,0:T(8,128)(2,1)} async-done(((bf16[16,2,2,16,1024]{4,3,2,1,0:T(8,128)(2,1)}), bf16[16,2,2,16,1024]{4,3,2,1,0:T(8,128)(2,1)}, u32[]{:S(2)}, u32[]{:S(2)}) %all-to-all-start.3) | async-done | bytes 2097184 | tf_op jit(solution)/shard_map/all_to_all | solution.py:168
  245.9 10.2 %shard_map.117.acc_ref = f32[32,16,1024]{2,1,0:T(8,128)} custom-call(bf16[16,2,2,16,1024]{4,3,2,1,0:T(8,128)(2,1)} %all-to-all-done.7.in_ref, bf16[8,32,16,1024]{3,2,1,0:T(8,128)(2,1)} %map_ref.15, bf16[512,512]{1,0:T(8,128)(2,1)} %constant.29.clone.kc_ref, bf16[512,512]{1,0:T(8,128)(2,1)} %constant.31.clone.ks_ref, ...), custom_call_target="tpu_custom_call", output_to_operand_aliasing={{}: (5, {})} | custom-call | tf_op jit(solution)/shard_map/pallas_call | solution.py:169
  256.1 10.2 %shard_map.118.acc_ref = f32[32,16,1024]{2,1,0:T(8,128)} custom-call(bf16[16,2,2,16,1024]{4,3,2,1,0:T(8,128)(2,1)} %copy-done.5, bf16[8,32,16,1024]{3,2,1,0:T(8,128)(2,1)} %map_ref.15, bf16[512,512]{1,0:T(8,128)(2,1)} %constant.29.clone.kc_ref, bf16[512,512]{1,0:T(8,128)(2,1)} %constant.31.clone.ks_ref, ...), custom_call_target="tpu_custom_call", output_to_operand_aliasing={{}: (5, {})} | custom-call | tf_op jit(solution)/shard_map/pallas_call | solution.py:169
  266.4 10.2 %shard_map.119.acc_ref = f32[32,16,1024]{2,1,0:T(8,128)} custom-call(bf16[16,2,2,16,1024]{4,3,2,1,0:T(8,128)(2,1)} %all-to-all-done.3.in_ref, bf16[8,32,16,1024]{3,2,1,0:T(8,128)(2,1)} %map_ref.15, bf16[512,512]{1,0:T(8,128)(2,1)} %constant.29.clone.kc_ref, bf16[512,512]{1,0:T(8,128)(2,1)} %constant.31.clone.ks_ref, ...), custom_call_target="tpu_custom_call", output_to_operand_aliasing={{}: (5, {})} | custom-call | tf_op jit(solution)/shard_map/pallas_call | solution.py:169
  277.9 10.2 %shard_map.120 = f32[32,16,1024]{2,1,0:T(8,128)} custom-call(bf16[16,2,2,16,1024]{4,3,2,1,0:T(8,128)(2,1)} %copy-done.6, bf16[8,32,16,1024]{3,2,1,0:T(8,128)(2,1)} %map_ref.15, bf16[512,512]{1,0:T(8,128)(2,1)} %constant.29.clone.kc_ref, bf16[512,512]{1,0:T(8,128)(2,1)} %constant.31.clone.ks_ref, ...), custom_call_target="tpu_custom_call", output_to_operand_aliasing={{}: (5, {})} | custom-call | tf_op jit(solution)/shard_map/pallas_call | solution.py:169
  289.9 24.1 %all_to_all.45 = bf16[8,4,16,1024]{3,2,1,0:T(8,128)(2,1)S(1)} all-to-all(bf16[8,4,16,1024]{3,2,1,0:T(8,128)(2,1)S(1)} %bitcast.1), channel_id=1, replica_groups=mesh['coil'=8,'pencil'=16] {'coil'}, dimensions={0} | all-to-all | bytes 2097152 | tf_op jit(solution)/shard_map/all_to_all | solution.py:189
  (26 shorter events, 29.6 us)
Async XLA Ops:
  0.0 113.5 %copy-start = (s32[32,256,4]{1,2,0:T(4,128)S(1)}, s32[32,256,4]{1,2,0:T(4,128)}, u32[]{:S(2)}) copy-start(s32[32,256,4]{1,2,0:T(4,128)} %param.13) | copy-start | bytes 393220
  8.3 34.3 %all-to-all-start.6 = ((bf16[16,2,2,16,1024]{4,3,2,1,0:T(8,128)(2,1)}), bf16[16,2,2,16,1024]{4,3,2,1,0:T(8,128)(2,1)S(1)}, u32[]{:S(2)}, u32[]{:S(2)}) async-start(bf16[16,2,2,16,1024]{4,3,2,1,0:T(8,128)(2,1)} %shard_map.115), calls=%async_computation.6 | async-start | bytes 4194304 | tf_op jit(solution)/shard_map/all_to_all | solution.py:152
  42.6 1.3 copy-start.4
  44.0 31.6 %all-to-all-start.4 = ((bf16[16,2,2,16,1024]{4,3,2,1,0:T(8,128)(2,1)}), bf16[16,2,2,16,1024]{4,3,2,1,0:T(8,128)(2,1)S(1)}, u32[]{:S(2)}, u32[]{:S(2)}) async-start(bf16[16,2,2,16,1024]{4,3,2,1,0:T(8,128)(2,1)} %shard_map.113), calls=%async_computation.4 | async-start | bytes 4194304 | tf_op jit(solution)/shard_map/all_to_all | solution.py:152
  75.5 1.4 copy-start.3
  76.9 31.6 %all-to-all-start.2 = ((bf16[16,2,2,16,1024]{4,3,2,1,0:T(8,128)(2,1)}), bf16[16,2,2,16,1024]{4,3,2,1,0:T(8,128)(2,1)S(1)}, u32[]{:S(2)}, u32[]{:S(2)}) async-start(bf16[16,2,2,16,1024]{4,3,2,1,0:T(8,128)(2,1)} %shard_map.111), calls=%async_computation.2 | async-start | bytes 4194304 | tf_op jit(solution)/shard_map/all_to_all | solution.py:152
  108.5 1.3 copy-start.2
  109.8 31.6 %all-to-all-start = ((bf16[16,2,2,16,1024]{4,3,2,1,0:T(8,128)(2,1)}), bf16[16,2,2,16,1024]{4,3,2,1,0:T(8,128)(2,1)S(1)}, u32[]{:S(2)}, u32[]{:S(2)}) async-start(bf16[16,2,2,16,1024]{4,3,2,1,0:T(8,128)(2,1)} %shard_map.109), calls=%async_computation | async-start | bytes 4194304 | tf_op jit(solution)/shard_map/all_to_all | solution.py:152
  141.4 1.4 copy-start.1
  142.7 32.3 %all-to-all-start.7 = ((bf16[16,2,2,16,1024]{4,3,2,1,0:T(8,128)(2,1)}), bf16[16,2,2,16,1024]{4,3,2,1,0:T(8,128)(2,1)}, u32[]{:S(2)}, u32[]{:S(2)}) async-start(bf16[16,2,2,16,1024]{4,3,2,1,0:T(8,128)(2,1)} %shard_map.116), calls=%async_computation.7 | async-start | bytes 4194304 | tf_op jit(solution)/shard_map/all_to_all | solution.py:168
  175.1 31.6 %all-to-all-start.5 = ((bf16[16,2,2,16,1024]{4,3,2,1,0:T(8,128)(2,1)}), bf16[16,2,2,16,1024]{4,3,2,1,0:T(8,128)(2,1)S(1)}, u32[]{:S(2)}, u32[]{:S(2)}) async-start(bf16[16,2,2,16,1024]{4,3,2,1,0:T(8,128)(2,1)} %shard_map.114), calls=%async_computation.5 | async-start | bytes 4194304 | tf_op jit(solution)/shard_map/all_to_all | solution.py:168
  206.7 1.4 copy-start.5
  208.0 32.5 %all-to-all-start.3 = ((bf16[16,2,2,16,1024]{4,3,2,1,0:T(8,128)(2,1)}), bf16[16,2,2,16,1024]{4,3,2,1,0:T(8,128)(2,1)}, u32[]{:S(2)}, u32[]{:S(2)}) async-start(bf16[16,2,2,16,1024]{4,3,2,1,0:T(8,128)(2,1)} %shard_map.112), calls=%async_computation.3 | async-start | bytes 4194304 | tf_op jit(solution)/shard_map/all_to_all | solution.py:168
  240.6 36.0 %all-to-all-start.1 = ((bf16[16,2,2,16,1024]{4,3,2,1,0:T(8,128)(2,1)}), bf16[16,2,2,16,1024]{4,3,2,1,0:T(8,128)(2,1)S(1)}, u32[]{:S(2)}, u32[]{:S(2)}) async-start(bf16[16,2,2,16,1024]{4,3,2,1,0:T(8,128)(2,1)} %shard_map.110), calls=%async_computation.1 | async-start | bytes 4194304 | tf_op jit(solution)/shard_map/all_to_all | solution.py:168
  276.6 1.3 copy-start.6

commit v4 on v3

--- a/solution.py
+++ b/solution.py
@@ -125,13 +125,13 @@
     mask = lax.dynamic_slice_in_dim(sample_mask, position * depth, depth, 0)
     mask = jnp.repeat(mask, segment, axis=2)
 
-    chunks = 4 if coils % 4 == 0 else 1
-    per = coils // chunks
+    tail = coils // 4
+    sizes = [coils - tail, tail] if tail > 0 else [coils]
     const2 = lambda c: (0, 0)
     const3 = lambda c: (0, 0, 0)
     acc = jnp.zeros((slices, rows, width), jnp.float32)
-    for chunk in range(chunks):
-        start = chunk * per
+    start = 0
+    for per in sizes:
         map_spec = pl.BlockSpec((None, slices, rows, width), lambda c, s=start: (c + s, 0, 0, 0))
         split = pl.pallas_call(
             forward_kernel,
@@ -184,6 +184,7 @@
                 vmem_limit_bytes=60 * 1024 * 1024, dimension_semantics=("arbitrary",)
             ),
         )(returned, coil_maps, kc_i, ks_i, inverse_x, acc)
+        start += per
     groups = lax.axis_size("coil")
     parts = acc.astype(jnp.bfloat16).reshape(groups, slices // groups, rows, width)
     parts = lax.all_to_all(parts, "coil", 0, 0, tiled=True)

time: 316 us -> 278 us (0.88)
  Pallas kernels: 99 us -> 79.4 us
  starting transfers between devices: 34.1 us -> 18.6 us
  local copies, waits for them, and re-layouts: 12.1 us -> 6.56 us
    pallas_call x4 -> x2, Pallas kernels: 40.9 us -> 31.5 us  [on_device(): pl.pallas_call(backward_kernel, grid=(per,), in_specs=[pl.BlockSpec((penc...]
    all_to_all x4 -> x2, starting transfers between devices: 16.5 us -> 8.35 us  [on_device(): returned = lax.all_to_all(lined, 'pencil', 0, 0, tiled=True)]
    all_to_all x4 -> x2, starting transfers between devices: 17.6 us -> 10.2 us  [on_device(): gathered = lax.all_to_all(split, 'pencil', 0, 0, tiled=True)]
    pallas_call x4 -> x2, Pallas kernels: 33 us -> 26.1 us  [on_device(): pl.pallas_call(forward_kernel, grid=(per,), in_specs=[map_spec, pl.BlockS...]
    all_to_all x4 -> x2, waiting for transfers between devices: 64.8 us -> 71.5 us  [on_device(): returned = lax.all_to_all(lined, 'pencil', 0, 0, tiled=True)]
    unnamed x14 -> x6, local copies, waits for them, and re-layouts: 8.08 us -> 2.65 us
    all_to_all x4 -> x2, waiting for transfers between devices: 78.1 us -> 74.7 us  [on_device(): gathered = lax.all_to_all(split, 'pencil', 0, 0, tiled=True)]
    pallas_call x4 -> x2, Pallas kernels: 25.1 us -> 21.8 us  [on_device(): pl.pallas_call(line_kernel, grid=(per, depth), in_specs=[pl.BlockSpec((pe...]
  transfers between devices with their start and end apart: 8 -> 4, of which waited for: 7 -> 4; matrix products, arithmetic and copies ran while one was open for 1% -> 1% of each run, Pallas kernels for 26% -> 19%
where the time goes in v4:
time: 278 us; the launch traced here: 277 us
  waiting for transfers between devices  146 us (53%)
  Pallas kernels  79.4 us (29%)
  blocking collectives  23.4 us (8%)
  starting transfers between devices  18.6 us (7%)
  local copies, waits for them, and re-layouts  6.56 us (2%)
    all_to_all x2, waiting for transfers between devices, on_device(): gathered = lax.all_to_all(split, 'pencil', 0, 0, tiled=True)  74.7 us
    all_to_all x2, waiting for transfers between devices, on_device(): returned = lax.all_to_all(lined, 'pencil', 0, 0, tiled=True)  71.5 us
    pallas_call x2, Pallas kernels, on_device(): pl.pallas_call(backward_kernel, grid=(per,), in_specs=[pl.BlockSpec((penc...  31.5 us
    pallas_call x2, Pallas kernels, on_device(): pl.pallas_call(forward_kernel, grid=(per,), in_specs=[map_spec, pl.BlockS...  26.1 us
    all_to_all x1, blocking collectives, on_device(): parts = lax.all_to_all(parts, 'coil', 0, 0, tiled=True)  23.4 us
    pallas_call x2, Pallas kernels, on_device(): pl.pallas_call(line_kernel, grid=(per, depth), in_specs=[pl.BlockSpec((pe...  21.8 us
    all_to_all x2, starting transfers between devices, on_device(): gathered = lax.all_to_all(split, 'pencil', 0, 0, tiled=True)  10.2 us
    all_to_all x2, starting transfers between devices, on_device(): returned = lax.all_to_all(lined, 'pencil', 0, 0, tiled=True)  8.35 us
  transfers between devices with their start and end apart: 4, of which 4 were waited for; matrix products, arithmetic and copies ran while one was open for 1% of the time, Pallas kernels for 19%

profile of v4, /device:TPU:0, one launch (start us, length us, event | category | flops | bytes accessed | tf_op | source)
XLA Modules:
  0.0 276.8 jit_solution(6671390866194036756)
XLA Ops:
  0.0 17.9 %shard_map.111 = bf16[16,6,2,16,1024]{4,3,2,1,0:T(8,128)(2,1)} custom-call(bf16[8,32,16,1024]{3,2,1,0:T(8,128)(2,1)} %map_ref.7, bf16[32,16,1024]{2,1,0:T(8,128)(2,1)} %obj_ref.3, bf16[1024,1024]{1,0:T(8,128)(2,1)} %constant.11.clone.fx_ref, bf16[512,512]{1,0:T(8,128)(2,1)} %constant.29.clone.kc_ref, bf16[512,512]{1,0:T(8,128)(2,1)} %constant.30.clone.ks_ref), custom_call_target="tpu_custom_call" | custom-call | tf_op jit(solution)/shard_map/pallas_call | solution.py:136
  17.9 6.5 %all-to-all-start.2 = ((bf16[16,6,2,16,1024]{4,3,2,1,0:T(8,128)(2,1)}), bf16[16,6,2,16,1024]{4,3,2,1,0:T(8,128)(2,1)}, u32[]{:S(2)}, u32[]{:S(2)}) async-start(bf16[16,6,2,16,1024]{4,3,2,1,0:T(8,128)(2,1)} %shard_map.111), calls=%async_computation.2 | async-start | bytes 12582912 | tf_op jit(solution)/shard_map/all_to_all | solution.py:152
  24.4 8.2 %shard_map.109 = bf16[16,2,2,16,1024]{4,3,2,1,0:T(8,128)(2,1)} custom-call(bf16[8,32,16,1024]{3,2,1,0:T(8,128)(2,1)} %map_ref.7, bf16[32,16,1024]{2,1,0:T(8,128)(2,1)} %obj_ref.3, bf16[1024,1024]{1,0:T(8,128)(2,1)} %constant.11.clone.fx_ref, bf16[512,512]{1,0:T(8,128)(2,1)} %constant.29.clone.kc_ref, bf16[512,512]{1,0:T(8,128)(2,1)} %constant.30.clone.ks_ref), custom_call_target="tpu_custom_call" | custom-call | tf_op jit(solution)/shard_map/pallas_call | solution.py:136
  32.6 64.6 %all-to-all-done.2.in_ref = bf16[16,6,2,16,1024]{4,3,2,1,0:T(8,128)(2,1)} async-done(((bf16[16,6,2,16,1024]{4,3,2,1,0:T(8,128)(2,1)}), bf16[16,6,2,16,1024]{4,3,2,1,0:T(8,128)(2,1)}, u32[]{:S(2)}, u32[]{:S(2)}) %all-to-all-start.2) | async-done | bytes 6291488 | tf_op jit(solution)/shard_map/all_to_all | solution.py:152
  97.3 3.7 %all-to-all-start = ((bf16[16,2,2,16,1024]{4,3,2,1,0:T(8,128)(2,1)}), bf16[16,2,2,16,1024]{4,3,2,1,0:T(8,128)(2,1)S(1)}, u32[]{:S(2)}, u32[]{:S(2)}) async-start(bf16[16,2,2,16,1024]{4,3,2,1,0:T(8,128)(2,1)} %shard_map.109), calls=%async_computation | async-start | bytes 4194304 | tf_op jit(solution)/shard_map/all_to_all | solution.py:152
  101.0 0.0 copy-done
  101.0 0.1 copy.14
  101.2 0.8 broadcast_in_dim.6
  102.0 1.4 reshape.6.mask_ref
  103.4 15.4 %shard_map.112 = bf16[16,6,2,16,1024]{4,3,2,1,0:T(8,128)(2,1)} custom-call(bf16[16,6,2,16,1024]{4,3,2,1,0:T(8,128)(2,1)} %all-to-all-done.2.in_ref, s32[2,256,512]{2,1,0:T(8,128)} %reshape.6.mask_ref, bf16[512,512]{1,0:T(8,128)(2,1)} %constant.32.clone.wf_ref, bf16[512,512]{1,0:T(8,128)(2,1)} %constant.33.clone.wi_ref), custom_call_target="tpu_custom_call" | custom-call | tf_op jit(solution)/shard_map/pallas_call | solution.py:153
  118.8 10.0 %all-to-all-done.in_ref = bf16[16,2,2,16,1024]{4,3,2,1,0:T(8,128)(2,1)S(1)} async-done(((bf16[16,2,2,16,1024]{4,3,2,1,0:T(8,128)(2,1)}), bf16[16,2,2,16,1024]{4,3,2,1,0:T(8,128)(2,1)S(1)}, u32[]{:S(2)}, u32[]{:S(2)}) %all-to-all-start) | async-done | bytes 2097184 | tf_op jit(solution)/shard_map/all_to_all | solution.py:152
  128.8 1.3 copy-done.1
  130.2 4.6 %all-to-all-start.3 = ((bf16[16,6,2,16,1024]{4,3,2,1,0:T(8,128)(2,1)}), bf16[16,6,2,16,1024]{4,3,2,1,0:T(8,128)(2,1)}, u32[]{:S(2)}, u32[]{:S(2)}) async-start(bf16[16,6,2,16,1024]{4,3,2,1,0:T(8,128)(2,1)} %shard_map.112), calls=%async_computation.3 | async-start | bytes 12582912 | tf_op jit(solution)/shard_map/all_to_all | solution.py:168
  134.8 6.3 %shard_map.110 = bf16[16,2,2,16,1024]{4,3,2,1,0:T(8,128)(2,1)} custom-call(bf16[16,2,2,16,1024]{4,3,2,1,0:T(8,128)(2,1)} %copy-done.1, s32[2,256,512]{2,1,0:T(8,128)} %reshape.6.mask_ref, bf16[512,512]{1,0:T(8,128)(2,1)} %constant.32.clone.wf_ref, bf16[512,512]{1,0:T(8,128)(2,1)} %constant.33.clone.wi_ref), custom_call_target="tpu_custom_call" | custom-call | tf_op jit(solution)/shard_map/pallas_call | solution.py:153
  141.1 66.5 %all-to-all-done.3.in_ref = bf16[16,6,2,16,1024]{4,3,2,1,0:T(8,128)(2,1)} async-done(((bf16[16,6,2,16,1024]{4,3,2,1,0:T(8,128)(2,1)}), bf16[16,6,2,16,1024]{4,3,2,1,0:T(8,128)(2,1)}, u32[]{:S(2)}, u32[]{:S(2)}) %all-to-all-start.3) | async-done | bytes 6291488 | tf_op jit(solution)/shard_map/all_to_all | solution.py:168
  207.6 3.7 %all-to-all-start.1 = ((bf16[16,2,2,16,1024]{4,3,2,1,0:T(8,128)(2,1)}), bf16[16,2,2,16,1024]{4,3,2,1,0:T(8,128)(2,1)S(1)}, u32[]{:S(2)}, u32[]{:S(2)}) async-start(bf16[16,2,2,16,1024]{4,3,2,1,0:T(8,128)(2,1)} %shard_map.110), calls=%async_computation.1 | async-start | bytes 4194304 | tf_op jit(solution)/shard_map/all_to_all | solution.py:168
  211.4 1.6 broadcast_in_dim.7.acc_ref
  212.9 21.3 %shard_map.113.acc_ref = f32[32,16,1024]{2,1,0:T(8,128)} custom-call(bf16[16,6,2,16,1024]{4,3,2,1,0:T(8,128)(2,1)} %all-to-all-done.3.in_ref, bf16[8,32,16,1024]{3,2,1,0:T(8,128)(2,1)} %map_ref.7, bf16[512,512]{1,0:T(8,128)(2,1)} %constant.29.clone.kc_ref, bf16[512,512]{1,0:T(8,128)(2,1)} %constant.31.clone.ks_ref, ...), custom_call_target="tpu_custom_call", output_to_operand_aliasing={{}: (5, {})} | custom-call | tf_op jit(solution)/shard_map/pallas_call | solution.py:169
  234.2 5.0 %all-to-all-done.1.in_ref = bf16[16,2,2,16,1024]{4,3,2,1,0:T(8,128)(2,1)S(1)} async-done(((bf16[16,2,2,16,1024]{4,3,2,1,0:T(8,128)(2,1)}), bf16[16,2,2,16,1024]{4,3,2,1,0:T(8,128)(2,1)S(1)}, u32[]{:S(2)}, u32[]{:S(2)}) %all-to-all-start.1) | async-done | bytes 2097184 | tf_op jit(solution)/shard_map/all_to_all | solution.py:168
  239.2 1.3 copy-done.2
  240.6 10.2 %shard_map.114 = f32[32,16,1024]{2,1,0:T(8,128)} custom-call(bf16[16,2,2,16,1024]{4,3,2,1,0:T(8,128)(2,1)} %copy-done.2, bf16[8,32,16,1024]{3,2,1,0:T(8,128)(2,1)} %map_ref.7, bf16[512,512]{1,0:T(8,128)(2,1)} %constant.29.clone.kc_ref, bf16[512,512]{1,0:T(8,128)(2,1)} %constant.31.clone.ks_ref, ...), custom_call_target="tpu_custom_call", output_to_operand_aliasing={{}: (5, {})} | custom-call | tf_op jit(solution)/shard_map/pallas_call | solution.py:169
  250.7 1.7 convert_element_type.6
  252.5 23.4 %all_to_all.25 = bf16[8,4,16,1024]{3,2,1,0:T(8,128)(2,1)S(1)} all-to-all(bf16[8,4,16,1024]{3,2,1,0:T(8,128)(2,1)S(1)} %bitcast.1), channel_id=1, replica_groups=mesh['coil'=8,'pencil'=16] {'coil'}, dimensions={0} | all-to-all | bytes 2097152 | tf_op jit(solution)/shard_map/all_to_all | solution.py:190
  275.9 0.9 convert_reduce_fusion
  (4 shorter events, 0.0 us)
Async XLA Ops:
  0.0 101.0 %copy-start = (s32[32,256,4]{1,2,0:T(4,128)S(1)}, s32[32,256,4]{1,2,0:T(4,128)}, u32[]{:S(2)}) copy-start(s32[32,256,4]{1,2,0:T(4,128)} %param.13) | copy-start | bytes 393220
  17.9 79.4 %all-to-all-start.2 = ((bf16[16,6,2,16,1024]{4,3,2,1,0:T(8,128)(2,1)}), bf16[16,6,2,16,1024]{4,3,2,1,0:T(8,128)(2,1)}, u32[]{:S(2)}, u32[]{:S(2)}) async-start(bf16[16,6,2,16,1024]{4,3,2,1,0:T(8,128)(2,1)} %shard_map.111), calls=%async_computation.2 | async-start | bytes 12582912 | tf_op jit(solution)/shard_map/all_to_all | solution.py:152
  97.3 31.6 %all-to-all-start = ((bf16[16,2,2,16,1024]{4,3,2,1,0:T(8,128)(2,1)}), bf16[16,2,2,16,1024]{4,3,2,1,0:T(8,128)(2,1)S(1)}, u32[]{:S(2)}, u32[]{:S(2)}) async-start(bf16[16,2,2,16,1024]{4,3,2,1,0:T(8,128)(2,1)} %shard_map.109), calls=%async_computation | async-start | bytes 4194304 | tf_op jit(solution)/shard_map/all_to_all | solution.py:152
  128.8 1.3 copy-start.1
  130.2 77.5 %all-to-all-start.3 = ((bf16[16,6,2,16,1024]{4,3,2,1,0:T(8,128)(2,1)}), bf16[16,6,2,16,1024]{4,3,2,1,0:T(8,128)(2,1)}, u32[]{:S(2)}, u32[]{:S(2)}) async-start(bf16[16,6,2,16,1024]{4,3,2,1,0:T(8,128)(2,1)} %shard_map.112), calls=%async_computation.3 | async-start | bytes 12582912 | tf_op jit(solution)/shard_map/all_to_all | solution.py:168
  207.6 31.6 %all-to-all-start.1 = ((bf16[16,2,2,16,1024]{4,3,2,1,0:T(8,128)(2,1)}), bf16[16,2,2,16,1024]{4,3,2,1,0:T(8,128)(2,1)S(1)}, u32[]{:S(2)}, u32[]{:S(2)}) async-start(bf16[16,2,2,16,1024]{4,3,2,1,0:T(8,128)(2,1)} %shard_map.110), calls=%async_computation.1 | async-start | bytes 4194304 | tf_op jit(solution)/shard_map/all_to_all | solution.py:168
  239.2 1.3 copy-start.2

commit v5 on v4

--- a/solution.py
+++ b/solution.py
@@ -1,3 +1,4 @@
+import functools
 import math
 
 import jax
@@ -77,15 +78,20 @@
     volume = in_ref[...].reshape(lines, width)
     stacked = jnp.concatenate([volume[:, :half], volume[:, half:]], axis=0)
     spectrum = dot32(wf_ref[...], stacked).astype(jnp.bfloat16)
-    keep = mask_ref[...] > 0
-    keep = jnp.concatenate([keep, keep], axis=0)
+    flags = mask_ref[...]
+    segments = flags.shape[1]
+    segment = half // segments
+    keep = jnp.concatenate(
+        [jnp.broadcast_to(flags[:, s : s + 1], (lines, segment)) for s in range(segments)], axis=1
+    )
+    keep = jnp.concatenate([keep, keep], axis=0) > 0
     sampled = jnp.where(keep, spectrum, jnp.zeros_like(spectrum))
     back = dot32(wi_ref[...], sampled).astype(jnp.bfloat16)
     result = jnp.concatenate([back[:lines], back[lines:]], axis=1)
     out_ref[...] = result.reshape(out_ref.shape)
 
 
-def backward_kernel(in_ref, map_ref, kc_ref, ks_ref, fx_ref, acc_ref, out_ref):
+def backward_kernel(first, last, in_ref, map_ref, kc_ref, ks_ref, fx_ref, *refs):
     depth, rows, width = map_ref.shape
     half = width // 2
     volume = in_ref[...].reshape(depth * rows, width)
@@ -97,12 +103,25 @@
     m_re, m_im = maps[:, :half], maps[:, half:]
     b_re, b_im = back_x[:, :half], back_x[:, half:]
     product = jnp.concatenate([m_re * b_re + m_im * b_im, m_re * b_im - m_im * b_re], axis=1)
-
-    @pl.when(pl.program_id(0) == 0)
+    product = product.reshape(depth, rows, width)
+    refs = list(refs)
+    acc_ref = None if first else refs.pop(0)
+    out_ref = refs.pop(0)
+    sum_ref = refs.pop(0) if last else out_ref
+    step = pl.program_id(0)
+
+    @pl.when(step == 0)
     def _():
-        out_ref[...] = acc_ref[...]
-
-    out_ref[...] += product.reshape(out_ref.shape)
+        sum_ref[...] = product if first else acc_ref[...] + product
+
+    @pl.when(step > 0)
+    def _():
+        sum_ref[...] += product
+
+    if last:
+        @pl.when(step == pl.num_programs(0) - 1)
+        def _():
+            out_ref[...] = sum_ref[...].astype(out_ref.dtype)
 
 
 def on_device(object_image, coil_maps, sample_mask):
@@ -113,7 +132,6 @@
     pencils = lax.axis_size("pencil")
     depth = slices // pencils
     lines = rows * pencils
-    segment = readout // sample_mask.shape[2]
     position = lax.axis_index("pencil")
 
     forward_x = readout_table(readout, -1.0)
@@ -123,13 +141,12 @@
     wf = block_table(lines, -1.0)
     wi = block_table(lines, 1.0)
     mask = lax.dynamic_slice_in_dim(sample_mask, position * depth, depth, 0)
-    mask = jnp.repeat(mask, segment, axis=2)
 
     tail = coils // 4
     sizes = [coils - tail, tail] if tail > 0 else [coils]
     const2 = lambda c: (0, 0)
     const3 = lambda c: (0, 0, 0)
-    acc = jnp.zeros((slices, rows, width), jnp.float32)
+    acc = None
     start = 0
     for per in sizes:
         map_spec = pl.BlockSpec((None, slices, rows, width), lambda c, s=start: (c + s, 0, 0, 0))
@@ -155,7 +172,7 @@
             grid=(per, depth),
             in_specs=[
                 pl.BlockSpec((pencils, None, None, rows, width), lambda c, k: (0, c, k, 0, 0)),
-                pl.BlockSpec((None, lines, readout), lambda c, k: (k, 0, 0)),
+                pl.BlockSpec((None, lines, sample_mask.shape[2]), lambda c, k: (k, 0, 0)),
                 pl.BlockSpec((2 * lines, 2 * lines), lambda c, k: (0, 0)),
                 pl.BlockSpec((2 * lines, 2 * lines), lambda c, k: (0, 0)),
             ],
@@ -166,27 +183,34 @@
             compiler_params=PARAMS,
         )(gathered, mask, wf, wi)
         returned = lax.all_to_all(lined, "pencil", 0, 0, tiled=True)
+        first, last = start == 0, start + per == coils
+        operands = [returned, coil_maps, kc_i, ks_i, inverse_x]
+        in_specs = [
+            pl.BlockSpec((pencils, None, depth, rows, width), lambda c: (0, c, 0, 0, 0)),
+            map_spec,
+            pl.BlockSpec((slices * rows, slices * rows), const2),
+            pl.BlockSpec((slices * rows, slices * rows), const2),
+            pl.BlockSpec((width, width), const2),
+        ]
+        if not first:
+            operands.append(acc)
+            in_specs.append(pl.BlockSpec((slices, rows, width), const3))
         acc = pl.pallas_call(
-            backward_kernel,
+            functools.partial(backward_kernel, first, last),
             grid=(per,),
-            in_specs=[
-                pl.BlockSpec((pencils, None, depth, rows, width), lambda c: (0, c, 0, 0, 0)),
-                map_spec,
-                pl.BlockSpec((slices * rows, slices * rows), const2),
-                pl.BlockSpec((slices * rows, slices * rows), const2),
-                pl.BlockSpec((width, width), const2),
-                pl.BlockSpec((slices, rows, width), const3),
-            ],
+            in_specs=in_specs,
             out_specs=pl.BlockSpec((slices, rows, width), const3),
-            out_shape=jax.ShapeDtypeStruct((slices, rows, width), jnp.float32),
-            input_output_aliases={5: 0},
+            out_shape=jax.ShapeDtypeStruct(
+                (slices, rows, width), jnp.bfloat16 if last else jnp.float32
+            ),
+            scratch_shapes=[pltpu.VMEM((slices, rows, width), jnp.float32)] if last else [],
             compiler_params=pltpu.CompilerParams(
                 vmem_limit_bytes=60 * 1024 * 1024, dimension_semantics=("arbitrary",)
             ),
-        )(returned, coil_maps, kc_i, ks_i, inverse_x, acc)
+        )(*operands)
         start += per
     groups = lax.axis_size("coil")
-    parts = acc.astype(jnp.bfloat16).reshape(groups, slices // groups, rows, width)
+    parts = acc.reshape(groups, slices // groups, rows, width)
     parts = lax.all_to_all(parts, "coil", 0, 0, tiled=True)
     return jnp.sum(parts.astype(jnp.float32), axis=0)
 

time: 278 us -> 276 us (level)
  waiting for transfers between devices: 146 us -> 151 us
  local copies, waits for them, and re-layouts: 6.56 us -> 3.48 us
  transfers between devices with their start and end apart: 4 -> 4, of which waited for: 4 -> 4; matrix products, arithmetic and copies ran while one was open for 1% -> 0% of each run, Pallas kernels for 19% -> 18%
where the time goes in v5:
time: 276 us; the launch traced here: 275 us
  waiting for transfers between devices  151 us (55%)
  Pallas kernels  76.9 us (28%)
  blocking collectives  23.6 us (9%)
  starting transfers between devices  18.6 us (7%)
  local copies, waits for them, and re-layouts  3.48 us (1%)
    all_to_all x2, waiting for transfers between devices, on_device(): gathered = lax.all_to_all(split, 'pencil', 0, 0, tiled=True)  77.1 us
    all_to_all x2, waiting for transfers between devices, on_device(): returned = lax.all_to_all(lined, 'pencil', 0, 0, tiled=True)  74.2 us
    pallas_call x2, Pallas kernels, on_device(): pl.pallas_call(functools.partial(backward_kernel, first, last), grid=(per...  30.2 us
    pallas_call x2, Pallas kernels, on_device(): pl.pallas_call(forward_kernel, grid=(per,), in_specs=[map_spec, pl.BlockS...  26.1 us
    all_to_all x1, blocking collectives, on_device(): parts = lax.all_to_all(parts, 'coil', 0, 0, tiled=True)  23.6 us
    pallas_call x2, Pallas kernels, on_device(): pl.pallas_call(line_kernel, grid=(per, depth), in_specs=[pl.BlockSpec((pe...  20.6 us
    all_to_all x2, starting transfers between devices, on_device(): gathered = lax.all_to_all(split, 'pencil', 0, 0, tiled=True)  10.2 us
    all_to_all x2, starting transfers between devices, on_device(): returned = lax.all_to_all(lined, 'pencil', 0, 0, tiled=True)  8.35 us
  transfers between devices with their start and end apart: 4, of which 4 were waited for; matrix products, arithmetic and copies ran while one was open for 0% of the time, Pallas kernels for 18%

profile of v5, /device:TPU:0, one launch (start us, length us, event | category | flops | bytes accessed | tf_op | source)
XLA Modules:
  0.0 274.8 jit_solution(7513590134596733890)
XLA Ops:
  0.0 0.0 copy-start
  0.0 17.9 %shard_map.111 = bf16[16,6,2,16,1024]{4,3,2,1,0:T(8,128)(2,1)} custom-call(bf16[8,32,16,1024]{3,2,1,0:T(8,128)(2,1)} %map_ref.7, bf16[32,16,1024]{2,1,0:T(8,128)(2,1)} %obj_ref.3, bf16[1024,1024]{1,0:T(8,128)(2,1)} %constant.26.clone.fx_ref, bf16[512,512]{1,0:T(8,128)(2,1)} %constant.28.clone.kc_ref, bf16[512,512]{1,0:T(8,128)(2,1)} %constant.29.clone.ks_ref), custom_call_target="tpu_custom_call" | custom-call | tf_op jit(solution)/shard_map/pallas_call | solution.py:153
  17.9 6.5 %all-to-all-start.2 = ((bf16[16,6,2,16,1024]{4,3,2,1,0:T(8,128)(2,1)}), bf16[16,6,2,16,1024]{4,3,2,1,0:T(8,128)(2,1)}, u32[]{:S(2)}, u32[]{:S(2)}) async-start(bf16[16,6,2,16,1024]{4,3,2,1,0:T(8,128)(2,1)} %shard_map.111), calls=%async_computation.2 | async-start | bytes 12582912 | tf_op jit(solution)/shard_map/all_to_all | solution.py:169
  24.4 8.2 %shard_map.109 = bf16[16,2,2,16,1024]{4,3,2,1,0:T(8,128)(2,1)} custom-call(bf16[8,32,16,1024]{3,2,1,0:T(8,128)(2,1)} %map_ref.7, bf16[32,16,1024]{2,1,0:T(8,128)(2,1)} %obj_ref.3, bf16[1024,1024]{1,0:T(8,128)(2,1)} %constant.26.clone.fx_ref, bf16[512,512]{1,0:T(8,128)(2,1)} %constant.28.clone.kc_ref, bf16[512,512]{1,0:T(8,128)(2,1)} %constant.29.clone.ks_ref), custom_call_target="tpu_custom_call" | custom-call | tf_op jit(solution)/shard_map/pallas_call | solution.py:153
  32.6 64.6 %all-to-all-done.2.in_ref = bf16[16,6,2,16,1024]{4,3,2,1,0:T(8,128)(2,1)} async-done(((bf16[16,6,2,16,1024]{4,3,2,1,0:T(8,128)(2,1)}), bf16[16,6,2,16,1024]{4,3,2,1,0:T(8,128)(2,1)}, u32[]{:S(2)}, u32[]{:S(2)}) %all-to-all-start.2) | async-done | bytes 6291488 | tf_op jit(solution)/shard_map/all_to_all | solution.py:169
  97.3 3.7 %all-to-all-start = ((bf16[16,2,2,16,1024]{4,3,2,1,0:T(8,128)(2,1)}), bf16[16,2,2,16,1024]{4,3,2,1,0:T(8,128)(2,1)S(1)}, u32[]{:S(2)}, u32[]{:S(2)}) async-start(bf16[16,2,2,16,1024]{4,3,2,1,0:T(8,128)(2,1)} %shard_map.109), calls=%async_computation | async-start | bytes 4194304 | tf_op jit(solution)/shard_map/all_to_all | solution.py:169
  101.0 0.0 copy-done
  101.0 0.9 copy.13.mask_ref
  101.9 14.5 %shard_map.112 = bf16[16,6,2,16,1024]{4,3,2,1,0:T(8,128)(2,1)} custom-call(bf16[16,6,2,16,1024]{4,3,2,1,0:T(8,128)(2,1)} %all-to-all-done.2.in_ref, s32[2,256,4]{2,1,0:T(8,128)} %copy.13.mask_ref, bf16[512,512]{1,0:T(8,128)(2,1)} %constant.31.clone.wf_ref, bf16[512,512]{1,0:T(8,128)(2,1)} %constant.32.clone.wi_ref), custom_call_target="tpu_custom_call" | custom-call | tf_op jit(solution)/shard_map/pallas_call | solution.py:170
  116.4 12.5 %all-to-all-done.in_ref = bf16[16,2,2,16,1024]{4,3,2,1,0:T(8,128)(2,1)S(1)} async-done(((bf16[16,2,2,16,1024]{4,3,2,1,0:T(8,128)(2,1)}), bf16[16,2,2,16,1024]{4,3,2,1,0:T(8,128)(2,1)S(1)}, u32[]{:S(2)}, u32[]{:S(2)}) %all-to-all-start) | async-done | bytes 2097184 | tf_op jit(solution)/shard_map/all_to_all | solution.py:169
  128.8 0.0 copy-start.1
  128.8 1.3 copy-done.1
  130.2 4.6 %all-to-all-start.3 = ((bf16[16,6,2,16,1024]{4,3,2,1,0:T(8,128)(2,1)}), bf16[16,6,2,16,1024]{4,3,2,1,0:T(8,128)(2,1)}, u32[]{:S(2)}, u32[]{:S(2)}) async-start(bf16[16,6,2,16,1024]{4,3,2,1,0:T(8,128)(2,1)} %shard_map.112), calls=%async_computation.3 | async-start | bytes 12582912 | tf_op jit(solution)/shard_map/all_to_all | solution.py:185
  134.8 6.1 %shard_map.110 = bf16[16,2,2,16,1024]{4,3,2,1,0:T(8,128)(2,1)} custom-call(bf16[16,2,2,16,1024]{4,3,2,1,0:T(8,128)(2,1)} %copy-done.1, s32[2,256,4]{2,1,0:T(8,128)} %copy.13.mask_ref, bf16[512,512]{1,0:T(8,128)(2,1)} %constant.31.clone.wf_ref, bf16[512,512]{1,0:T(8,128)(2,1)} %constant.32.clone.wi_ref), custom_call_target="tpu_custom_call" | custom-call | tf_op jit(solution)/shard_map/pallas_call | solution.py:170
  140.8 66.8 %all-to-all-done.3.in_ref = bf16[16,6,2,16,1024]{4,3,2,1,0:T(8,128)(2,1)} async-done(((bf16[16,6,2,16,1024]{4,3,2,1,0:T(8,128)(2,1)}), bf16[16,6,2,16,1024]{4,3,2,1,0:T(8,128)(2,1)}, u32[]{:S(2)}, u32[]{:S(2)}) %all-to-all-start.3) | async-done | bytes 6291488 | tf_op jit(solution)/shard_map/all_to_all | solution.py:185
  207.6 3.7 %all-to-all-start.1 = ((bf16[16,2,2,16,1024]{4,3,2,1,0:T(8,128)(2,1)}), bf16[16,2,2,16,1024]{4,3,2,1,0:T(8,128)(2,1)S(1)}, u32[]{:S(2)}, u32[]{:S(2)}) async-start(bf16[16,2,2,16,1024]{4,3,2,1,0:T(8,128)(2,1)} %shard_map.110), calls=%async_computation.1 | async-start | bytes 4194304 | tf_op jit(solution)/shard_map/all_to_all | solution.py:185
  211.4 20.4 %shard_map.113.refs_0_ = f32[32,16,1024]{2,1,0:T(8,128)} custom-call(bf16[16,6,2,16,1024]{4,3,2,1,0:T(8,128)(2,1)} %all-to-all-done.3.in_ref, bf16[8,32,16,1024]{3,2,1,0:T(8,128)(2,1)} %map_ref.7, bf16[512,512]{1,0:T(8,128)(2,1)} %constant.28.clone.kc_ref, bf16[512,512]{1,0:T(8,128)(2,1)} %constant.30.clone.ks_ref, bf16[1024,1024]{1,0:T(8,128)(2,1)} %constant.27.clone.fx_ref), custom_call_target="tpu_custom_call" | custom-call | tf_op jit(solution)/shard_map/pallas_call | solution.py:198
  231.8 7.4 %all-to-all-done.1.in_ref = bf16[16,2,2,16,1024]{4,3,2,1,0:T(8,128)(2,1)S(1)} async-done(((bf16[16,2,2,16,1024]{4,3,2,1,0:T(8,128)(2,1)}), bf16[16,2,2,16,1024]{4,3,2,1,0:T(8,128)(2,1)S(1)}, u32[]{:S(2)}, u32[]{:S(2)}) %all-to-all-start.1) | async-done | bytes 2097184 | tf_op jit(solution)/shard_map/all_to_all | solution.py:185
  239.2 0.0 copy-start.2
  239.2 1.3 copy-done.2
  240.5 9.8 %shard_map.114 = bf16[32,16,1024]{2,1,0:T(8,128)(2,1)} custom-call(bf16[16,2,2,16,1024]{4,3,2,1,0:T(8,128)(2,1)} %copy-done.2, bf16[8,32,16,1024]{3,2,1,0:T(8,128)(2,1)} %map_ref.7, bf16[512,512]{1,0:T(8,128)(2,1)} %constant.28.clone.kc_ref, bf16[512,512]{1,0:T(8,128)(2,1)} %constant.30.clone.ks_ref, bf16[1024,1024]{1,0:T(8,128)(2,1)} %constant.27.clone.fx_ref, ...), custom_call_target="tpu_custom_call" | custom-call | tf_op jit(solution)/shard_map/pallas_call | solution.py:198
  250.3 23.6 %all_to_all.25 = bf16[8,4,16,1024]{3,2,1,0:T(8,128)(2,1)S(1)} all-to-all(bf16[8,4,16,1024]{3,2,1,0:T(8,128)(2,1)} %bitcast.1), channel_id=1, replica_groups=mesh['coil'=8,'pencil'=16] {'coil'}, dimensions={0} | all-to-all | bytes 2097152 | tf_op jit(solution)/shard_map/all_to_all | solution.py:214
  274.0 0.9 convert_reduce_fusion
  (1 shorter events, 0.0 us)
Async XLA Ops:
  0.0 101.0 %copy-start = (s32[32,256,4]{1,2,0:T(4,128)S(1)}, s32[32,256,4]{1,2,0:T(4,128)}, u32[]{:S(2)}) copy-start(s32[32,256,4]{1,2,0:T(4,128)} %param.13) | copy-start | bytes 393220
  17.9 79.4 %all-to-all-start.2 = ((bf16[16,6,2,16,1024]{4,3,2,1,0:T(8,128)(2,1)}), bf16[16,6,2,16,1024]{4,3,2,1,0:T(8,128)(2,1)}, u32[]{:S(2)}, u32[]{:S(2)}) async-start(bf16[16,6,2,16,1024]{4,3,2,1,0:T(8,128)(2,1)} %shard_map.111), calls=%async_computation.2 | async-start | bytes 12582912 | tf_op jit(solution)/shard_map/all_to_all | solution.py:169
  97.3 31.6 %all-to-all-start = ((bf16[16,2,2,16,1024]{4,3,2,1,0:T(8,128)(2,1)}), bf16[16,2,2,16,1024]{4,3,2,1,0:T(8,128)(2,1)S(1)}, u32[]{:S(2)}, u32[]{:S(2)}) async-start(bf16[16,2,2,16,1024]{4,3,2,1,0:T(8,128)(2,1)} %shard_map.109), calls=%async_computation | async-start | bytes 4194304 | tf_op jit(solution)/shard_map/all_to_all | solution.py:169
  128.8 1.3 copy-start.1
  130.2 77.5 %all-to-all-start.3 = ((bf16[16,6,2,16,1024]{4,3,2,1,0:T(8,128)(2,1)}), bf16[16,6,2,16,1024]{4,3,2,1,0:T(8,128)(2,1)}, u32[]{:S(2)}, u32[]{:S(2)}) async-start(bf16[16,6,2,16,1024]{4,3,2,1,0:T(8,128)(2,1)} %shard_map.112), calls=%async_computation.3 | async-start | bytes 12582912 | tf_op jit(solution)/shard_map/all_to_all | solution.py:185
  207.6 31.6 %all-to-all-start.1 = ((bf16[16,2,2,16,1024]{4,3,2,1,0:T(8,128)(2,1)}), bf16[16,2,2,16,1024]{4,3,2,1,0:T(8,128)(2,1)S(1)}, u32[]{:S(2)}, u32[]{:S(2)}) async-start(bf16[16,2,2,16,1024]{4,3,2,1,0:T(8,128)(2,1)} %shard_map.110), calls=%async_computation.1 | async-start | bytes 4194304 | tf_op jit(solution)/shard_map/all_to_all | solution.py:185
  239.2 1.3 copy-start.2

commit v6 on v5

--- a/solution.py
+++ b/solution.py
@@ -71,7 +71,7 @@
     out_ref[...] = along_z.reshape(out_ref.shape)
 
 
-def line_kernel(in_ref, mask_ref, wf_ref, wi_ref, out_ref):
+def line_kernel(aliased, in_ref, mask_ref, wf_ref, wi_ref, *refs):
     groups, rows, width = in_ref.shape
     half = width // 2
     lines = groups * rows
@@ -88,6 +88,7 @@
     sampled = jnp.where(keep, spectrum, jnp.zeros_like(spectrum))
     back = dot32(wi_ref[...], sampled).astype(jnp.bfloat16)
     result = jnp.concatenate([back[:lines], back[lines:]], axis=1)
+    out_ref = refs[-1]
     out_ref[...] = result.reshape(out_ref.shape)
 
 
@@ -142,19 +143,23 @@
     wi = block_table(lines, 1.0)
     mask = lax.dynamic_slice_in_dim(sample_mask, position * depth, depth, 0)
 
-    tail = coils // 4
-    sizes = [coils - tail, tail] if tail > 0 else [coils]
+    q = coils // 4
+    outgoing = [q, 2 * q, q] if q > 0 else [coils]
+    incoming = [3 * q, q] if q > 0 else [coils]
     const2 = lambda c: (0, 0)
     const3 = lambda c: (0, 0, 0)
-    acc = None
+
+    def map_spec(start):
+        return pl.BlockSpec((None, slices, rows, width), lambda c: (c + start, 0, 0, 0))
+
+    gathered = []
     start = 0
-    for per in sizes:
-        map_spec = pl.BlockSpec((None, slices, rows, width), lambda c, s=start: (c + s, 0, 0, 0))
+    for per in outgoing:
         split = pl.pallas_call(
             forward_kernel,
             grid=(per,),
             in_specs=[
-                map_spec,
+                map_spec(start),
                 pl.BlockSpec((slices, rows, width), const3),
                 pl.BlockSpec((width, width), const2),
                 pl.BlockSpec((slices * rows, slices * rows), const2),
@@ -166,28 +171,48 @@
             out_shape=jax.ShapeDtypeStruct((pencils, per, depth, rows, width), jnp.bfloat16),
             compiler_params=PARAMS,
         )(coil_maps, object_image, forward_x, kc_f, ks_f)
-        gathered = lax.all_to_all(split, "pencil", 0, 0, tiled=True)
-        lined = pl.pallas_call(
-            line_kernel,
+        gathered.append((start, per, lax.all_to_all(split, "pencil", 0, 0, tiled=True)))
+        start += per
+
+    offsets = [sum(incoming[:j]) for j in range(len(incoming))]
+    buffers = [None] * len(incoming)
+    for start, per, volume in gathered:
+        j = max(i for i in range(len(incoming)) if offsets[i] <= start)
+        shift = start - offsets[j]
+        operands = [volume, mask, wf, wi]
+        in_specs = [
+            pl.BlockSpec((pencils, None, None, rows, width), lambda c, k: (0, c, k, 0, 0)),
+            pl.BlockSpec((None, lines, sample_mask.shape[2]), lambda c, k: (k, 0, 0)),
+            pl.BlockSpec((2 * lines, 2 * lines), lambda c, k: (0, 0)),
+            pl.BlockSpec((2 * lines, 2 * lines), lambda c, k: (0, 0)),
+        ]
+        aliases = {}
+        if buffers[j] is not None:
+            operands.append(buffers[j])
+            in_specs.append(pl.BlockSpec(memory_space=pl.ANY))
+            aliases = {4: 0}
+        buffers[j] = pl.pallas_call(
+            functools.partial(line_kernel, buffers[j] is not None),
             grid=(per, depth),
-            in_specs=[
-                pl.BlockSpec((pencils, None, None, rows, width), lambda c, k: (0, c, k, 0, 0)),
-                pl.BlockSpec((None, lines, sample_mask.shape[2]), lambda c, k: (k, 0, 0)),
-                pl.BlockSpec((2 * lines, 2 * lines), lambda c, k: (0, 0)),
-                pl.BlockSpec((2 * lines, 2 * lines), lambda c, k: (0, 0)),
-            ],
+            in_specs=in_specs,
             out_specs=pl.BlockSpec(
-                (pencils, None, None, rows, width), lambda c, k: (0, c, k, 0, 0)
-            ),
-            out_shape=jax.ShapeDtypeStruct((pencils, per, depth, rows, width), jnp.bfloat16),
+                (pencils, None, None, rows, width), lambda c, k: (0, c + shift, k, 0, 0)
+            ),
+            out_shape=jax.ShapeDtypeStruct(
+                (pencils, incoming[j], depth, rows, width), jnp.bfloat16
+            ),
+            input_output_aliases=aliases,
             compiler_params=PARAMS,
-        )(gathered, mask, wf, wi)
+        )(*operands)
+
+    acc = None
+    for start, per, lined in zip(offsets, incoming, buffers):
         returned = lax.all_to_all(lined, "pencil", 0, 0, tiled=True)
         first, last = start == 0, start + per == coils
         operands = [returned, coil_maps, kc_i, ks_i, inverse_x]
         in_specs = [
             pl.BlockSpec((pencils, None, depth, rows, width), lambda c: (0, c, 0, 0, 0)),
-            map_spec,
+            map_spec(start),
             pl.BlockSpec((slices * rows, slices * rows), const2),
             pl.BlockSpec((slices * rows, slices * rows), const2),
             pl.BlockSpec((width, width), const2),
@@ -208,7 +233,6 @@
                 vmem_limit_bytes=60 * 1024 * 1024, dimension_semantics=("arbitrary",)
             ),
         )(*operands)
-        start += per
     groups = lax.axis_size("coil")
     parts = acc.reshape(groups, slices // groups, rows, width)
     parts = lax.all_to_all(parts, "coil", 0, 0, tiled=True)

time: 276 us -> 277 us (level)
  waiting for transfers between devices: 151 us -> 142 us
  Pallas kernels: 76.9 us -> 81.9 us
  starting transfers between devices: 18.6 us -> 23.2 us
    all_to_all x2 -> x3, waiting for transfers between devices: 77.1 us -> 67.8 us  [on_device(): lax.all_to_all(split, 'pencil', 0, 0, tiled=True)]
    pallas_call x4 -> x6, Pallas kernels: 46.7 us -> 51.6 us  [the longest x3 29.5 us: on_device(): pl.pallas_call(forward_kernel, grid=(per,), in_specs=[map_spec(start), pl...]
    all_to_all x2 -> x3, starting transfers between devices: 10.2 us -> 14.7 us  [on_device(): lax.all_to_all(split, 'pencil', 0, 0, tiled=True)]
  transfers between devices with their start and end apart: 4 -> 5, of which waited for: 4 -> 5; matrix products, arithmetic and copies ran while one was open for 0% -> 0% of each run, Pallas kernels for 18% -> 23%
where the time goes in v6:
time: 277 us; the launch traced here: 276 us
  waiting for transfers between devices  142 us (51%)
  Pallas kernels  81.9 us (30%)
  blocking collectives  23.6 us (9%)
  starting transfers between devices  23.2 us (8%)
  local copies, waits for them, and re-layouts  4.8 us (2%)
    all_to_all x2, waiting for transfers between devices, on_device(): returned = lax.all_to_all(lined, 'pencil', 0, 0, tiled=True)  74.1 us
    all_to_all x3, waiting for transfers between devices, on_device(): lax.all_to_all(split, 'pencil', 0, 0, tiled=True)  67.8 us
    pallas_call x2, Pallas kernels, on_device(): pl.pallas_call(functools.partial(backward_kernel, first, last), grid=(per...  30.2 us
    pallas_call x3, Pallas kernels, on_device(): pl.pallas_call(forward_kernel, grid=(per,), in_specs=[map_spec(start), pl...  29.5 us
    all_to_all x1, blocking collectives, on_device(): parts = lax.all_to_all(parts, 'coil', 0, 0, tiled=True)  23.6 us
    pallas_call x3, Pallas kernels, on_device(): pl.pallas_call(functools.partial(line_kernel, buffers[j] is not None), gr...  22.2 us
    all_to_all x3, starting transfers between devices, on_device(): lax.all_to_all(split, 'pencil', 0, 0, tiled=True)  14.7 us
    all_to_all x2, starting transfers between devices, on_device(): returned = lax.all_to_all(lined, 'pencil', 0, 0, tiled=True)  8.53 us
  transfers between devices with their start and end apart: 5, of which 5 were waited for; matrix products, arithmetic and copies ran while one was open for 0% of the time, Pallas kernels for 23%

profile of v6, /device:TPU:0, one launch (start us, length us, event | category | flops | bytes accessed | tf_op | source)
XLA Modules:
  0.0 276.4 jit_solution(17033683243122988461)
XLA Ops:
  0.0 8.2 %shard_map.112 = bf16[16,2,2,16,1024]{4,3,2,1,0:T(8,128)(2,1)} custom-call(bf16[8,32,16,1024]{3,2,1,0:T(8,128)(2,1)} %map_ref.9, bf16[32,16,1024]{2,1,0:T(8,128)(2,1)} %obj_ref.5, bf16[1024,1024]{1,0:T(8,128)(2,1)} %constant.26.clone.fx_ref, bf16[512,512]{1,0:T(8,128)(2,1)} %constant.28.clone.kc_ref, bf16[512,512]{1,0:T(8,128)(2,1)} %constant.29.clone.ks_ref), custom_call_target="tpu_custom_call" | custom-call | tf_op jit(solution)/shard_map/pallas_call | solution.py:158
  8.2 6.4 %all-to-all-start.3 = ((bf16[16,2,2,16,1024]{4,3,2,1,0:T(8,128)(2,1)}), bf16[16,2,2,16,1024]{4,3,2,1,0:T(8,128)(2,1)S(1)}, u32[]{:S(2)}, u32[]{:S(2)}) async-start(bf16[16,2,2,16,1024]{4,3,2,1,0:T(8,128)(2,1)} %shard_map.112), calls=%async_computation.3 | async-start | bytes 4194304 | tf_op jit(solution)/shard_map/all_to_all | solution.py:174
  14.7 13.0 %shard_map.111 = bf16[16,4,2,16,1024]{4,3,2,1,0:T(8,128)(2,1)} custom-call(bf16[8,32,16,1024]{3,2,1,0:T(8,128)(2,1)} %map_ref.9, bf16[32,16,1024]{2,1,0:T(8,128)(2,1)} %obj_ref.5, bf16[1024,1024]{1,0:T(8,128)(2,1)} %constant.26.clone.fx_ref, bf16[512,512]{1,0:T(8,128)(2,1)} %constant.28.clone.kc_ref, bf16[512,512]{1,0:T(8,128)(2,1)} %constant.29.clone.ks_ref), custom_call_target="tpu_custom_call" | custom-call | tf_op jit(solution)/shard_map/pallas_call | solution.py:158
  27.7 14.9 %all-to-all-done.3.in_ref = bf16[16,2,2,16,1024]{4,3,2,1,0:T(8,128)(2,1)S(1)} async-done(((bf16[16,2,2,16,1024]{4,3,2,1,0:T(8,128)(2,1)}), bf16[16,2,2,16,1024]{4,3,2,1,0:T(8,128)(2,1)S(1)}, u32[]{:S(2)}, u32[]{:S(2)}) %all-to-all-start.3) | async-done | bytes 2097184 | tf_op jit(solution)/shard_map/all_to_all | solution.py:174
  42.6 1.3 copy-done.1
  43.9 4.5 %all-to-all-start.2 = ((bf16[16,4,2,16,1024]{4,3,2,1,0:T(8,128)(2,1)}), bf16[16,4,2,16,1024]{4,3,2,1,0:T(8,128)(2,1)}, u32[]{:S(2)}, u32[]{:S(2)}) async-start(bf16[16,4,2,16,1024]{4,3,2,1,0:T(8,128)(2,1)} %shard_map.111), calls=%async_computation.2 | async-start | bytes 8388608 | tf_op jit(solution)/shard_map/all_to_all | solution.py:174
  48.4 8.2 %shard_map.109 = bf16[16,2,2,16,1024]{4,3,2,1,0:T(8,128)(2,1)} custom-call(bf16[8,32,16,1024]{3,2,1,0:T(8,128)(2,1)} %map_ref.9, bf16[32,16,1024]{2,1,0:T(8,128)(2,1)} %obj_ref.5, bf16[1024,1024]{1,0:T(8,128)(2,1)} %constant.26.clone.fx_ref, bf16[512,512]{1,0:T(8,128)(2,1)} %constant.28.clone.kc_ref, bf16[512,512]{1,0:T(8,128)(2,1)} %constant.29.clone.ks_ref), custom_call_target="tpu_custom_call" | custom-call | tf_op jit(solution)/shard_map/pallas_call | solution.py:158
  56.7 42.1 %all-to-all-done.2.in_ref = bf16[16,4,2,16,1024]{4,3,2,1,0:T(8,128)(2,1)} async-done(((bf16[16,4,2,16,1024]{4,3,2,1,0:T(8,128)(2,1)}), bf16[16,4,2,16,1024]{4,3,2,1,0:T(8,128)(2,1)}, u32[]{:S(2)}, u32[]{:S(2)}) %all-to-all-start.2) | async-done | bytes 4194336 | tf_op jit(solution)/shard_map/all_to_all | solution.py:174
  98.8 3.7 %all-to-all-start = ((bf16[16,2,2,16,1024]{4,3,2,1,0:T(8,128)(2,1)}), bf16[16,2,2,16,1024]{4,3,2,1,0:T(8,128)(2,1)S(1)}, u32[]{:S(2)}, u32[]{:S(2)}) async-start(bf16[16,2,2,16,1024]{4,3,2,1,0:T(8,128)(2,1)} %shard_map.109), calls=%async_computation | async-start | bytes 4194304 | tf_op jit(solution)/shard_map/all_to_all | solution.py:174
  102.6 0.9 copy.14.mask_ref
  103.4 6.0 %shard_map.113.refs_0_ = bf16[16,6,2,16,1024]{4,3,2,1,0:T(8,128)(2,1)} custom-call(bf16[16,2,2,16,1024]{4,3,2,1,0:T(8,128)(2,1)} %copy-done.1, s32[2,256,4]{2,1,0:T(8,128)} %copy.14.mask_ref, bf16[512,512]{1,0:T(8,128)(2,1)} %constant.31.clone.wf_ref, bf16[512,512]{1,0:T(8,128)(2,1)} %constant.32.clone.wi_ref), custom_call_target="tpu_custom_call" | custom-call | tf_op jit(solution)/shard_map/pallas_call | solution.py:194
  109.4 10.2 %shard_map.114 = bf16[16,6,2,16,1024]{4,3,2,1,0:T(8,128)(2,1)} custom-call(bf16[16,4,2,16,1024]{4,3,2,1,0:T(8,128)(2,1)} %all-to-all-done.2.in_ref, s32[2,256,4]{2,1,0:T(8,128)} %copy.14.mask_ref, bf16[512,512]{1,0:T(8,128)(2,1)} %constant.31.clone.wf_ref, bf16[512,512]{1,0:T(8,128)(2,1)} %constant.32.clone.wi_ref, ...), custom_call_target="tpu_custom_call", output_to_operand_aliasing={{}: (4, {})} | custom-call | tf_op jit(solution)/shard_map/pallas_call | solution.py:194
  119.6 10.8 %all-to-all-done.in_ref = bf16[16,2,2,16,1024]{4,3,2,1,0:T(8,128)(2,1)S(1)} async-done(((bf16[16,2,2,16,1024]{4,3,2,1,0:T(8,128)(2,1)}), bf16[16,2,2,16,1024]{4,3,2,1,0:T(8,128)(2,1)S(1)}, u32[]{:S(2)}, u32[]{:S(2)}) %all-to-all-start) | async-done | bytes 2097184 | tf_op jit(solution)/shard_map/all_to_all | solution.py:174
  130.4 1.3 copy-done.2
  131.7 4.6 %all-to-all-start.4 = ((bf16[16,6,2,16,1024]{4,3,2,1,0:T(8,128)(2,1)}), bf16[16,6,2,16,1024]{4,3,2,1,0:T(8,128)(2,1)}, u32[]{:S(2)}, u32[]{:S(2)}) async-start(bf16[16,6,2,16,1024]{4,3,2,1,0:T(8,128)(2,1)} %shard_map.114), calls=%async_computation.4 | async-start | bytes 12582912 | tf_op jit(solution)/shard_map/all_to_all | solution.py:210
  136.3 6.0 %shard_map.110 = bf16[16,2,2,16,1024]{4,3,2,1,0:T(8,128)(2,1)} custom-call(bf16[16,2,2,16,1024]{4,3,2,1,0:T(8,128)(2,1)} %copy-done.2, s32[2,256,4]{2,1,0:T(8,128)} %copy.14.mask_ref, bf16[512,512]{1,0:T(8,128)(2,1)} %constant.31.clone.wf_ref, bf16[512,512]{1,0:T(8,128)(2,1)} %constant.32.clone.wi_ref), custom_call_target="tpu_custom_call" | custom-call | tf_op jit(solution)/shard_map/pallas_call | solution.py:194
  142.3 66.9 %all-to-all-done.4.in_ref = bf16[16,6,2,16,1024]{4,3,2,1,0:T(8,128)(2,1)} async-done(((bf16[16,6,2,16,1024]{4,3,2,1,0:T(8,128)(2,1)}), bf16[16,6,2,16,1024]{4,3,2,1,0:T(8,128)(2,1)}, u32[]{:S(2)}, u32[]{:S(2)}) %all-to-all-start.4) | async-done | bytes 6291488 | tf_op jit(solution)/shard_map/all_to_all | solution.py:210
  209.2 3.9 %all-to-all-start.1 = ((bf16[16,2,2,16,1024]{4,3,2,1,0:T(8,128)(2,1)}), bf16[16,2,2,16,1024]{4,3,2,1,0:T(8,128)(2,1)S(1)}, u32[]{:S(2)}, u32[]{:S(2)}) async-start(bf16[16,2,2,16,1024]{4,3,2,1,0:T(8,128)(2,1)} %shard_map.110), calls=%async_computation.1 | async-start | bytes 4194304 | tf_op jit(solution)/shard_map/all_to_all | solution.py:210
  213.1 20.4 %shard_map.115.refs_0_ = f32[32,16,1024]{2,1,0:T(8,128)} custom-call(bf16[16,6,2,16,1024]{4,3,2,1,0:T(8,128)(2,1)} %all-to-all-done.4.in_ref, bf16[8,32,16,1024]{3,2,1,0:T(8,128)(2,1)} %map_ref.9, bf16[512,512]{1,0:T(8,128)(2,1)} %constant.28.clone.kc_ref, bf16[512,512]{1,0:T(8,128)(2,1)} %constant.30.clone.ks_ref, bf16[1024,1024]{1,0:T(8,128)(2,1)} %constant.27.clone.fx_ref), custom_call_target="tpu_custom_call" | custom-call | tf_op jit(solution)/shard_map/pallas_call | solution.py:223
  233.5 7.3 %all-to-all-done.1.in_ref = bf16[16,2,2,16,1024]{4,3,2,1,0:T(8,128)(2,1)S(1)} async-done(((bf16[16,2,2,16,1024]{4,3,2,1,0:T(8,128)(2,1)}), bf16[16,2,2,16,1024]{4,3,2,1,0:T(8,128)(2,1)S(1)}, u32[]{:S(2)}, u32[]{:S(2)}) %all-to-all-start.1) | async-done | bytes 2097184 | tf_op jit(solution)/shard_map/all_to_all | solution.py:210
  240.8 1.3 copy-done.3
  242.1 9.8 %shard_map.116 = bf16[32,16,1024]{2,1,0:T(8,128)(2,1)} custom-call(bf16[16,2,2,16,1024]{4,3,2,1,0:T(8,128)(2,1)} %copy-done.3, bf16[8,32,16,1024]{3,2,1,0:T(8,128)(2,1)} %map_ref.9, bf16[512,512]{1,0:T(8,128)(2,1)} %constant.28.clone.kc_ref, bf16[512,512]{1,0:T(8,128)(2,1)} %constant.30.clone.ks_ref, bf16[1024,1024]{1,0:T(8,128)(2,1)} %constant.27.clone.fx_ref, ...), custom_call_target="tpu_custom_call" | custom-call | tf_op jit(solution)/shard_map/pallas_call | solution.py:223
  251.9 23.6 %all_to_all.30 = bf16[8,4,16,1024]{3,2,1,0:T(8,128)(2,1)S(1)} all-to-all(bf16[8,4,16,1024]{3,2,1,0:T(8,128)(2,1)} %bitcast.1), channel_id=1, replica_groups=mesh['coil'=8,'pencil'=16] {'coil'}, dimensions={0} | all-to-all | bytes 2097152 | tf_op jit(solution)/shard_map/all_to_all | solution.py:238
  275.6 0.9 convert_reduce_fusion
  (6 shorter events, 0.0 us)
Async XLA Ops:
  0.0 102.5 %copy-start = (s32[32,256,4]{1,2,0:T(4,128)S(1)}, s32[32,256,4]{1,2,0:T(4,128)}, u32[]{:S(2)}) copy-start(s32[32,256,4]{1,2,0:T(4,128)} %param.13) | copy-start | bytes 393220
  8.2 34.3 %all-to-all-start.3 = ((bf16[16,2,2,16,1024]{4,3,2,1,0:T(8,128)(2,1)}), bf16[16,2,2,16,1024]{4,3,2,1,0:T(8,128)(2,1)S(1)}, u32[]{:S(2)}, u32[]{:S(2)}) async-start(bf16[16,2,2,16,1024]{4,3,2,1,0:T(8,128)(2,1)} %shard_map.112), calls=%async_computation.3 | async-start | bytes 4194304 | tf_op jit(solution)/shard_map/all_to_all | solution.py:174
  42.6 1.3 copy-start.1
  43.9 54.9 %all-to-all-start.2 = ((bf16[16,4,2,16,1024]{4,3,2,1,0:T(8,128)(2,1)}), bf16[16,4,2,16,1024]{4,3,2,1,0:T(8,128)(2,1)}, u32[]{:S(2)}, u32[]{:S(2)}) async-start(bf16[16,4,2,16,1024]{4,3,2,1,0:T(8,128)(2,1)} %shard_map.111), calls=%async_computation.2 | async-start | bytes 8388608 | tf_op jit(solution)/shard_map/all_to_all | solution.py:174
  98.8 31.6 %all-to-all-start = ((bf16[16,2,2,16,1024]{4,3,2,1,0:T(8,128)(2,1)}), bf16[16,2,2,16,1024]{4,3,2,1,0:T(8,128)(2,1)S(1)}, u32[]{:S(2)}, u32[]{:S(2)}) async-start(bf16[16,2,2,16,1024]{4,3,2,1,0:T(8,128)(2,1)} %shard_map.109), calls=%async_computation | async-start | bytes 4194304 | tf_op jit(solution)/shard_map/all_to_all | solution.py:174
  130.4 1.3 copy-start.2
  131.7 77.5 %all-to-all-start.4 = ((bf16[16,6,2,16,1024]{4,3,2,1,0:T(8,128)(2,1)}), bf16[16,6,2,16,1024]{4,3,2,1,0:T(8,128)(2,1)}, u32[]{:S(2)}, u32[]{:S(2)}) async-start(bf16[16,6,2,16,1024]{4,3,2,1,0:T(8,128)(2,1)} %shard_map.114), calls=%async_computation.4 | async-start | bytes 12582912 | tf_op jit(solution)/shard_map/all_to_all | solution.py:210
  209.2 31.6 %all-to-all-start.1 = ((bf16[16,2,2,16,1024]{4,3,2,1,0:T(8,128)(2,1)}), bf16[16,2,2,16,1024]{4,3,2,1,0:T(8,128)(2,1)S(1)}, u32[]{:S(2)}, u32[]{:S(2)}) async-start(bf16[16,2,2,16,1024]{4,3,2,1,0:T(8,128)(2,1)} %shard_map.110), calls=%async_computation.1 | async-start | bytes 4194304 | tf_op jit(solution)/shard_map/all_to_all | solution.py:210
  240.8 1.3 copy-start.3

commit v7 on v5

--- a/solution.py
+++ b/solution.py
@@ -55,7 +55,7 @@
 PARAMS = pltpu.CompilerParams(vmem_limit_bytes=60 * 1024 * 1024)
 
 
-def forward_kernel(map_ref, obj_ref, fx_ref, kc_ref, ks_ref, out_ref):
+def forward_kernel(map_ref, obj_ref, kc_ref, ks_ref, out_ref):
     depth, rows, width = map_ref.shape
     half = width // 2
     maps = map_ref[...].reshape(depth * rows, width).astype(jnp.float32)
@@ -64,18 +64,17 @@
     o_re, o_im = obj[:, :half], obj[:, half:]
     image = jnp.concatenate([m_re * o_re - m_im * o_im, m_re * o_im + m_im * o_re], axis=1)
     image = image.astype(jnp.bfloat16)
-    along_x = dot32(image, fx_ref[...]).astype(jnp.bfloat16)
-    direct = dot32(kc_ref[...], along_x)
-    crossed = dot32(ks_ref[...], along_x)
+    direct = dot32(kc_ref[...], image)
+    crossed = dot32(ks_ref[...], image)
     along_z = turn_add(direct, crossed, half).astype(jnp.bfloat16)
     out_ref[...] = along_z.reshape(out_ref.shape)
 
 
-def line_kernel(in_ref, mask_ref, wf_ref, wi_ref, out_ref):
+def line_kernel(in_ref, mask_ref, fx_ref, fxi_ref, wf_ref, wi_ref, out_ref):
     groups, rows, width = in_ref.shape
     half = width // 2
     lines = groups * rows
-    volume = in_ref[...].reshape(lines, width)
+    volume = dot32(in_ref[...].reshape(lines, width), fx_ref[...]).astype(jnp.bfloat16)
     stacked = jnp.concatenate([volume[:, :half], volume[:, half:]], axis=0)
     spectrum = dot32(wf_ref[...], stacked).astype(jnp.bfloat16)
     flags = mask_ref[...]
@@ -88,17 +87,17 @@
     sampled = jnp.where(keep, spectrum, jnp.zeros_like(spectrum))
     back = dot32(wi_ref[...], sampled).astype(jnp.bfloat16)
     result = jnp.concatenate([back[:lines], back[lines:]], axis=1)
+    result = dot32(result, fxi_ref[...]).astype(jnp.bfloat16)
     out_ref[...] = result.reshape(out_ref.shape)
 
 
-def backward_kernel(first, last, in_ref, map_ref, kc_ref, ks_ref, fx_ref, *refs):
+def backward_kernel(first, last, in_ref, map_ref, kc_ref, ks_ref, *refs):
     depth, rows, width = map_ref.shape
     half = width // 2
     volume = in_ref[...].reshape(depth * rows, width)
     direct = dot32(kc_ref[...], volume)
     crossed = dot32(ks_ref[...], volume)
-    back_z = turn_add(direct, crossed, half).astype(jnp.bfloat16)
-    back_x = dot32(back_z, fx_ref[...]).astype(jnp.bfloat16).astype(jnp.float32)
+    back_x = turn_add(direct, crossed, half).astype(jnp.bfloat16).astype(jnp.float32)
     maps = map_ref[...].reshape(depth * rows, width).astype(jnp.float32)
     m_re, m_im = maps[:, :half], maps[:, half:]
     b_re, b_im = back_x[:, :half], back_x[:, half:]
@@ -142,7 +141,7 @@
     wi = block_table(lines, 1.0)
     mask = lax.dynamic_slice_in_dim(sample_mask, position * depth, depth, 0)
 
-    tail = coils // 4
+    tail = (3 * coils) // 8
     sizes = [coils - tail, tail] if tail > 0 else [coils]
     const2 = lambda c: (0, 0)
     const3 = lambda c: (0, 0, 0)
@@ -156,7 +155,6 @@
             in_specs=[
                 map_spec,
                 pl.BlockSpec((slices, rows, width), const3),
-                pl.BlockSpec((width, width), const2),
                 pl.BlockSpec((slices * rows, slices * rows), const2),
                 pl.BlockSpec((slices * rows, slices * rows), const2),
             ],
@@ -165,7 +163,7 @@
             ),
             out_shape=jax.ShapeDtypeStruct((pencils, per, depth, rows, width), jnp.bfloat16),
             compiler_params=PARAMS,
-        )(coil_maps, object_image, forward_x, kc_f, ks_f)
+        )(coil_maps, object_image, kc_f, ks_f)
         gathered = lax.all_to_all(split, "pencil", 0, 0, tiled=True)
         lined = pl.pallas_call(
             line_kernel,
@@ -173,6 +171,8 @@
             in_specs=[
                 pl.BlockSpec((pencils, None, None, rows, width), lambda c, k: (0, c, k, 0, 0)),
                 pl.BlockSpec((None, lines, sample_mask.shape[2]), lambda c, k: (k, 0, 0)),
+                pl.BlockSpec((width, width), lambda c, k: (0, 0)),
+                pl.BlockSpec((width, width), lambda c, k: (0, 0)),
                 pl.BlockSpec((2 * lines, 2 * lines), lambda c, k: (0, 0)),
                 pl.BlockSpec((2 * lines, 2 * lines), lambda c, k: (0, 0)),
             ],
@@ -181,16 +181,15 @@
             ),
             out_shape=jax.ShapeDtypeStruct((pencils, per, depth, rows, width), jnp.bfloat16),
             compiler_params=PARAMS,
-        )(gathered, mask, wf, wi)
+        )(gathered, mask, forward_x, inverse_x, wf, wi)
         returned = lax.all_to_all(lined, "pencil", 0, 0, tiled=True)
         first, last = start == 0, start + per == coils
-        operands = [returned, coil_maps, kc_i, ks_i, inverse_x]
+        operands = [returned, coil_maps, kc_i, ks_i]
         in_specs = [
             pl.BlockSpec((pencils, None, depth, rows, width), lambda c: (0, c, 0, 0, 0)),
             map_spec,
             pl.BlockSpec((slices * rows, slices * rows), const2),
             pl.BlockSpec((slices * rows, slices * rows), const2),
-            pl.BlockSpec((width, width), const2),
         ]
         if not first:
             operands.append(acc)

time: 276 us -> 268 us (0.971)
  waiting for transfers between devices: 151 us -> 143 us
    pallas_call x2, Pallas kernels: 20.6 us -> 37.8 us  [on_device(): pl.pallas_call(line_kernel, grid=(per, depth), in_specs=[pl.BlockSpec((pe...]
    pallas_call x2, Pallas kernels: 30.2 us -> 20.6 us  [on_device(): pl.pallas_call(functools.partial(backward_kernel, first, last), grid=(per...]
    pallas_call x2, Pallas kernels: 26.1 us -> 18.1 us  [on_device(): pl.pallas_call(forward_kernel, grid=(per,), in_specs=[map_spec, pl.BlockS...]
    all_to_all x2, waiting for transfers between devices: 77.1 us -> 69.6 us  [on_device(): gathered = lax.all_to_all(split, 'pencil', 0, 0, tiled=True)]
  transfers between devices with their start and end apart: 4 -> 4, of which waited for: 4 -> 4; matrix products, arithmetic and copies ran while one was open for 0% -> 0% of each run, Pallas kernels for 18% -> 21%
where the time goes in v7:
time: 268 us; the launch traced here: 267 us
  waiting for transfers between devices  143 us (53%)
  Pallas kernels  76.5 us (29%)
  blocking collectives  23.6 us (9%)
  starting transfers between devices  18.6 us (7%)
  local copies, waits for them, and re-layouts  4.13 us (2%)
    all_to_all x2, waiting for transfers between devices, on_device(): returned = lax.all_to_all(lined, 'pencil', 0, 0, tiled=True)  73.9 us
    all_to_all x2, waiting for transfers between devices, on_device(): gathered = lax.all_to_all(split, 'pencil', 0, 0, tiled=True)  69.6 us
    pallas_call x2, Pallas kernels, on_device(): pl.pallas_call(line_kernel, grid=(per, depth), in_specs=[pl.BlockSpec((pe...  37.8 us
    all_to_all x1, blocking collectives, on_device(): parts = lax.all_to_all(parts, 'coil', 0, 0, tiled=True)  23.6 us
    pallas_call x2, Pallas kernels, on_device(): pl.pallas_call(functools.partial(backward_kernel, first, last), grid=(per...  20.6 us
    pallas_call x2, Pallas kernels, on_device(): pl.pallas_call(forward_kernel, grid=(per,), in_specs=[map_spec, pl.BlockS...  18.1 us
    all_to_all x2, starting transfers between devices, on_device(): gathered = lax.all_to_all(split, 'pencil', 0, 0, tiled=True)  10.2 us
    all_to_all x2, starting transfers between devices, on_device(): returned = lax.all_to_all(lined, 'pencil', 0, 0, tiled=True)  8.34 us
  transfers between devices with their start and end apart: 4, of which 4 were waited for; matrix products, arithmetic and copies ran while one was open for 0% of the time, Pallas kernels for 21%

profile of v7, /device:TPU:0, one launch (start us, length us, event | category | flops | bytes accessed | tf_op | source)
XLA Modules:
  0.0 267.2 jit_solution(980830624176835443)
XLA Ops:
  0.0 0.0 copy-start
  0.0 10.6 %shard_map.111 = bf16[16,5,2,16,1024]{4,3,2,1,0:T(8,128)(2,1)} custom-call(bf16[8,32,16,1024]{3,2,1,0:T(8,128)(2,1)} %map_ref.7, bf16[32,16,1024]{2,1,0:T(8,128)(2,1)} %obj_ref.3, bf16[512,512]{1,0:T(8,128)(2,1)} %constant.28.clone.kc_ref, bf16[512,512]{1,0:T(8,128)(2,1)} %constant.29.clone.ks_ref), custom_call_target="tpu_custom_call" | custom-call | tf_op jit(solution)/shard_map/pallas_call | solution.py:152
  10.6 6.5 %all-to-all-start.2 = ((bf16[16,5,2,16,1024]{4,3,2,1,0:T(8,128)(2,1)}), bf16[16,5,2,16,1024]{4,3,2,1,0:T(8,128)(2,1)}, u32[]{:S(2)}, u32[]{:S(2)}) async-start(bf16[16,5,2,16,1024]{4,3,2,1,0:T(8,128)(2,1)} %shard_map.111), calls=%async_computation.2 | async-start | bytes 10485760 | tf_op jit(solution)/shard_map/all_to_all | solution.py:167
  17.0 7.5 %shard_map.109 = bf16[16,3,2,16,1024]{4,3,2,1,0:T(8,128)(2,1)} custom-call(bf16[8,32,16,1024]{3,2,1,0:T(8,128)(2,1)} %map_ref.7, bf16[32,16,1024]{2,1,0:T(8,128)(2,1)} %obj_ref.3, bf16[512,512]{1,0:T(8,128)(2,1)} %constant.28.clone.kc_ref, bf16[512,512]{1,0:T(8,128)(2,1)} %constant.29.clone.ks_ref), custom_call_target="tpu_custom_call" | custom-call | tf_op jit(solution)/shard_map/pallas_call | solution.py:152
  24.6 54.1 %all-to-all-done.2.in_ref = bf16[16,5,2,16,1024]{4,3,2,1,0:T(8,128)(2,1)} async-done(((bf16[16,5,2,16,1024]{4,3,2,1,0:T(8,128)(2,1)}), bf16[16,5,2,16,1024]{4,3,2,1,0:T(8,128)(2,1)}, u32[]{:S(2)}, u32[]{:S(2)}) %all-to-all-start.2) | async-done | bytes 5242912 | tf_op jit(solution)/shard_map/all_to_all | solution.py:167
  78.7 3.7 %all-to-all-start = ((bf16[16,3,2,16,1024]{4,3,2,1,0:T(8,128)(2,1)}), bf16[16,3,2,16,1024]{4,3,2,1,0:T(8,128)(2,1)S(1)}, u32[]{:S(2)}, u32[]{:S(2)}) async-start(bf16[16,3,2,16,1024]{4,3,2,1,0:T(8,128)(2,1)} %shard_map.109), calls=%async_computation | async-start | bytes 6291456 | tf_op jit(solution)/shard_map/all_to_all | solution.py:167
  82.4 0.0 copy-done
  82.5 0.9 copy.13.mask_ref
  83.3 22.7 %shard_map.112 = bf16[16,5,2,16,1024]{4,3,2,1,0:T(8,128)(2,1)} custom-call(bf16[16,5,2,16,1024]{4,3,2,1,0:T(8,128)(2,1)} %all-to-all-done.2.in_ref, s32[2,256,4]{2,1,0:T(8,128)} %copy.13.mask_ref, bf16[1024,1024]{1,0:T(8,128)(2,1)} %constant.26.clone.fx_ref, bf16[1024,1024]{1,0:T(8,128)(2,1)} %constant.27.clone.fxi_ref, ...), custom_call_target="tpu_custom_call" | custom-call | tf_op jit(solution)/shard_map/pallas_call | solution.py:168
  106.1 15.5 %all-to-all-done.in_ref = bf16[16,3,2,16,1024]{4,3,2,1,0:T(8,128)(2,1)S(1)} async-done(((bf16[16,3,2,16,1024]{4,3,2,1,0:T(8,128)(2,1)}), bf16[16,3,2,16,1024]{4,3,2,1,0:T(8,128)(2,1)S(1)}, u32[]{:S(2)}, u32[]{:S(2)}) %all-to-all-start) | async-done | bytes 3145760 | tf_op jit(solution)/shard_map/all_to_all | solution.py:167
  121.5 0.0 copy-start.1
  121.5 1.6 copy-done.1
  123.2 4.6 %all-to-all-start.3 = ((bf16[16,5,2,16,1024]{4,3,2,1,0:T(8,128)(2,1)}), bf16[16,5,2,16,1024]{4,3,2,1,0:T(8,128)(2,1)}, u32[]{:S(2)}, u32[]{:S(2)}) async-start(bf16[16,5,2,16,1024]{4,3,2,1,0:T(8,128)(2,1)} %shard_map.112), calls=%async_computation.3 | async-start | bytes 10485760 | tf_op jit(solution)/shard_map/all_to_all | solution.py:185
  127.8 15.0 %shard_map.110 = bf16[16,3,2,16,1024]{4,3,2,1,0:T(8,128)(2,1)} custom-call(bf16[16,3,2,16,1024]{4,3,2,1,0:T(8,128)(2,1)} %copy-done.1, s32[2,256,4]{2,1,0:T(8,128)} %copy.13.mask_ref, bf16[1024,1024]{1,0:T(8,128)(2,1)} %constant.26.clone.fx_ref, bf16[1024,1024]{1,0:T(8,128)(2,1)} %constant.27.clone.fxi_ref, bf16[512,512]{1,0:T(8,128)(2,1)} %constant.31.clone.wf_ref, ...), custom_call_target="tpu_custom_call" | custom-call | tf_op jit(solution)/shard_map/pallas_call | solution.py:168
  142.8 46.6 %all-to-all-done.3.in_ref = bf16[16,5,2,16,1024]{4,3,2,1,0:T(8,128)(2,1)} async-done(((bf16[16,5,2,16,1024]{4,3,2,1,0:T(8,128)(2,1)}), bf16[16,5,2,16,1024]{4,3,2,1,0:T(8,128)(2,1)}, u32[]{:S(2)}, u32[]{:S(2)}) %all-to-all-start.3) | async-done | bytes 5242912 | tf_op jit(solution)/shard_map/all_to_all | solution.py:185
  189.4 3.7 %all-to-all-start.1 = ((bf16[16,3,2,16,1024]{4,3,2,1,0:T(8,128)(2,1)}), bf16[16,3,2,16,1024]{4,3,2,1,0:T(8,128)(2,1)S(1)}, u32[]{:S(2)}, u32[]{:S(2)}) async-start(bf16[16,3,2,16,1024]{4,3,2,1,0:T(8,128)(2,1)} %shard_map.110), calls=%async_computation.1 | async-start | bytes 6291456 | tf_op jit(solution)/shard_map/all_to_all | solution.py:185
  193.1 11.8 %shard_map.113.refs_0_ = f32[32,16,1024]{2,1,0:T(8,128)} custom-call(bf16[16,5,2,16,1024]{4,3,2,1,0:T(8,128)(2,1)} %all-to-all-done.3.in_ref, bf16[8,32,16,1024]{3,2,1,0:T(8,128)(2,1)} %map_ref.7, bf16[512,512]{1,0:T(8,128)(2,1)} %constant.28.clone.kc_ref, bf16[512,512]{1,0:T(8,128)(2,1)} %constant.30.clone.ks_ref), custom_call_target="tpu_custom_call" | custom-call | tf_op jit(solution)/shard_map/pallas_call | solution.py:197
  204.9 27.3 %all-to-all-done.1.in_ref = bf16[16,3,2,16,1024]{4,3,2,1,0:T(8,128)(2,1)S(1)} async-done(((bf16[16,3,2,16,1024]{4,3,2,1,0:T(8,128)(2,1)}), bf16[16,3,2,16,1024]{4,3,2,1,0:T(8,128)(2,1)S(1)}, u32[]{:S(2)}, u32[]{:S(2)}) %all-to-all-start.1) | async-done | bytes 3145760 | tf_op jit(solution)/shard_map/all_to_all | solution.py:185
  232.2 0.0 copy-start.2
  232.2 1.6 copy-done.2
  233.8 8.9 %shard_map.114 = bf16[32,16,1024]{2,1,0:T(8,128)(2,1)} custom-call(bf16[16,3,2,16,1024]{4,3,2,1,0:T(8,128)(2,1)} %copy-done.2, bf16[8,32,16,1024]{3,2,1,0:T(8,128)(2,1)} %map_ref.7, bf16[512,512]{1,0:T(8,128)(2,1)} %constant.28.clone.kc_ref, bf16[512,512]{1,0:T(8,128)(2,1)} %constant.30.clone.ks_ref, f32[32,16,1024]{2,1,0:T(8,128)} %shard_map.113.refs_0_), custom_call_target="tpu_custom_call" | custom-call | tf_op jit(solution)/shard_map/pallas_call | solution.py:197
  242.7 23.6 %all_to_all.25 = bf16[8,4,16,1024]{3,2,1,0:T(8,128)(2,1)S(1)} all-to-all(bf16[8,4,16,1024]{3,2,1,0:T(8,128)(2,1)} %bitcast.1), channel_id=1, replica_groups=mesh['coil'=8,'pencil'=16] {'coil'}, dimensions={0} | all-to-all | bytes 2097152 | tf_op jit(solution)/shard_map/all_to_all | solution.py:213
  266.4 0.9 convert_reduce_fusion
  (1 shorter events, 0.0 us)
Async XLA Ops:
  0.0 82.4 %copy-start = (s32[32,256,4]{1,2,0:T(4,128)S(1)}, s32[32,256,4]{1,2,0:T(4,128)}, u32[]{:S(2)}) copy-start(s32[32,256,4]{1,2,0:T(4,128)} %param.13) | copy-start | bytes 393220
  10.6 68.1 %all-to-all-start.2 = ((bf16[16,5,2,16,1024]{4,3,2,1,0:T(8,128)(2,1)}), bf16[16,5,2,16,1024]{4,3,2,1,0:T(8,128)(2,1)}, u32[]{:S(2)}, u32[]{:S(2)}) async-start(bf16[16,5,2,16,1024]{4,3,2,1,0:T(8,128)(2,1)} %shard_map.111), calls=%async_computation.2 | async-start | bytes 10485760 | tf_op jit(solution)/shard_map/all_to_all | solution.py:167
  78.7 42.8 %all-to-all-start = ((bf16[16,3,2,16,1024]{4,3,2,1,0:T(8,128)(2,1)}), bf16[16,3,2,16,1024]{4,3,2,1,0:T(8,128)(2,1)S(1)}, u32[]{:S(2)}, u32[]{:S(2)}) async-start(bf16[16,3,2,16,1024]{4,3,2,1,0:T(8,128)(2,1)} %shard_map.109), calls=%async_computation | async-start | bytes 6291456 | tf_op jit(solution)/shard_map/all_to_all | solution.py:167
  121.5 1.6 copy-start.1
  123.2 66.2 %all-to-all-start.3 = ((bf16[16,5,2,16,1024]{4,3,2,1,0:T(8,128)(2,1)}), bf16[16,5,2,16,1024]{4,3,2,1,0:T(8,128)(2,1)}, u32[]{:S(2)}, u32[]{:S(2)}) async-start(bf16[16,5,2,16,1024]{4,3,2,1,0:T(8,128)(2,1)} %shard_map.112), calls=%async_computation.3 | async-start | bytes 10485760 | tf_op jit(solution)/shard_map/all_to_all | solution.py:185
  189.4 42.8 %all-to-all-start.1 = ((bf16[16,3,2,16,1024]{4,3,2,1,0:T(8,128)(2,1)}), bf16[16,3,2,16,1024]{4,3,2,1,0:T(8,128)(2,1)S(1)}, u32[]{:S(2)}, u32[]{:S(2)}) async-start(bf16[16,3,2,16,1024]{4,3,2,1,0:T(8,128)(2,1)} %shard_map.110), calls=%async_computation.1 | async-start | bytes 6291456 | tf_op jit(solution)/shard_map/all_to_all | solution.py:185
  232.2 1.6 copy-start.2

commit v8 on v7

--- a/solution.py
+++ b/solution.py
@@ -141,7 +141,7 @@
     wi = block_table(lines, 1.0)
     mask = lax.dynamic_slice_in_dim(sample_mask, position * depth, depth, 0)
 
-    tail = (3 * coils) // 8
+    tail = coils // 2
     sizes = [coils - tail, tail] if tail > 0 else [coils]
     const2 = lambda c: (0, 0)
     const3 = lambda c: (0, 0, 0)

time: 268 us -> 266 us (level)
  local copies, waits for them, and re-layouts: 4.13 us -> 0.87 us
    unnamed x7 -> x3, local copies, waits for them, and re-layouts: 4.12 us -> 0.86 us
where the time goes in v8:
time: 266 us
  waiting for transfers between devices  144 us (54%)
  Pallas kernels  76.4 us (29%)
  blocking collectives  23.6 us (9%)
  starting transfers between devices  20.1 us (8%)
    all_to_all x2, waiting for transfers between devices, on_device(): gathered = lax.all_to_all(split, 'pencil', 0, 0, tiled=True)  72 us
    all_to_all x2, waiting for transfers between devices, on_device(): returned = lax.all_to_all(lined, 'pencil', 0, 0, tiled=True)  71.8 us
    pallas_call x2, Pallas kernels, on_device(): pl.pallas_call(line_kernel, grid=(per, depth), in_specs=[pl.BlockSpec((pe...  37.8 us
    all_to_all x1, blocking collectives, on_device(): parts = lax.all_to_all(parts, 'coil', 0, 0, tiled=True)  23.6 us
    pallas_call x2, Pallas kernels, on_device(): pl.pallas_call(functools.partial(backward_kernel, first, last), grid=(per...  20.6 us
    pallas_call x2, Pallas kernels, on_device(): pl.pallas_call(forward_kernel, grid=(per,), in_specs=[map_spec, pl.BlockS...  18 us
    all_to_all x2, starting transfers between devices, on_device(): gathered = lax.all_to_all(split, 'pencil', 0, 0, tiled=True)  11 us
    all_to_all x2, starting transfers between devices, on_device(): returned = lax.all_to_all(lined, 'pencil', 0, 0, tiled=True)  9.09 us
  transfers between devices with their start and end apart: 4, of which 4 were waited for; matrix products, arithmetic and copies ran while one was open for 0% of the time, Pallas kernels for 21%

profile of v8, /device:TPU:0, one launch (start us, length us, event | category | flops | bytes accessed | tf_op | source)
XLA Modules:
  0.0 265.8 jit_solution(3710956904614121567)
XLA Ops:
  0.0 0.0 copy-start
  0.0 9.0 %shard_map.111 = bf16[16,4,2,16,1024]{4,3,2,1,0:T(8,128)(2,1)} custom-call(bf16[8,32,16,1024]{3,2,1,0:T(8,128)(2,1)} %map_ref.7, bf16[32,16,1024]{2,1,0:T(8,128)(2,1)} %obj_ref.3, bf16[512,512]{1,0:T(8,128)(2,1)} %constant.28.clone.kc_ref, bf16[512,512]{1,0:T(8,128)(2,1)} %constant.29.clone.ks_ref), custom_call_target="tpu_custom_call" | custom-call | tf_op jit(solution)/shard_map/pallas_call | solution.py:152
  9.0 6.5 %all-to-all-start.2 = ((bf16[16,4,2,16,1024]{4,3,2,1,0:T(8,128)(2,1)}), bf16[16,4,2,16,1024]{4,3,2,1,0:T(8,128)(2,1)}, u32[]{:S(2)}, u32[]{:S(2)}) async-start(bf16[16,4,2,16,1024]{4,3,2,1,0:T(8,128)(2,1)} %shard_map.111), calls=%async_computation.2 | async-start | bytes 8388608 | tf_op jit(solution)/shard_map/all_to_all | solution.py:167
  15.5 9.0 %shard_map.109 = bf16[16,4,2,16,1024]{4,3,2,1,0:T(8,128)(2,1)} custom-call(bf16[8,32,16,1024]{3,2,1,0:T(8,128)(2,1)} %map_ref.7, bf16[32,16,1024]{2,1,0:T(8,128)(2,1)} %obj_ref.3, bf16[512,512]{1,0:T(8,128)(2,1)} %constant.28.clone.kc_ref, bf16[512,512]{1,0:T(8,128)(2,1)} %constant.29.clone.ks_ref), custom_call_target="tpu_custom_call" | custom-call | tf_op jit(solution)/shard_map/pallas_call | solution.py:152
  24.5 41.4 %all-to-all-done.2.in_ref = bf16[16,4,2,16,1024]{4,3,2,1,0:T(8,128)(2,1)} async-done(((bf16[16,4,2,16,1024]{4,3,2,1,0:T(8,128)(2,1)}), bf16[16,4,2,16,1024]{4,3,2,1,0:T(8,128)(2,1)}, u32[]{:S(2)}, u32[]{:S(2)}) %all-to-all-start.2) | async-done | bytes 4194336 | tf_op jit(solution)/shard_map/all_to_all | solution.py:167
  65.9 4.5 %all-to-all-start = ((bf16[16,4,2,16,1024]{4,3,2,1,0:T(8,128)(2,1)}), bf16[16,4,2,16,1024]{4,3,2,1,0:T(8,128)(2,1)}, u32[]{:S(2)}, u32[]{:S(2)}) async-start(bf16[16,4,2,16,1024]{4,3,2,1,0:T(8,128)(2,1)} %shard_map.109), calls=%async_computation | async-start | bytes 8388608 | tf_op jit(solution)/shard_map/all_to_all | solution.py:167
  70.5 0.0 copy-done
  70.5 0.9 copy.13.mask_ref
  71.4 18.9 %shard_map.112 = bf16[16,4,2,16,1024]{4,3,2,1,0:T(8,128)(2,1)} custom-call(bf16[16,4,2,16,1024]{4,3,2,1,0:T(8,128)(2,1)} %all-to-all-done.2.in_ref, s32[2,256,4]{2,1,0:T(8,128)} %copy.13.mask_ref, bf16[1024,1024]{1,0:T(8,128)(2,1)} %constant.26.clone.fx_ref, bf16[1024,1024]{1,0:T(8,128)(2,1)} %constant.27.clone.fxi_ref, ...), custom_call_target="tpu_custom_call" | custom-call | tf_op jit(solution)/shard_map/pallas_call | solution.py:168
  90.3 30.6 %all-to-all-done.in_ref = bf16[16,4,2,16,1024]{4,3,2,1,0:T(8,128)(2,1)} async-done(((bf16[16,4,2,16,1024]{4,3,2,1,0:T(8,128)(2,1)}), bf16[16,4,2,16,1024]{4,3,2,1,0:T(8,128)(2,1)}, u32[]{:S(2)}, u32[]{:S(2)}) %all-to-all-start) | async-done | bytes 4194336 | tf_op jit(solution)/shard_map/all_to_all | solution.py:167
  120.8 4.5 %all-to-all-start.3 = ((bf16[16,4,2,16,1024]{4,3,2,1,0:T(8,128)(2,1)}), bf16[16,4,2,16,1024]{4,3,2,1,0:T(8,128)(2,1)}, u32[]{:S(2)}, u32[]{:S(2)}) async-start(bf16[16,4,2,16,1024]{4,3,2,1,0:T(8,128)(2,1)} %shard_map.112), calls=%async_computation.3 | async-start | bytes 8388608 | tf_op jit(solution)/shard_map/all_to_all | solution.py:185
  125.4 18.9 %shard_map.110 = bf16[16,4,2,16,1024]{4,3,2,1,0:T(8,128)(2,1)} custom-call(bf16[16,4,2,16,1024]{4,3,2,1,0:T(8,128)(2,1)} %all-to-all-done.in_ref, s32[2,256,4]{2,1,0:T(8,128)} %copy.13.mask_ref, bf16[1024,1024]{1,0:T(8,128)(2,1)} %constant.26.clone.fx_ref, bf16[1024,1024]{1,0:T(8,128)(2,1)} %constant.27.clone.fxi_ref, ...), custom_call_target="tpu_custom_call" | custom-call | tf_op jit(solution)/shard_map/pallas_call | solution.py:168
  144.3 31.5 %all-to-all-done.3.in_ref = bf16[16,4,2,16,1024]{4,3,2,1,0:T(8,128)(2,1)} async-done(((bf16[16,4,2,16,1024]{4,3,2,1,0:T(8,128)(2,1)}), bf16[16,4,2,16,1024]{4,3,2,1,0:T(8,128)(2,1)}, u32[]{:S(2)}, u32[]{:S(2)}) %all-to-all-start.3) | async-done | bytes 4194336 | tf_op jit(solution)/shard_map/all_to_all | solution.py:185
  175.8 4.5 %all-to-all-start.1 = ((bf16[16,4,2,16,1024]{4,3,2,1,0:T(8,128)(2,1)}), bf16[16,4,2,16,1024]{4,3,2,1,0:T(8,128)(2,1)}, u32[]{:S(2)}, u32[]{:S(2)}) async-start(bf16[16,4,2,16,1024]{4,3,2,1,0:T(8,128)(2,1)} %shard_map.110), calls=%async_computation.1 | async-start | bytes 8388608 | tf_op jit(solution)/shard_map/all_to_all | solution.py:185
  180.3 10.0 %shard_map.113.refs_0_ = f32[32,16,1024]{2,1,0:T(8,128)} custom-call(bf16[16,4,2,16,1024]{4,3,2,1,0:T(8,128)(2,1)} %all-to-all-done.3.in_ref, bf16[8,32,16,1024]{3,2,1,0:T(8,128)(2,1)} %map_ref.7, bf16[512,512]{1,0:T(8,128)(2,1)} %constant.28.clone.kc_ref, bf16[512,512]{1,0:T(8,128)(2,1)} %constant.30.clone.ks_ref), custom_call_target="tpu_custom_call" | custom-call | tf_op jit(solution)/shard_map/pallas_call | solution.py:197
  190.3 40.3 %all-to-all-done.1.in_ref = bf16[16,4,2,16,1024]{4,3,2,1,0:T(8,128)(2,1)} async-done(((bf16[16,4,2,16,1024]{4,3,2,1,0:T(8,128)(2,1)}), bf16[16,4,2,16,1024]{4,3,2,1,0:T(8,128)(2,1)}, u32[]{:S(2)}, u32[]{:S(2)}) %all-to-all-start.1) | async-done | bytes 4194336 | tf_op jit(solution)/shard_map/all_to_all | solution.py:185
  230.7 10.6 %shard_map.114 = bf16[32,16,1024]{2,1,0:T(8,128)(2,1)} custom-call(bf16[16,4,2,16,1024]{4,3,2,1,0:T(8,128)(2,1)} %all-to-all-done.1.in_ref, bf16[8,32,16,1024]{3,2,1,0:T(8,128)(2,1)} %map_ref.7, bf16[512,512]{1,0:T(8,128)(2,1)} %constant.28.clone.kc_ref, bf16[512,512]{1,0:T(8,128)(2,1)} %constant.30.clone.ks_ref, f32[32,16,1024]{2,1,0:T(8,128)} %shard_map.113.refs_0_), custom_call_target="tpu_custom_call" | custom-call | tf_op jit(solution)/shard_map/pallas_call | solution.py:197
  241.3 23.6 %all_to_all.25 = bf16[8,4,16,1024]{3,2,1,0:T(8,128)(2,1)S(1)} all-to-all(bf16[8,4,16,1024]{3,2,1,0:T(8,128)(2,1)} %bitcast.1), channel_id=1, replica_groups=mesh['coil'=8,'pencil'=16] {'coil'}, dimensions={0} | all-to-all | bytes 2097152 | tf_op jit(solution)/shard_map/all_to_all | solution.py:213
  264.9 0.9 convert_reduce_fusion
  (1 shorter events, 0.0 us)
Async XLA Ops:
  0.0 70.5 %copy-start = (s32[32,256,4]{1,2,0:T(4,128)S(1)}, s32[32,256,4]{1,2,0:T(4,128)}, u32[]{:S(2)}) copy-start(s32[32,256,4]{1,2,0:T(4,128)} %param.13) | copy-start | bytes 393220
  9.0 56.9 %all-to-all-start.2 = ((bf16[16,4,2,16,1024]{4,3,2,1,0:T(8,128)(2,1)}), bf16[16,4,2,16,1024]{4,3,2,1,0:T(8,128)(2,1)}, u32[]{:S(2)}, u32[]{:S(2)}) async-start(bf16[16,4,2,16,1024]{4,3,2,1,0:T(8,128)(2,1)} %shard_map.111), calls=%async_computation.2 | async-start | bytes 8388608 | tf_op jit(solution)/shard_map/all_to_all | solution.py:167
  65.9 54.9 %all-to-all-start = ((bf16[16,4,2,16,1024]{4,3,2,1,0:T(8,128)(2,1)}), bf16[16,4,2,16,1024]{4,3,2,1,0:T(8,128)(2,1)}, u32[]{:S(2)}, u32[]{:S(2)}) async-start(bf16[16,4,2,16,1024]{4,3,2,1,0:T(8,128)(2,1)} %shard_map.109), calls=%async_computation | async-start | bytes 8388608 | tf_op jit(solution)/shard_map/all_to_all | solution.py:167
  120.8 54.9 %all-to-all-start.3 = ((bf16[16,4,2,16,1024]{4,3,2,1,0:T(8,128)(2,1)}), bf16[16,4,2,16,1024]{4,3,2,1,0:T(8,128)(2,1)}, u32[]{:S(2)}, u32[]{:S(2)}) async-start(bf16[16,4,2,16,1024]{4,3,2,1,0:T(8,128)(2,1)} %shard_map.112), calls=%async_computation.3 | async-start | bytes 8388608 | tf_op jit(solution)/shard_map/all_to_all | solution.py:185
  175.8 54.9 %all-to-all-start.1 = ((bf16[16,4,2,16,1024]{4,3,2,1,0:T(8,128)(2,1)}), bf16[16,4,2,16,1024]{4,3,2,1,0:T(8,128)(2,1)}, u32[]{:S(2)}, u32[]{:S(2)}) async-start(bf16[16,4,2,16,1024]{4,3,2,1,0:T(8,128)(2,1)} %shard_map.110), calls=%async_computation.1 | async-start | bytes 8388608 | tf_op jit(solution)/shard_map/all_to_all | solution.py:185

commit v9 on v8

--- a/solution.py
+++ b/solution.py
@@ -58,15 +58,21 @@
 def forward_kernel(map_ref, obj_ref, kc_ref, ks_ref, out_ref):
     depth, rows, width = map_ref.shape
     half = width // 2
-    maps = map_ref[...].reshape(depth * rows, width).astype(jnp.float32)
-    obj = obj_ref[...].reshape(depth * rows, width).astype(jnp.float32)
-    m_re, m_im = maps[:, :half], maps[:, half:]
-    o_re, o_im = obj[:, :half], obj[:, half:]
-    image = jnp.concatenate([m_re * o_re - m_im * o_im, m_re * o_im + m_im * o_re], axis=1)
-    image = image.astype(jnp.bfloat16)
-    direct = dot32(kc_ref[...], image)
-    crossed = dot32(ks_ref[...], image)
-    along_z = turn_add(direct, crossed, half).astype(jnp.bfloat16)
+    band = kc_ref.shape[0] // depth
+    maps = map_ref[...].astype(jnp.float32)
+    obj = obj_ref[...].astype(jnp.float32)
+    m_re, m_im = maps[..., :half], maps[..., half:]
+    o_re, o_im = obj[..., :half], obj[..., half:]
+    image = jnp.concatenate([m_re * o_re - m_im * o_im, m_re * o_im + m_im * o_re], axis=-1)
+    pieces = []
+    for h in range(rows // band):
+        part = image[:, h * band : (h + 1) * band, :].reshape(depth * band, width)
+        part = part.astype(jnp.bfloat16)
+        direct = dot32(kc_ref[...], part)
+        crossed = dot32(ks_ref[...], part)
+        along_z = turn_add(direct, crossed, half).astype(jnp.bfloat16).astype(jnp.float32)
+        pieces.append(along_z.reshape(depth, band, width))
+    along_z = jnp.concatenate(pieces, axis=1).astype(jnp.bfloat16)
     out_ref[...] = along_z.reshape(out_ref.shape)
 
 
@@ -94,15 +100,24 @@
 def backward_kernel(first, last, in_ref, map_ref, kc_ref, ks_ref, *refs):
     depth, rows, width = map_ref.shape
     half = width // 2
-    volume = in_ref[...].reshape(depth * rows, width)
-    direct = dot32(kc_ref[...], volume)
-    crossed = dot32(ks_ref[...], volume)
-    back_x = turn_add(direct, crossed, half).astype(jnp.bfloat16).astype(jnp.float32)
-    maps = map_ref[...].reshape(depth * rows, width).astype(jnp.float32)
-    m_re, m_im = maps[:, :half], maps[:, half:]
-    b_re, b_im = back_x[:, :half], back_x[:, half:]
-    product = jnp.concatenate([m_re * b_re + m_im * b_im, m_re * b_im - m_im * b_re], axis=1)
-    product = product.reshape(depth, rows, width)
+    band = kc_ref.shape[0] // depth
+    volume = in_ref[...].reshape(depth, rows, width).astype(jnp.float32)
+    maps = map_ref[...].astype(jnp.float32)
+    pieces = []
+    for h in range(rows // band):
+        part = volume[:, h * band : (h + 1) * band, :].reshape(depth * band, width)
+        part = part.astype(jnp.bfloat16)
+        direct = dot32(kc_ref[...], part)
+        crossed = dot32(ks_ref[...], part)
+        back_x = turn_add(direct, crossed, half).astype(jnp.bfloat16).astype(jnp.float32)
+        coil = maps[:, h * band : (h + 1) * band, :].reshape(depth * band, width)
+        m_re, m_im = coil[:, :half], coil[:, half:]
+        b_re, b_im = back_x[:, :half], back_x[:, half:]
+        piece = jnp.concatenate(
+            [m_re * b_re + m_im * b_im, m_re * b_im - m_im * b_re], axis=1
+        )
+        pieces.append(piece.reshape(depth, band, width))
+    product = jnp.concatenate(pieces, axis=1)
     refs = list(refs)
     acc_ref = None if first else refs.pop(0)
     out_ref = refs.pop(0)
@@ -135,8 +150,9 @@
 
     forward_x = readout_table(readout, -1.0)
     inverse_x = readout_table(readout, 1.0)
-    kc_f, ks_f = slice_tables(slices, -1.0, rows)
-    kc_i, ks_i = slice_tables(slices, 1.0, rows)
+    band = 8 if rows % 8 == 0 else rows
+    kc_f, ks_f = slice_tables(slices, -1.0, band)
+    kc_i, ks_i = slice_tables(slices, 1.0, band)
     wf = block_table(lines, -1.0)
     wi = block_table(lines, 1.0)
     mask = lax.dynamic_slice_in_dim(sample_mask, position * depth, depth, 0)
@@ -155,8 +171,8 @@
             in_specs=[
                 map_spec,
                 pl.BlockSpec((slices, rows, width), const3),
-                pl.BlockSpec((slices * rows, slices * rows), const2),
-                pl.BlockSpec((slices * rows, slices * rows), const2),
+                pl.BlockSpec((slices * band, slices * band), const2),
+                pl.BlockSpec((slices * band, slices * band), const2),
             ],
             out_specs=pl.BlockSpec(
                 (pencils, None, depth, rows, width), lambda c: (0, c, 0, 0, 0)
@@ -188,8 +204,8 @@
         in_specs = [
             pl.BlockSpec((pencils, None, depth, rows, width), lambda c: (0, c, 0, 0, 0)),
             map_spec,
-            pl.BlockSpec((slices * rows, slices * rows), const2),
-            pl.BlockSpec((slices * rows, slices * rows), const2),
+            pl.BlockSpec((slices * band, slices * band), const2),
+            pl.BlockSpec((slices * band, slices * band), const2),
         ]
         if not first:
             operands.append(acc)

time: 266 us -> 263 us (0.989)
  Pallas kernels: 76.4 us -> 69.3 us
  waiting for transfers between devices: 144 us -> 147 us
    pallas_call x2, Pallas kernels: 20.6 us -> 16.6 us  [on_device(): pl.pallas_call(functools.partial(backward_kernel, first, last), grid=(per...]
    pallas_call x2, Pallas kernels: 18 us -> 14.9 us  [on_device(): pl.pallas_call(forward_kernel, grid=(per,), in_specs=[map_spec, pl.BlockS...]
  transfers between devices with their start and end apart: 4 -> 4, of which waited for: 4 -> 4; matrix products, arithmetic and copies ran while one was open for 0% -> 0% of each run, Pallas kernels for 21% -> 20%
where the time goes in v9:
time: 263 us; the launch traced here: 262 us
  waiting for transfers between devices  147 us (56%)
  Pallas kernels  69.3 us (26%)
  blocking collectives  23.6 us (9%)
  starting transfers between devices  20.1 us (8%)
    all_to_all x2, waiting for transfers between devices, on_device(): returned = lax.all_to_all(lined, 'pencil', 0, 0, tiled=True)  73.8 us
    all_to_all x2, waiting for transfers between devices, on_device(): gathered = lax.all_to_all(split, 'pencil', 0, 0, tiled=True)  73.5 us
    pallas_call x2, Pallas kernels, on_device(): pl.pallas_call(line_kernel, grid=(per, depth), in_specs=[pl.BlockSpec((pe...  37.8 us
    all_to_all x1, blocking collectives, on_device(): parts = lax.all_to_all(parts, 'coil', 0, 0, tiled=True)  23.6 us
    pallas_call x2, Pallas kernels, on_device(): pl.pallas_call(functools.partial(backward_kernel, first, last), grid=(per...  16.6 us
    pallas_call x2, Pallas kernels, on_device(): pl.pallas_call(forward_kernel, grid=(per,), in_specs=[map_spec, pl.BlockS...  14.9 us
    all_to_all x2, starting transfers between devices, on_device(): gathered = lax.all_to_all(split, 'pencil', 0, 0, tiled=True)  11 us
    all_to_all x2, starting transfers between devices, on_device(): returned = lax.all_to_all(lined, 'pencil', 0, 0, tiled=True)  9.09 us
  transfers between devices with their start and end apart: 4, of which 4 were waited for; matrix products, arithmetic and copies ran while one was open for 0% of the time, Pallas kernels for 20%

profile of v9, /device:TPU:0, one launch (start us, length us, event | category | flops | bytes accessed | tf_op | source)
XLA Modules:
  0.0 262.2 jit_solution(15472403550532408830)
XLA Ops:
  0.0 0.0 copy-start
  0.0 7.4 %shard_map.111 = bf16[16,4,2,16,1024]{4,3,2,1,0:T(8,128)(2,1)} custom-call(bf16[8,32,16,1024]{3,2,1,0:T(8,128)(2,1)} %map_ref.7, bf16[32,16,1024]{2,1,0:T(8,128)(2,1)} %obj_ref.3, bf16[256,256]{1,0:T(8,128)(2,1)} %constant.28.clone.kc_ref, bf16[256,256]{1,0:T(8,128)(2,1)} %constant.29.clone.ks_ref), custom_call_target="tpu_custom_call" | custom-call | tf_op jit(solution)/shard_map/pallas_call | solution.py:168
  7.5 6.5 %all-to-all-start.2 = ((bf16[16,4,2,16,1024]{4,3,2,1,0:T(8,128)(2,1)}), bf16[16,4,2,16,1024]{4,3,2,1,0:T(8,128)(2,1)}, u32[]{:S(2)}, u32[]{:S(2)}) async-start(bf16[16,4,2,16,1024]{4,3,2,1,0:T(8,128)(2,1)} %shard_map.111), calls=%async_computation.2 | async-start | bytes 8388608 | tf_op jit(solution)/shard_map/all_to_all | solution.py:183
  13.9 7.5 %shard_map.109 = bf16[16,4,2,16,1024]{4,3,2,1,0:T(8,128)(2,1)} custom-call(bf16[8,32,16,1024]{3,2,1,0:T(8,128)(2,1)} %map_ref.7, bf16[32,16,1024]{2,1,0:T(8,128)(2,1)} %obj_ref.3, bf16[256,256]{1,0:T(8,128)(2,1)} %constant.28.clone.kc_ref, bf16[256,256]{1,0:T(8,128)(2,1)} %constant.29.clone.ks_ref), custom_call_target="tpu_custom_call" | custom-call | tf_op jit(solution)/shard_map/pallas_call | solution.py:168
  21.4 43.0 %all-to-all-done.2.in_ref = bf16[16,4,2,16,1024]{4,3,2,1,0:T(8,128)(2,1)} async-done(((bf16[16,4,2,16,1024]{4,3,2,1,0:T(8,128)(2,1)}), bf16[16,4,2,16,1024]{4,3,2,1,0:T(8,128)(2,1)}, u32[]{:S(2)}, u32[]{:S(2)}) %all-to-all-start.2) | async-done | bytes 4194336 | tf_op jit(solution)/shard_map/all_to_all | solution.py:183
  64.4 4.5 %all-to-all-start = ((bf16[16,4,2,16,1024]{4,3,2,1,0:T(8,128)(2,1)}), bf16[16,4,2,16,1024]{4,3,2,1,0:T(8,128)(2,1)}, u32[]{:S(2)}, u32[]{:S(2)}) async-start(bf16[16,4,2,16,1024]{4,3,2,1,0:T(8,128)(2,1)} %shard_map.109), calls=%async_computation | async-start | bytes 8388608 | tf_op jit(solution)/shard_map/all_to_all | solution.py:183
  68.9 0.0 copy-done
  68.9 0.9 copy.13.mask_ref
  69.8 18.9 %shard_map.112 = bf16[16,4,2,16,1024]{4,3,2,1,0:T(8,128)(2,1)} custom-call(bf16[16,4,2,16,1024]{4,3,2,1,0:T(8,128)(2,1)} %all-to-all-done.2.in_ref, s32[2,256,4]{2,1,0:T(8,128)} %copy.13.mask_ref, bf16[1024,1024]{1,0:T(8,128)(2,1)} %constant.26.clone.fx_ref, bf16[1024,1024]{1,0:T(8,128)(2,1)} %constant.27.clone.fxi_ref, ...), custom_call_target="tpu_custom_call" | custom-call | tf_op jit(solution)/shard_map/pallas_call | solution.py:184
  88.7 30.6 %all-to-all-done.in_ref = bf16[16,4,2,16,1024]{4,3,2,1,0:T(8,128)(2,1)} async-done(((bf16[16,4,2,16,1024]{4,3,2,1,0:T(8,128)(2,1)}), bf16[16,4,2,16,1024]{4,3,2,1,0:T(8,128)(2,1)}, u32[]{:S(2)}, u32[]{:S(2)}) %all-to-all-start) | async-done | bytes 4194336 | tf_op jit(solution)/shard_map/all_to_all | solution.py:183
  119.3 4.5 %all-to-all-start.3 = ((bf16[16,4,2,16,1024]{4,3,2,1,0:T(8,128)(2,1)}), bf16[16,4,2,16,1024]{4,3,2,1,0:T(8,128)(2,1)}, u32[]{:S(2)}, u32[]{:S(2)}) async-start(bf16[16,4,2,16,1024]{4,3,2,1,0:T(8,128)(2,1)} %shard_map.112), calls=%async_computation.3 | async-start | bytes 8388608 | tf_op jit(solution)/shard_map/all_to_all | solution.py:201
  123.8 18.9 %shard_map.110 = bf16[16,4,2,16,1024]{4,3,2,1,0:T(8,128)(2,1)} custom-call(bf16[16,4,2,16,1024]{4,3,2,1,0:T(8,128)(2,1)} %all-to-all-done.in_ref, s32[2,256,4]{2,1,0:T(8,128)} %copy.13.mask_ref, bf16[1024,1024]{1,0:T(8,128)(2,1)} %constant.26.clone.fx_ref, bf16[1024,1024]{1,0:T(8,128)(2,1)} %constant.27.clone.fxi_ref, ...), custom_call_target="tpu_custom_call" | custom-call | tf_op jit(solution)/shard_map/pallas_call | solution.py:184
  142.7 31.5 %all-to-all-done.3.in_ref = bf16[16,4,2,16,1024]{4,3,2,1,0:T(8,128)(2,1)} async-done(((bf16[16,4,2,16,1024]{4,3,2,1,0:T(8,128)(2,1)}), bf16[16,4,2,16,1024]{4,3,2,1,0:T(8,128)(2,1)}, u32[]{:S(2)}, u32[]{:S(2)}) %all-to-all-start.3) | async-done | bytes 4194336 | tf_op jit(solution)/shard_map/all_to_all | solution.py:201
  174.2 4.5 %all-to-all-start.1 = ((bf16[16,4,2,16,1024]{4,3,2,1,0:T(8,128)(2,1)}), bf16[16,4,2,16,1024]{4,3,2,1,0:T(8,128)(2,1)}, u32[]{:S(2)}, u32[]{:S(2)}) async-start(bf16[16,4,2,16,1024]{4,3,2,1,0:T(8,128)(2,1)} %shard_map.110), calls=%async_computation.1 | async-start | bytes 8388608 | tf_op jit(solution)/shard_map/all_to_all | solution.py:201
  178.7 8.0 %shard_map.113.refs_0_ = f32[32,16,1024]{2,1,0:T(8,128)} custom-call(bf16[16,4,2,16,1024]{4,3,2,1,0:T(8,128)(2,1)} %all-to-all-done.3.in_ref, bf16[8,32,16,1024]{3,2,1,0:T(8,128)(2,1)} %map_ref.7, bf16[256,256]{1,0:T(8,128)(2,1)} %constant.28.clone.kc_ref, bf16[256,256]{1,0:T(8,128)(2,1)} %constant.30.clone.ks_ref), custom_call_target="tpu_custom_call" | custom-call | tf_op jit(solution)/shard_map/pallas_call | solution.py:213
  186.8 42.4 %all-to-all-done.1.in_ref = bf16[16,4,2,16,1024]{4,3,2,1,0:T(8,128)(2,1)} async-done(((bf16[16,4,2,16,1024]{4,3,2,1,0:T(8,128)(2,1)}), bf16[16,4,2,16,1024]{4,3,2,1,0:T(8,128)(2,1)}, u32[]{:S(2)}, u32[]{:S(2)}) %all-to-all-start.1) | async-done | bytes 4194336 | tf_op jit(solution)/shard_map/all_to_all | solution.py:201
  229.1 8.6 %shard_map.114 = bf16[32,16,1024]{2,1,0:T(8,128)(2,1)} custom-call(bf16[16,4,2,16,1024]{4,3,2,1,0:T(8,128)(2,1)} %all-to-all-done.1.in_ref, bf16[8,32,16,1024]{3,2,1,0:T(8,128)(2,1)} %map_ref.7, bf16[256,256]{1,0:T(8,128)(2,1)} %constant.28.clone.kc_ref, bf16[256,256]{1,0:T(8,128)(2,1)} %constant.30.clone.ks_ref, f32[32,16,1024]{2,1,0:T(8,128)} %shard_map.113.refs_0_), custom_call_target="tpu_custom_call" | custom-call | tf_op jit(solution)/shard_map/pallas_call | solution.py:213
  237.7 23.6 %all_to_all.25 = bf16[8,4,16,1024]{3,2,1,0:T(8,128)(2,1)S(1)} all-to-all(bf16[8,4,16,1024]{3,2,1,0:T(8,128)(2,1)} %bitcast.1), channel_id=1, replica_groups=mesh['coil'=8,'pencil'=16] {'coil'}, dimensions={0} | all-to-all | bytes 2097152 | tf_op jit(solution)/shard_map/all_to_all | solution.py:229
  261.3 0.9 convert_reduce_fusion
  (1 shorter events, 0.0 us)
Async XLA Ops:
  0.0 68.9 %copy-start = (s32[32,256,4]{1,2,0:T(4,128)S(1)}, s32[32,256,4]{1,2,0:T(4,128)}, u32[]{:S(2)}) copy-start(s32[32,256,4]{1,2,0:T(4,128)} %param.13) | copy-start | bytes 393220
  7.5 56.9 %all-to-all-start.2 = ((bf16[16,4,2,16,1024]{4,3,2,1,0:T(8,128)(2,1)}), bf16[16,4,2,16,1024]{4,3,2,1,0:T(8,128)(2,1)}, u32[]{:S(2)}, u32[]{:S(2)}) async-start(bf16[16,4,2,16,1024]{4,3,2,1,0:T(8,128)(2,1)} %shard_map.111), calls=%async_computation.2 | async-start | bytes 8388608 | tf_op jit(solution)/shard_map/all_to_all | solution.py:183
  64.4 54.9 %all-to-all-start = ((bf16[16,4,2,16,1024]{4,3,2,1,0:T(8,128)(2,1)}), bf16[16,4,2,16,1024]{4,3,2,1,0:T(8,128)(2,1)}, u32[]{:S(2)}, u32[]{:S(2)}) async-start(bf16[16,4,2,16,1024]{4,3,2,1,0:T(8,128)(2,1)} %shard_map.109), calls=%async_computation | async-start | bytes 8388608 | tf_op jit(solution)/shard_map/all_to_all | solution.py:183
  119.3 54.9 %all-to-all-start.3 = ((bf16[16,4,2,16,1024]{4,3,2,1,0:T(8,128)(2,1)}), bf16[16,4,2,16,1024]{4,3,2,1,0:T(8,128)(2,1)}, u32[]{:S(2)}, u32[]{:S(2)}) async-start(bf16[16,4,2,16,1024]{4,3,2,1,0:T(8,128)(2,1)} %shard_map.112), calls=%async_computation.3 | async-start | bytes 8388608 | tf_op jit(solution)/shard_map/all_to_all | solution.py:201
  174.2 54.9 %all-to-all-start.1 = ((bf16[16,4,2,16,1024]{4,3,2,1,0:T(8,128)(2,1)}), bf16[16,4,2,16,1024]{4,3,2,1,0:T(8,128)(2,1)}, u32[]{:S(2)}, u32[]{:S(2)}) async-start(bf16[16,4,2,16,1024]{4,3,2,1,0:T(8,128)(2,1)} %shard_map.110), calls=%async_computation.1 | async-start | bytes 8388608 | tf_op jit(solution)/shard_map/all_to_all | solution.py:201

commit v10 on v9

--- a/solution.py
+++ b/solution.py
@@ -21,18 +21,21 @@
     return (cosine, sine_part)
 
 
-def readout_table(length, direction):
-    cosine, sine_part = dft_tables(length, direction)
-    upper = np.concatenate([cosine, sine_part], axis=1)
-    lower = np.concatenate([-sine_part, cosine], axis=1)
-    return jnp.asarray(np.concatenate([upper, lower], axis=0))
-
-
-def block_table(length, direction):
-    cosine, sine_part = dft_tables(length, direction)
-    upper = np.concatenate([cosine, -sine_part], axis=1)
-    lower = np.concatenate([sine_part, cosine], axis=1)
-    return jnp.asarray(np.concatenate([upper, lower], axis=0))
+def complex_tables(length):
+    cosine, sine_part = dft_tables(length, -1.0)
+    return lax.optimization_barrier((jnp.asarray(cosine), jnp.asarray(sine_part)))
+
+
+def readout_table(cosine, sine_part):
+    upper = jnp.concatenate([cosine, sine_part], axis=1)
+    lower = jnp.concatenate([-sine_part, cosine], axis=1)
+    return jnp.concatenate([upper, lower], axis=0)
+
+
+def block_table(cosine, sine_part):
+    upper = jnp.concatenate([cosine, -sine_part], axis=1)
+    lower = jnp.concatenate([sine_part, cosine], axis=1)
+    return jnp.concatenate([upper, lower], axis=0)
 
 
 def slice_tables(length, direction, rows):
@@ -148,13 +151,15 @@
     lines = rows * pencils
     position = lax.axis_index("pencil")
 
-    forward_x = readout_table(readout, -1.0)
-    inverse_x = readout_table(readout, 1.0)
+    cos_x, sin_x = complex_tables(readout)
+    forward_x = readout_table(cos_x, sin_x)
+    inverse_x = readout_table(cos_x, -sin_x)
     band = 8 if rows % 8 == 0 else rows
     kc_f, ks_f = slice_tables(slices, -1.0, band)
     kc_i, ks_i = slice_tables(slices, 1.0, band)
-    wf = block_table(lines, -1.0)
-    wi = block_table(lines, 1.0)
+    cos_y, sin_y = complex_tables(lines)
+    wf = block_table(cos_y, sin_y)
+    wi = block_table(cos_y, -sin_y)
     mask = lax.dynamic_slice_in_dim(sample_mask, position * depth, depth, 0)
 
     tail = coils // 2

time: 263 us -> 263 us (level)
  other arithmetic: 0.88 us -> 12 us
  waiting for transfers between devices: 147 us -> 136 us
    all_to_all x2, waiting for transfers between devices: 73.5 us -> 62.4 us  [on_device(): gathered = lax.all_to_all(split, 'pencil', 0, 0, tiled=True)]
    concatenate x0 -> x2, other arithmetic: none -> 11 us  [the longest x1 9.99 us: readout_table(): return jnp.concatenate([upper, lower], axis=0)]
  transfers between devices with their start and end apart: 4 -> 4, of which waited for: 4 -> 4; matrix products, arithmetic and copies ran while one was open for 0% -> 5% of each run, Pallas kernels for 20% -> 20%
where the time goes in v10:
time: 263 us; the launch traced here: 262 us
  waiting for transfers between devices  136 us (52%)
  Pallas kernels  69.2 us (26%)
  blocking collectives  23.6 us (9%)
  starting transfers between devices  20.3 us (8%)
  other arithmetic  12 us (5%)
    all_to_all x2, waiting for transfers between devices, on_device(): returned = lax.all_to_all(lined, 'pencil', 0, 0, tiled=True)  73.7 us
    all_to_all x2, waiting for transfers between devices, on_device(): gathered = lax.all_to_all(split, 'pencil', 0, 0, tiled=True)  62.4 us
    pallas_call x2, Pallas kernels, on_device(): pl.pallas_call(line_kernel, grid=(per, depth), in_specs=[pl.BlockSpec((pe...  37.8 us
    all_to_all x1, blocking collectives, on_device(): parts = lax.all_to_all(parts, 'coil', 0, 0, tiled=True)  23.6 us
    pallas_call x2, Pallas kernels, on_device(): pl.pallas_call(functools.partial(backward_kernel, first, last), grid=(per...  16.5 us
    pallas_call x2, Pallas kernels, on_device(): pl.pallas_call(forward_kernel, grid=(per,), in_specs=[map_spec, pl.BlockS...  14.9 us
    all_to_all x2, starting transfers between devices, on_device(): gathered = lax.all_to_all(split, 'pencil', 0, 0, tiled=True)  11 us
    concatenate x1, other arithmetic, readout_table(): return jnp.concatenate([upper, lower], axis=0)  9.99 us
  transfers between devices with their start and end apart: 4, of which 4 were waited for; matrix products, arithmetic and copies ran while one was open for 5% of the time, Pallas kernels for 20%

profile of v10, /device:TPU:0, one launch (start us, length us, event | category | flops | bytes accessed | tf_op | source)
XLA Modules:
  0.0 262.1 jit_solution(3789599435938796613)
XLA Ops:
  0.0 0.0 copy-start
  0.0 7.4 %shard_map.111 = bf16[16,4,2,16,1024]{4,3,2,1,0:T(8,128)(2,1)} custom-call(bf16[8,32,16,1024]{3,2,1,0:T(8,128)(2,1)} %map_ref.7, bf16[32,16,1024]{2,1,0:T(8,128)(2,1)} %obj_ref.3, bf16[256,256]{1,0:T(8,128)(2,1)} %constant.28.clone.kc_ref, bf16[256,256]{1,0:T(8,128)(2,1)} %constant.29.clone.ks_ref), custom_call_target="tpu_custom_call" | custom-call | tf_op jit(solution)/shard_map/pallas_call | solution.py:173
  7.4 6.5 %all-to-all-start.2 = ((bf16[16,4,2,16,1024]{4,3,2,1,0:T(8,128)(2,1)}), bf16[16,4,2,16,1024]{4,3,2,1,0:T(8,128)(2,1)}, u32[]{:S(2)}, u32[]{:S(2)}) async-start(bf16[16,4,2,16,1024]{4,3,2,1,0:T(8,128)(2,1)} %shard_map.111), calls=%async_computation.2 | async-start | bytes 8388608 | tf_op jit(solution)/shard_map/all_to_all | solution.py:188
  13.9 7.4 %shard_map.109 = bf16[16,4,2,16,1024]{4,3,2,1,0:T(8,128)(2,1)} custom-call(bf16[8,32,16,1024]{3,2,1,0:T(8,128)(2,1)} %map_ref.7, bf16[32,16,1024]{2,1,0:T(8,128)(2,1)} %obj_ref.3, bf16[256,256]{1,0:T(8,128)(2,1)} %constant.28.clone.kc_ref, bf16[256,256]{1,0:T(8,128)(2,1)} %constant.29.clone.ks_ref), custom_call_target="tpu_custom_call" | custom-call | tf_op jit(solution)/shard_map/pallas_call | solution.py:173
  21.4 0.0 copy-start.3
  21.4 42.9 %all-to-all-done.2.in_ref = bf16[16,4,2,16,1024]{4,3,2,1,0:T(8,128)(2,1)} async-done(((bf16[16,4,2,16,1024]{4,3,2,1,0:T(8,128)(2,1)}), bf16[16,4,2,16,1024]{4,3,2,1,0:T(8,128)(2,1)}, u32[]{:S(2)}, u32[]{:S(2)}) %all-to-all-start.2) | async-done | bytes 4194336 | tf_op jit(solution)/shard_map/all_to_all | solution.py:188
  64.3 4.5 %all-to-all-start = ((bf16[16,4,2,16,1024]{4,3,2,1,0:T(8,128)(2,1)}), bf16[16,4,2,16,1024]{4,3,2,1,0:T(8,128)(2,1)}, u32[]{:S(2)}, u32[]{:S(2)}) async-start(bf16[16,4,2,16,1024]{4,3,2,1,0:T(8,128)(2,1)} %shard_map.109), calls=%async_computation | async-start | bytes 8388608 | tf_op jit(solution)/shard_map/all_to_all | solution.py:188
  68.9 0.0 copy-done.2
  68.9 0.0 copy-done
  68.9 0.9 copy.13.mask_ref
  69.8 0.1 neg.4
  69.9 1.0 fusion.3
  71.0 10.0 %fusion.1 = (bf16[1024,1024]{1,0:T(8,128)(2,1)}, bf16[1024,1024]{1,0:T(8,128)(2,1)}) fusion(bf16[512,512]{1,0:T(8,128)(2,1)S(1)} %copy-done.3, bf16[512,512]{1,0:T(8,128)(2,1)S(1)} %copy-done.1, bf16[512,512]{1,0:T(8,128)(2,1)S(1)} %neg.4), kind=kLoop, calls=%fused_computation.5 | loop fusion | flops 14680064 | bytes 5767168 | tf_op jit(solution)/shard_map/concatenate | solution.py:32
  80.9 18.9 %shard_map.112 = bf16[16,4,2,16,1024]{4,3,2,1,0:T(8,128)(2,1)} custom-call(bf16[16,4,2,16,1024]{4,3,2,1,0:T(8,128)(2,1)} %all-to-all-done.2.in_ref, s32[2,256,4]{2,1,0:T(8,128)} %copy.13.mask_ref, bf16[1024,1024]{1,0:T(8,128)(2,1)} %get-tuple-element.14.fx_ref, bf16[1024,1024]{1,0:T(8,128)(2,1)} %get-tuple-element.13.fxi_ref, ...), custom_call_target="tpu_custom_call" | custom-call | tf_op jit(solution)/shard_map/pallas_call | solution.py:189
  99.8 19.4 %all-to-all-done.in_ref = bf16[16,4,2,16,1024]{4,3,2,1,0:T(8,128)(2,1)} async-done(((bf16[16,4,2,16,1024]{4,3,2,1,0:T(8,128)(2,1)}), bf16[16,4,2,16,1024]{4,3,2,1,0:T(8,128)(2,1)}, u32[]{:S(2)}, u32[]{:S(2)}) %all-to-all-start) | async-done | bytes 4194336 | tf_op jit(solution)/shard_map/all_to_all | solution.py:188
  119.2 4.5 %all-to-all-start.3 = ((bf16[16,4,2,16,1024]{4,3,2,1,0:T(8,128)(2,1)}), bf16[16,4,2,16,1024]{4,3,2,1,0:T(8,128)(2,1)}, u32[]{:S(2)}, u32[]{:S(2)}) async-start(bf16[16,4,2,16,1024]{4,3,2,1,0:T(8,128)(2,1)} %shard_map.112), calls=%async_computation.3 | async-start | bytes 8388608 | tf_op jit(solution)/shard_map/all_to_all | solution.py:206
  123.8 18.9 %shard_map.110 = bf16[16,4,2,16,1024]{4,3,2,1,0:T(8,128)(2,1)} custom-call(bf16[16,4,2,16,1024]{4,3,2,1,0:T(8,128)(2,1)} %all-to-all-done.in_ref, s32[2,256,4]{2,1,0:T(8,128)} %copy.13.mask_ref, bf16[1024,1024]{1,0:T(8,128)(2,1)} %get-tuple-element.14.fx_ref, bf16[1024,1024]{1,0:T(8,128)(2,1)} %get-tuple-element.13.fxi_ref, ...), custom_call_target="tpu_custom_call" | custom-call | tf_op jit(solution)/shard_map/pallas_call | solution.py:189
  142.7 31.5 %all-to-all-done.3.in_ref = bf16[16,4,2,16,1024]{4,3,2,1,0:T(8,128)(2,1)} async-done(((bf16[16,4,2,16,1024]{4,3,2,1,0:T(8,128)(2,1)}), bf16[16,4,2,16,1024]{4,3,2,1,0:T(8,128)(2,1)}, u32[]{:S(2)}, u32[]{:S(2)}) %all-to-all-start.3) | async-done | bytes 4194336 | tf_op jit(solution)/shard_map/all_to_all | solution.py:206
  174.2 4.7 %all-to-all-start.1 = ((bf16[16,4,2,16,1024]{4,3,2,1,0:T(8,128)(2,1)}), bf16[16,4,2,16,1024]{4,3,2,1,0:T(8,128)(2,1)}, u32[]{:S(2)}, u32[]{:S(2)}) async-start(bf16[16,4,2,16,1024]{4,3,2,1,0:T(8,128)(2,1)} %shard_map.110), calls=%async_computation.1 | async-start | bytes 8388608 | tf_op jit(solution)/shard_map/all_to_all | solution.py:206
  178.9 8.0 %shard_map.113.refs_0_ = f32[32,16,1024]{2,1,0:T(8,128)} custom-call(bf16[16,4,2,16,1024]{4,3,2,1,0:T(8,128)(2,1)} %all-to-all-done.3.in_ref, bf16[8,32,16,1024]{3,2,1,0:T(8,128)(2,1)} %map_ref.7, bf16[256,256]{1,0:T(8,128)(2,1)} %constant.28.clone.kc_ref, bf16[256,256]{1,0:T(8,128)(2,1)} %constant.30.clone.ks_ref), custom_call_target="tpu_custom_call" | custom-call | tf_op jit(solution)/shard_map/pallas_call | solution.py:218
  186.9 42.2 %all-to-all-done.1.in_ref = bf16[16,4,2,16,1024]{4,3,2,1,0:T(8,128)(2,1)} async-done(((bf16[16,4,2,16,1024]{4,3,2,1,0:T(8,128)(2,1)}), bf16[16,4,2,16,1024]{4,3,2,1,0:T(8,128)(2,1)}, u32[]{:S(2)}, u32[]{:S(2)}) %all-to-all-start.1) | async-done | bytes 4194336 | tf_op jit(solution)/shard_map/all_to_all | solution.py:206
  229.1 8.6 %shard_map.114 = bf16[32,16,1024]{2,1,0:T(8,128)(2,1)} custom-call(bf16[16,4,2,16,1024]{4,3,2,1,0:T(8,128)(2,1)} %all-to-all-done.1.in_ref, bf16[8,32,16,1024]{3,2,1,0:T(8,128)(2,1)} %map_ref.7, bf16[256,256]{1,0:T(8,128)(2,1)} %constant.28.clone.kc_ref, bf16[256,256]{1,0:T(8,128)(2,1)} %constant.30.clone.ks_ref, f32[32,16,1024]{2,1,0:T(8,128)} %shard_map.113.refs_0_), custom_call_target="tpu_custom_call" | custom-call | tf_op jit(solution)/shard_map/pallas_call | solution.py:218
  237.6 23.6 %all_to_all.25 = bf16[8,4,16,1024]{3,2,1,0:T(8,128)(2,1)S(1)} all-to-all(bf16[8,4,16,1024]{3,2,1,0:T(8,128)(2,1)} %bitcast.1), channel_id=1, replica_groups=mesh['coil'=8,'pencil'=16] {'coil'}, dimensions={0} | all-to-all | bytes 2097152 | tf_op jit(solution)/shard_map/all_to_all | solution.py:234
  261.3 0.9 convert_reduce_fusion
  (8 shorter events, 0.0 us)
Async XLA Ops:
  0.0 68.9 %copy-start = (s32[32,256,4]{1,2,0:T(4,128)S(1)}, s32[32,256,4]{1,2,0:T(4,128)}, u32[]{:S(2)}) copy-start(s32[32,256,4]{1,2,0:T(4,128)} %param.13) | copy-start | bytes 393220
  7.4 56.9 %all-to-all-start.2 = ((bf16[16,4,2,16,1024]{4,3,2,1,0:T(8,128)(2,1)}), bf16[16,4,2,16,1024]{4,3,2,1,0:T(8,128)(2,1)}, u32[]{:S(2)}, u32[]{:S(2)}) async-start(bf16[16,4,2,16,1024]{4,3,2,1,0:T(8,128)(2,1)} %shard_map.111), calls=%async_computation.2 | async-start | bytes 8388608 | tf_op jit(solution)/shard_map/all_to_all | solution.py:188
  21.4 47.5 %copy-start.2 = (bf16[256,256]{1,0:T(8,128)(2,1)S(1)}, bf16[256,256]{1,0:T(8,128)(2,1)}, u32[]{:S(2)}) copy-start(bf16[256,256]{1,0:T(8,128)(2,1)} %constant.32.clone) | copy-start | bytes 393220
  21.4 48.5 %copy-start.1 = (bf16[512,512]{1,0:T(8,128)(2,1)S(1)}, bf16[512,512]{1,0:T(8,128)(2,1)}, u32[]{:S(2)}) copy-start(bf16[512,512]{1,0:T(8,128)(2,1)} %constant.27.clone) | copy-start | bytes 1572868
  21.4 48.5 %copy-start.4 = (bf16[256,256]{1,0:T(8,128)(2,1)S(1)}, bf16[256,256]{1,0:T(8,128)(2,1)}, u32[]{:S(2)}) copy-start(bf16[256,256]{1,0:T(8,128)(2,1)} %constant.31.clone) | copy-start | bytes 393220
  21.4 49.6 %copy-start.3 = (bf16[512,512]{1,0:T(8,128)(2,1)S(1)}, bf16[512,512]{1,0:T(8,128)(2,1)}, u32[]{:S(2)}) copy-start(bf16[512,512]{1,0:T(8,128)(2,1)} %constant.26.clone) | copy-start | bytes 1572868
  64.3 54.9 %all-to-all-start = ((bf16[16,4,2,16,1024]{4,3,2,1,0:T(8,128)(2,1)}), bf16[16,4,2,16,1024]{4,3,2,1,0:T(8,128)(2,1)}, u32[]{:S(2)}, u32[]{:S(2)}) async-start(bf16[16,4,2,16,1024]{4,3,2,1,0:T(8,128)(2,1)} %shard_map.109), calls=%async_computation | async-start | bytes 8388608 | tf_op jit(solution)/shard_map/all_to_all | solution.py:188
  119.2 54.9 %all-to-all-start.3 = ((bf16[16,4,2,16,1024]{4,3,2,1,0:T(8,128)(2,1)}), bf16[16,4,2,16,1024]{4,3,2,1,0:T(8,128)(2,1)}, u32[]{:S(2)}, u32[]{:S(2)}) async-start(bf16[16,4,2,16,1024]{4,3,2,1,0:T(8,128)(2,1)} %shard_map.112), calls=%async_computation.3 | async-start | bytes 8388608 | tf_op jit(solution)/shard_map/all_to_all | solution.py:206
  174.2 54.9 %all-to-all-start.1 = ((bf16[16,4,2,16,1024]{4,3,2,1,0:T(8,128)(2,1)}), bf16[16,4,2,16,1024]{4,3,2,1,0:T(8,128)(2,1)}, u32[]{:S(2)}, u32[]{:S(2)}) async-start(bf16[16,4,2,16,1024]{4,3,2,1,0:T(8,128)(2,1)} %shard_map.110), calls=%async_computation.1 | async-start | bytes 8388608 | tf_op jit(solution)/shard_map/all_to_all | solution.py:206

commit v11 on v10

--- a/solution.py
+++ b/solution.py
@@ -151,26 +151,20 @@
     lines = rows * pencils
     position = lax.axis_index("pencil")
 
-    cos_x, sin_x = complex_tables(readout)
-    forward_x = readout_table(cos_x, sin_x)
-    inverse_x = readout_table(cos_x, -sin_x)
     band = 8 if rows % 8 == 0 else rows
     kc_f, ks_f = slice_tables(slices, -1.0, band)
     kc_i, ks_i = slice_tables(slices, 1.0, band)
-    cos_y, sin_y = complex_tables(lines)
-    wf = block_table(cos_y, sin_y)
-    wi = block_table(cos_y, -sin_y)
     mask = lax.dynamic_slice_in_dim(sample_mask, position * depth, depth, 0)
 
-    tail = coils // 2
+    tail = coils // 4
     sizes = [coils - tail, tail] if tail > 0 else [coils]
     const2 = lambda c: (0, 0)
     const3 = lambda c: (0, 0, 0)
-    acc = None
+    splits = []
     start = 0
     for per in sizes:
         map_spec = pl.BlockSpec((None, slices, rows, width), lambda c, s=start: (c + s, 0, 0, 0))
-        split = pl.pallas_call(
+        splits.append(pl.pallas_call(
             forward_kernel,
             grid=(per,),
             in_specs=[
@@ -184,8 +178,24 @@
             ),
             out_shape=jax.ShapeDtypeStruct((pencils, per, depth, rows, width), jnp.bfloat16),
             compiler_params=PARAMS,
-        )(coil_maps, object_image, kc_f, ks_f)
-        gathered = lax.all_to_all(split, "pencil", 0, 0, tiled=True)
+        )(coil_maps, object_image, kc_f, ks_f))
+        start += per
+
+    cos_x, sin_x = complex_tables(readout)
+    cos_y, sin_y = complex_tables(lines)
+    forward_x = readout_table(cos_x, sin_x)
+    inverse_x = readout_table(cos_x, -sin_x)
+    wf = block_table(cos_y, sin_y)
+    wi = block_table(cos_y, -sin_y)
+    forward_x, inverse_x, wf, wi, splits[-1] = lax.optimization_barrier(
+        (forward_x, inverse_x, wf, wi, splits[-1])
+    )
+    volumes = [lax.all_to_all(split, "pencil", 0, 0, tiled=True) for split in splits]
+
+    acc = None
+    start = 0
+    for per, gathered in zip(sizes, volumes):
+        map_spec = pl.BlockSpec((None, slices, rows, width), lambda c, s=start: (c + s, 0, 0, 0))
         lined = pl.pallas_call(
             line_kernel,
             grid=(per, depth),

time: 263 us -> 264 us (level)
  local copies, waits for them, and re-layouts: 0.89 us -> 3.56 us
    all_to_all x2, waiting for transfers between devices: 62.4 us -> 57.2 us  [on_device(): lax.all_to_all(split, 'pencil', 0, 0, tiled=True)]
    all_to_all x2, waiting for transfers between devices: 73.7 us -> 78.6 us  [on_device(): returned = lax.all_to_all(lined, 'pencil', 0, 0, tiled=True)]
    unnamed x11 -> x15, local copies, waits for them, and re-layouts: 0.88 us -> 3.55 us
where the time goes in v11:
time: 264 us
  waiting for transfers between devices  136 us (52%)
  Pallas kernels  69.3 us (26%)
  blocking collectives  23.6 us (9%)
  starting transfers between devices  19.4 us (7%)
  other arithmetic  12 us (5%)
  local copies, waits for them, and re-layouts  3.56 us (1%)
    all_to_all x2, waiting for transfers between devices, on_device(): returned = lax.all_to_all(lined, 'pencil', 0, 0, tiled=True)  78.6 us
    all_to_all x2, waiting for transfers between devices, on_device(): lax.all_to_all(split, 'pencil', 0, 0, tiled=True)  57.2 us
    pallas_call x2, Pallas kernels, on_device(): pl.pallas_call(line_kernel, grid=(per, depth), in_specs=[pl.BlockSpec((pe...  37.8 us
    all_to_all x1, blocking collectives, on_device(): parts = lax.all_to_all(parts, 'coil', 0, 0, tiled=True)  23.6 us
    pallas_call x2, Pallas kernels, on_device(): pl.pallas_call(functools.partial(backward_kernel, first, last), grid=(per...  16.5 us
    pallas_call x2, Pallas kernels, on_device(): pl.pallas_call(forward_kernel, grid=(per,), in_specs=[map_spec, pl.BlockS...  15 us
    all_to_all x2, starting transfers between devices, on_device(): lax.all_to_all(split, 'pencil', 0, 0, tiled=True)  10.2 us
    concatenate x1, other arithmetic, readout_table(): return jnp.concatenate([upper, lower], axis=0)  9.98 us
  transfers between devices with their start and end apart: 4, of which 4 were waited for; matrix products, arithmetic and copies ran while one was open for 5% of the time, Pallas kernels for 20%

profile of v11, /device:TPU:0, one launch (start us, length us, event | category | flops | bytes accessed | tf_op | source)
XLA Modules:
  0.0 263.8 jit_solution(3235303526572428148)
XLA Ops:
  0.0 10.2 %shard_map.111 = bf16[16,6,2,16,1024]{4,3,2,1,0:T(8,128)(2,1)} custom-call(bf16[8,32,16,1024]{3,2,1,0:T(8,128)(2,1)} %map_ref.7, bf16[32,16,1024]{2,1,0:T(8,128)(2,1)} %obj_ref.3, bf16[256,256]{1,0:T(8,128)(2,1)} %constant.26.clone.kc_ref, bf16[256,256]{1,0:T(8,128)(2,1)} %constant.27.clone.ks_ref), custom_call_target="tpu_custom_call" | custom-call | tf_op jit(solution)/shard_map/pallas_call | solution.py:167
  10.2 6.5 %all-to-all-start.2 = ((bf16[16,6,2,16,1024]{4,3,2,1,0:T(8,128)(2,1)}), bf16[16,6,2,16,1024]{4,3,2,1,0:T(8,128)(2,1)}, u32[]{:S(2)}, u32[]{:S(2)}) async-start(bf16[16,6,2,16,1024]{4,3,2,1,0:T(8,128)(2,1)} %shard_map.111), calls=%async_computation.2 | async-start | bytes 12582912 | tf_op jit(solution)/shard_map/all_to_all | solution.py:193
  16.7 0.0 copy-start.4
  16.7 0.0 copy-start.6
  16.7 4.8 %shard_map.109 = bf16[16,2,2,16,1024]{4,3,2,1,0:T(8,128)(2,1)} custom-call(bf16[8,32,16,1024]{3,2,1,0:T(8,128)(2,1)} %map_ref.7, bf16[32,16,1024]{2,1,0:T(8,128)(2,1)} %obj_ref.3, bf16[256,256]{1,0:T(8,128)(2,1)} %constant.26.clone.kc_ref, bf16[256,256]{1,0:T(8,128)(2,1)} %constant.27.clone.ks_ref), custom_call_target="tpu_custom_call" | custom-call | tf_op jit(solution)/shard_map/pallas_call | solution.py:167
  21.6 0.1 neg.4
  21.7 1.1 fusion.3
  22.8 10.0 %fusion.1 = (bf16[1024,1024]{1,0:T(8,128)(2,1)}, bf16[1024,1024]{1,0:T(8,128)(2,1)}) fusion(bf16[512,512]{1,0:T(8,128)(2,1)S(1)} %copy-done.5, bf16[512,512]{1,0:T(8,128)(2,1)S(1)} %copy-done.3, bf16[512,512]{1,0:T(8,128)(2,1)S(1)} %neg.4), kind=kLoop, calls=%fused_computation.5 | loop fusion | flops 14680064 | bytes 5767168 | tf_op jit(solution)/shard_map/concatenate | solution.py:32
  32.7 56.8 %all-to-all-done.2.in_ref = bf16[16,6,2,16,1024]{4,3,2,1,0:T(8,128)(2,1)} async-done(((bf16[16,6,2,16,1024]{4,3,2,1,0:T(8,128)(2,1)}), bf16[16,6,2,16,1024]{4,3,2,1,0:T(8,128)(2,1)}, u32[]{:S(2)}, u32[]{:S(2)}) %all-to-all-start.2) | async-done | bytes 6291488 | tf_op jit(solution)/shard_map/all_to_all | solution.py:193
  89.5 3.7 %all-to-all-start = ((bf16[16,2,2,16,1024]{4,3,2,1,0:T(8,128)(2,1)}), bf16[16,2,2,16,1024]{4,3,2,1,0:T(8,128)(2,1)S(1)}, u32[]{:S(2)}, u32[]{:S(2)}) async-start(bf16[16,2,2,16,1024]{4,3,2,1,0:T(8,128)(2,1)} %shard_map.109), calls=%async_computation | async-start | bytes 4194304 | tf_op jit(solution)/shard_map/all_to_all | solution.py:193
  93.3 0.9 copy.13.mask_ref
  94.2 26.6 %shard_map.112 = bf16[16,6,2,16,1024]{4,3,2,1,0:T(8,128)(2,1)} custom-call(bf16[16,6,2,16,1024]{4,3,2,1,0:T(8,128)(2,1)} %all-to-all-done.2.in_ref, s32[2,256,4]{2,1,0:T(8,128)} %copy.13.mask_ref, bf16[1024,1024]{1,0:T(8,128)(2,1)} %get-tuple-element.19.fx_ref, bf16[1024,1024]{1,0:T(8,128)(2,1)} %get-tuple-element.20.fxi_ref, ...), custom_call_target="tpu_custom_call" | custom-call | tf_op jit(solution)/shard_map/pallas_call | solution.py:199
  120.8 0.4 all-to-all-done.in_ref
  121.1 1.3 copy-done.1
  122.5 5.3 %all-to-all-start.3 = ((bf16[16,6,2,16,1024]{4,3,2,1,0:T(8,128)(2,1)}), bf16[16,6,2,16,1024]{4,3,2,1,0:T(8,128)(2,1)}, u32[]{:S(2)}, u32[]{:S(2)}) async-start(bf16[16,6,2,16,1024]{4,3,2,1,0:T(8,128)(2,1)} %shard_map.112), calls=%async_computation.3 | async-start | bytes 12582912 | tf_op jit(solution)/shard_map/all_to_all | solution.py:216
  127.8 11.2 %shard_map.110 = bf16[16,2,2,16,1024]{4,3,2,1,0:T(8,128)(2,1)} custom-call(bf16[16,2,2,16,1024]{4,3,2,1,0:T(8,128)(2,1)} %copy-done.1, s32[2,256,4]{2,1,0:T(8,128)} %copy.13.mask_ref, bf16[1024,1024]{1,0:T(8,128)(2,1)} %get-tuple-element.19.fx_ref, bf16[1024,1024]{1,0:T(8,128)(2,1)} %get-tuple-element.20.fxi_ref, bf16[512,512]{1,0:T(8,128)(2,1)} %get-tuple-element.21.wf_ref, ...), custom_call_target="tpu_custom_call" | custom-call | tf_op jit(solution)/shard_map/pallas_call | solution.py:199
  138.9 61.7 %all-to-all-done.3.in_ref = bf16[16,6,2,16,1024]{4,3,2,1,0:T(8,128)(2,1)} async-done(((bf16[16,6,2,16,1024]{4,3,2,1,0:T(8,128)(2,1)}), bf16[16,6,2,16,1024]{4,3,2,1,0:T(8,128)(2,1)}, u32[]{:S(2)}, u32[]{:S(2)}) %all-to-all-start.3) | async-done | bytes 6291488 | tf_op jit(solution)/shard_map/all_to_all | solution.py:216
  200.7 3.9 %all-to-all-start.1 = ((bf16[16,2,2,16,1024]{4,3,2,1,0:T(8,128)(2,1)}), bf16[16,2,2,16,1024]{4,3,2,1,0:T(8,128)(2,1)S(1)}, u32[]{:S(2)}, u32[]{:S(2)}) async-start(bf16[16,2,2,16,1024]{4,3,2,1,0:T(8,128)(2,1)} %shard_map.110), calls=%async_computation.1 | async-start | bytes 4194304 | tf_op jit(solution)/shard_map/all_to_all | solution.py:216
  204.6 10.8 %shard_map.113.refs_0_ = f32[32,16,1024]{2,1,0:T(8,128)} custom-call(bf16[16,6,2,16,1024]{4,3,2,1,0:T(8,128)(2,1)} %all-to-all-done.3.in_ref, bf16[8,32,16,1024]{3,2,1,0:T(8,128)(2,1)} %map_ref.7, bf16[256,256]{1,0:T(8,128)(2,1)} %constant.26.clone.kc_ref, bf16[256,256]{1,0:T(8,128)(2,1)} %constant.28.clone.ks_ref), custom_call_target="tpu_custom_call" | custom-call | tf_op jit(solution)/shard_map/pallas_call | solution.py:228
  215.3 16.9 %all-to-all-done.1.in_ref = bf16[16,2,2,16,1024]{4,3,2,1,0:T(8,128)(2,1)S(1)} async-done(((bf16[16,2,2,16,1024]{4,3,2,1,0:T(8,128)(2,1)}), bf16[16,2,2,16,1024]{4,3,2,1,0:T(8,128)(2,1)S(1)}, u32[]{:S(2)}, u32[]{:S(2)}) %all-to-all-start.1) | async-done | bytes 2097184 | tf_op jit(solution)/shard_map/all_to_all | solution.py:216
  232.2 1.3 copy-done.2
  233.6 5.7 %shard_map.114 = bf16[32,16,1024]{2,1,0:T(8,128)(2,1)} custom-call(bf16[16,2,2,16,1024]{4,3,2,1,0:T(8,128)(2,1)} %copy-done.2, bf16[8,32,16,1024]{3,2,1,0:T(8,128)(2,1)} %map_ref.7, bf16[256,256]{1,0:T(8,128)(2,1)} %constant.26.clone.kc_ref, bf16[256,256]{1,0:T(8,128)(2,1)} %constant.28.clone.ks_ref, f32[32,16,1024]{2,1,0:T(8,128)} %shard_map.113.refs_0_), custom_call_target="tpu_custom_call" | custom-call | tf_op jit(solution)/shard_map/pallas_call | solution.py:228
  239.3 23.6 %all_to_all.25 = bf16[8,4,16,1024]{3,2,1,0:T(8,128)(2,1)S(1)} all-to-all(bf16[8,4,16,1024]{3,2,1,0:T(8,128)(2,1)} %bitcast.1), channel_id=1, replica_groups=mesh['coil'=8,'pencil'=16] {'coil'}, dimensions={0} | all-to-all | bytes 2097152 | tf_op jit(solution)/shard_map/all_to_all | solution.py:244
  262.9 0.9 convert_reduce_fusion
  (12 shorter events, 0.1 us)
Async XLA Ops:
  0.0 93.3 %copy-start = (s32[32,256,4]{1,2,0:T(4,128)S(1)}, s32[32,256,4]{1,2,0:T(4,128)}, u32[]{:S(2)}) copy-start(s32[32,256,4]{1,2,0:T(4,128)} %param.13) | copy-start | bytes 393220
  10.2 79.4 %all-to-all-start.2 = ((bf16[16,6,2,16,1024]{4,3,2,1,0:T(8,128)(2,1)}), bf16[16,6,2,16,1024]{4,3,2,1,0:T(8,128)(2,1)}, u32[]{:S(2)}, u32[]{:S(2)}) async-start(bf16[16,6,2,16,1024]{4,3,2,1,0:T(8,128)(2,1)} %shard_map.111), calls=%async_computation.2 | async-start | bytes 12582912 | tf_op jit(solution)/shard_map/all_to_all | solution.py:193
  16.7 4.9 %copy-start.4 = (bf16[256,256]{1,0:T(8,128)(2,1)S(1)}, bf16[256,256]{1,0:T(8,128)(2,1)}, u32[]{:S(2)}) copy-start(bf16[256,256]{1,0:T(8,128)(2,1)} %constant.32.clone) | copy-start | bytes 393220
  16.7 4.9 %copy-start.3 = (bf16[512,512]{1,0:T(8,128)(2,1)S(1)}, bf16[512,512]{1,0:T(8,128)(2,1)}, u32[]{:S(2)}) copy-start(bf16[512,512]{1,0:T(8,128)(2,1)} %constant.30.clone) | copy-start | bytes 1572868
  16.7 5.0 %copy-start.6 = (bf16[256,256]{1,0:T(8,128)(2,1)S(1)}, bf16[256,256]{1,0:T(8,128)(2,1)}, u32[]{:S(2)}) copy-start(bf16[256,256]{1,0:T(8,128)(2,1)} %constant.31.clone) | copy-start | bytes 393220
  16.7 6.1 %copy-start.5 = (bf16[512,512]{1,0:T(8,128)(2,1)S(1)}, bf16[512,512]{1,0:T(8,128)(2,1)}, u32[]{:S(2)}) copy-start(bf16[512,512]{1,0:T(8,128)(2,1)} %constant.29.clone) | copy-start | bytes 1572868
  89.5 31.6 %all-to-all-start = ((bf16[16,2,2,16,1024]{4,3,2,1,0:T(8,128)(2,1)}), bf16[16,2,2,16,1024]{4,3,2,1,0:T(8,128)(2,1)S(1)}, u32[]{:S(2)}, u32[]{:S(2)}) async-start(bf16[16,2,2,16,1024]{4,3,2,1,0:T(8,128)(2,1)} %shard_map.109), calls=%async_computation | async-start | bytes 4194304 | tf_op jit(solution)/shard_map/all_to_all | solution.py:193
  121.1 1.3 copy-start.1
  122.5 78.2 %all-to-all-start.3 = ((bf16[16,6,2,16,1024]{4,3,2,1,0:T(8,128)(2,1)}), bf16[16,6,2,16,1024]{4,3,2,1,0:T(8,128)(2,1)}, u32[]{:S(2)}, u32[]{:S(2)}) async-start(bf16[16,6,2,16,1024]{4,3,2,1,0:T(8,128)(2,1)} %shard_map.112), calls=%async_computation.3 | async-start | bytes 12582912 | tf_op jit(solution)/shard_map/all_to_all | solution.py:216
  200.7 31.6 %all-to-all-start.1 = ((bf16[16,2,2,16,1024]{4,3,2,1,0:T(8,128)(2,1)}), bf16[16,2,2,16,1024]{4,3,2,1,0:T(8,128)(2,1)S(1)}, u32[]{:S(2)}, u32[]{:S(2)}) async-start(bf16[16,2,2,16,1024]{4,3,2,1,0:T(8,128)(2,1)} %shard_map.110), calls=%async_computation.1 | async-start | bytes 4194304 | tf_op jit(solution)/shard_map/all_to_all | solution.py:216
  232.2 1.3 copy-start.2

commit v12 on v10

--- a/solution.py
+++ b/solution.py
@@ -67,16 +67,15 @@
     m_re, m_im = maps[..., :half], maps[..., half:]
     o_re, o_im = obj[..., :half], obj[..., half:]
     image = jnp.concatenate([m_re * o_re - m_im * o_im, m_re * o_im + m_im * o_re], axis=-1)
-    pieces = []
     for h in range(rows // band):
         part = image[:, h * band : (h + 1) * band, :].reshape(depth * band, width)
         part = part.astype(jnp.bfloat16)
         direct = dot32(kc_ref[...], part)
         crossed = dot32(ks_ref[...], part)
-        along_z = turn_add(direct, crossed, half).astype(jnp.bfloat16).astype(jnp.float32)
-        pieces.append(along_z.reshape(depth, band, width))
-    along_z = jnp.concatenate(pieces, axis=1).astype(jnp.bfloat16)
-    out_ref[...] = along_z.reshape(out_ref.shape)
+        along_z = turn_add(direct, crossed, half).astype(jnp.bfloat16)
+        out_ref[:, :, h * band : (h + 1) * band, :] = along_z.reshape(
+            out_ref.shape[:2] + (band, width)
+        )
 
 
 def line_kernel(in_ref, mask_ref, fx_ref, fxi_ref, wf_ref, wi_ref, out_ref):
@@ -104,12 +103,10 @@
     depth, rows, width = map_ref.shape
     half = width // 2
     band = kc_ref.shape[0] // depth
-    volume = in_ref[...].reshape(depth, rows, width).astype(jnp.float32)
     maps = map_ref[...].astype(jnp.float32)
     pieces = []
     for h in range(rows // band):
-        part = volume[:, h * band : (h + 1) * band, :].reshape(depth * band, width)
-        part = part.astype(jnp.bfloat16)
+        part = in_ref[:, :, h * band : (h + 1) * band, :].reshape(depth * band, width)
         direct = dot32(kc_ref[...], part)
         crossed = dot32(ks_ref[...], part)
         back_x = turn_add(direct, crossed, half).astype(jnp.bfloat16).astype(jnp.float32)

time: 263 us -> 263 us (level)
  no operation moved by 1% of the time
where the time goes in v12:
time: 263 us; the launch traced here: 262 us
  waiting for transfers between devices  136 us (52%)
  Pallas kernels  69.2 us (26%)
  blocking collectives  23.6 us (9%)
  starting transfers between devices  20.3 us (8%)
  other arithmetic  12 us (5%)
    all_to_all x2, waiting for transfers between devices, on_device(): returned = lax.all_to_all(lined, 'pencil', 0, 0, tiled=True)  73.7 us
    all_to_all x2, waiting for transfers between devices, on_device(): gathered = lax.all_to_all(split, 'pencil', 0, 0, tiled=True)  62.4 us
    pallas_call x2, Pallas kernels, on_device(): pl.pallas_call(line_kernel, grid=(per, depth), in_specs=[pl.BlockSpec((pe...  37.8 us
    all_to_all x1, blocking collectives, on_device(): parts = lax.all_to_all(parts, 'coil', 0, 0, tiled=True)  23.6 us
    pallas_call x2, Pallas kernels, on_device(): pl.pallas_call(functools.partial(backward_kernel, first, last), grid=(per...  16.5 us
    pallas_call x2, Pallas kernels, on_device(): pl.pallas_call(forward_kernel, grid=(per,), in_specs=[map_spec, pl.BlockS...  14.9 us
    all_to_all x2, starting transfers between devices, on_device(): gathered = lax.all_to_all(split, 'pencil', 0, 0, tiled=True)  11 us
    concatenate x1, other arithmetic, readout_table(): return jnp.concatenate([upper, lower], axis=0)  9.99 us
  transfers between devices with their start and end apart: 4, of which 4 were waited for; matrix products, arithmetic and copies ran while one was open for 5% of the time, Pallas kernels for 20%

profile of v12, /device:TPU:0, one launch (start us, length us, event | category | flops | bytes accessed | tf_op | source)
XLA Modules:
  0.0 262.1 jit_solution(16280081540726050870)
XLA Ops:
  0.0 0.0 copy-start
  0.0 7.4 %shard_map.111 = bf16[16,4,2,16,1024]{4,3,2,1,0:T(8,128)(2,1)} custom-call(bf16[8,32,16,1024]{3,2,1,0:T(8,128)(2,1)} %map_ref.7, bf16[32,16,1024]{2,1,0:T(8,128)(2,1)} %obj_ref.3, bf16[256,256]{1,0:T(8,128)(2,1)} %constant.28.clone.kc_ref, bf16[256,256]{1,0:T(8,128)(2,1)} %constant.29.clone.ks_ref), custom_call_target="tpu_custom_call" | custom-call | tf_op jit(solution)/shard_map/pallas_call | solution.py:170
  7.4 6.5 %all-to-all-start.2 = ((bf16[16,4,2,16,1024]{4,3,2,1,0:T(8,128)(2,1)}), bf16[16,4,2,16,1024]{4,3,2,1,0:T(8,128)(2,1)}, u32[]{:S(2)}, u32[]{:S(2)}) async-start(bf16[16,4,2,16,1024]{4,3,2,1,0:T(8,128)(2,1)} %shard_map.111), calls=%async_computation.2 | async-start | bytes 8388608 | tf_op jit(solution)/shard_map/all_to_all | solution.py:185
  13.9 7.5 %shard_map.109 = bf16[16,4,2,16,1024]{4,3,2,1,0:T(8,128)(2,1)} custom-call(bf16[8,32,16,1024]{3,2,1,0:T(8,128)(2,1)} %map_ref.7, bf16[32,16,1024]{2,1,0:T(8,128)(2,1)} %obj_ref.3, bf16[256,256]{1,0:T(8,128)(2,1)} %constant.28.clone.kc_ref, bf16[256,256]{1,0:T(8,128)(2,1)} %constant.29.clone.ks_ref), custom_call_target="tpu_custom_call" | custom-call | tf_op jit(solution)/shard_map/pallas_call | solution.py:170
  21.4 0.0 copy-start.3
  21.4 42.9 %all-to-all-done.2.in_ref = bf16[16,4,2,16,1024]{4,3,2,1,0:T(8,128)(2,1)} async-done(((bf16[16,4,2,16,1024]{4,3,2,1,0:T(8,128)(2,1)}), bf16[16,4,2,16,1024]{4,3,2,1,0:T(8,128)(2,1)}, u32[]{:S(2)}, u32[]{:S(2)}) %all-to-all-start.2) | async-done | bytes 4194336 | tf_op jit(solution)/shard_map/all_to_all | solution.py:185
  64.3 4.5 %all-to-all-start = ((bf16[16,4,2,16,1024]{4,3,2,1,0:T(8,128)(2,1)}), bf16[16,4,2,16,1024]{4,3,2,1,0:T(8,128)(2,1)}, u32[]{:S(2)}, u32[]{:S(2)}) async-start(bf16[16,4,2,16,1024]{4,3,2,1,0:T(8,128)(2,1)} %shard_map.109), calls=%async_computation | async-start | bytes 8388608 | tf_op jit(solution)/shard_map/all_to_all | solution.py:185
  68.9 0.0 copy-done.2
  68.9 0.0 copy-done
  69.0 0.9 copy.13.mask_ref
  69.8 0.1 neg.4
  69.9 1.0 fusion.3
  71.0 10.0 %fusion.1 = (bf16[1024,1024]{1,0:T(8,128)(2,1)}, bf16[1024,1024]{1,0:T(8,128)(2,1)}) fusion(bf16[512,512]{1,0:T(8,128)(2,1)S(1)} %copy-done.3, bf16[512,512]{1,0:T(8,128)(2,1)S(1)} %copy-done.1, bf16[512,512]{1,0:T(8,128)(2,1)S(1)} %neg.4), kind=kLoop, calls=%fused_computation.5 | loop fusion | flops 14680064 | bytes 5767168 | tf_op jit(solution)/shard_map/concatenate | solution.py:32
  81.0 18.9 %shard_map.112 = bf16[16,4,2,16,1024]{4,3,2,1,0:T(8,128)(2,1)} custom-call(bf16[16,4,2,16,1024]{4,3,2,1,0:T(8,128)(2,1)} %all-to-all-done.2.in_ref, s32[2,256,4]{2,1,0:T(8,128)} %copy.13.mask_ref, bf16[1024,1024]{1,0:T(8,128)(2,1)} %get-tuple-element.14.fx_ref, bf16[1024,1024]{1,0:T(8,128)(2,1)} %get-tuple-element.13.fxi_ref, ...), custom_call_target="tpu_custom_call" | custom-call | tf_op jit(solution)/shard_map/pallas_call | solution.py:186
  99.8 19.4 %all-to-all-done.in_ref = bf16[16,4,2,16,1024]{4,3,2,1,0:T(8,128)(2,1)} async-done(((bf16[16,4,2,16,1024]{4,3,2,1,0:T(8,128)(2,1)}), bf16[16,4,2,16,1024]{4,3,2,1,0:T(8,128)(2,1)}, u32[]{:S(2)}, u32[]{:S(2)}) %all-to-all-start) | async-done | bytes 4194336 | tf_op jit(solution)/shard_map/all_to_all | solution.py:185
  119.2 4.5 %all-to-all-start.3 = ((bf16[16,4,2,16,1024]{4,3,2,1,0:T(8,128)(2,1)}), bf16[16,4,2,16,1024]{4,3,2,1,0:T(8,128)(2,1)}, u32[]{:S(2)}, u32[]{:S(2)}) async-start(bf16[16,4,2,16,1024]{4,3,2,1,0:T(8,128)(2,1)} %shard_map.112), calls=%async_computation.3 | async-start | bytes 8388608 | tf_op jit(solution)/shard_map/all_to_all | solution.py:203
  123.8 18.9 %shard_map.110 = bf16[16,4,2,16,1024]{4,3,2,1,0:T(8,128)(2,1)} custom-call(bf16[16,4,2,16,1024]{4,3,2,1,0:T(8,128)(2,1)} %all-to-all-done.in_ref, s32[2,256,4]{2,1,0:T(8,128)} %copy.13.mask_ref, bf16[1024,1024]{1,0:T(8,128)(2,1)} %get-tuple-element.14.fx_ref, bf16[1024,1024]{1,0:T(8,128)(2,1)} %get-tuple-element.13.fxi_ref, ...), custom_call_target="tpu_custom_call" | custom-call | tf_op jit(solution)/shard_map/pallas_call | solution.py:186
  142.7 31.5 %all-to-all-done.3.in_ref = bf16[16,4,2,16,1024]{4,3,2,1,0:T(8,128)(2,1)} async-done(((bf16[16,4,2,16,1024]{4,3,2,1,0:T(8,128)(2,1)}), bf16[16,4,2,16,1024]{4,3,2,1,0:T(8,128)(2,1)}, u32[]{:S(2)}, u32[]{:S(2)}) %all-to-all-start.3) | async-done | bytes 4194336 | tf_op jit(solution)/shard_map/all_to_all | solution.py:203
  174.2 4.7 %all-to-all-start.1 = ((bf16[16,4,2,16,1024]{4,3,2,1,0:T(8,128)(2,1)}), bf16[16,4,2,16,1024]{4,3,2,1,0:T(8,128)(2,1)}, u32[]{:S(2)}, u32[]{:S(2)}) async-start(bf16[16,4,2,16,1024]{4,3,2,1,0:T(8,128)(2,1)} %shard_map.110), calls=%async_computation.1 | async-start | bytes 8388608 | tf_op jit(solution)/shard_map/all_to_all | solution.py:203
  178.9 8.0 %shard_map.113.refs_0_ = f32[32,16,1024]{2,1,0:T(8,128)} custom-call(bf16[16,4,2,16,1024]{4,3,2,1,0:T(8,128)(2,1)} %all-to-all-done.3.in_ref, bf16[8,32,16,1024]{3,2,1,0:T(8,128)(2,1)} %map_ref.7, bf16[256,256]{1,0:T(8,128)(2,1)} %constant.28.clone.kc_ref, bf16[256,256]{1,0:T(8,128)(2,1)} %constant.30.clone.ks_ref), custom_call_target="tpu_custom_call" | custom-call | tf_op jit(solution)/shard_map/pallas_call | solution.py:215
  186.9 42.2 %all-to-all-done.1.in_ref = bf16[16,4,2,16,1024]{4,3,2,1,0:T(8,128)(2,1)} async-done(((bf16[16,4,2,16,1024]{4,3,2,1,0:T(8,128)(2,1)}), bf16[16,4,2,16,1024]{4,3,2,1,0:T(8,128)(2,1)}, u32[]{:S(2)}, u32[]{:S(2)}) %all-to-all-start.1) | async-done | bytes 4194336 | tf_op jit(solution)/shard_map/all_to_all | solution.py:203
  229.1 8.6 %shard_map.114 = bf16[32,16,1024]{2,1,0:T(8,128)(2,1)} custom-call(bf16[16,4,2,16,1024]{4,3,2,1,0:T(8,128)(2,1)} %all-to-all-done.1.in_ref, bf16[8,32,16,1024]{3,2,1,0:T(8,128)(2,1)} %map_ref.7, bf16[256,256]{1,0:T(8,128)(2,1)} %constant.28.clone.kc_ref, bf16[256,256]{1,0:T(8,128)(2,1)} %constant.30.clone.ks_ref, f32[32,16,1024]{2,1,0:T(8,128)} %shard_map.113.refs_0_), custom_call_target="tpu_custom_call" | custom-call | tf_op jit(solution)/shard_map/pallas_call | solution.py:215
  237.6 23.6 %all_to_all.25 = bf16[8,4,16,1024]{3,2,1,0:T(8,128)(2,1)S(1)} all-to-all(bf16[8,4,16,1024]{3,2,1,0:T(8,128)(2,1)} %bitcast.1), channel_id=1, replica_groups=mesh['coil'=8,'pencil'=16] {'coil'}, dimensions={0} | all-to-all | bytes 2097152 | tf_op jit(solution)/shard_map/all_to_all | solution.py:231
  261.3 0.9 convert_reduce_fusion
  (8 shorter events, 0.0 us)
Async XLA Ops:
  0.0 68.9 %copy-start = (s32[32,256,4]{1,2,0:T(4,128)S(1)}, s32[32,256,4]{1,2,0:T(4,128)}, u32[]{:S(2)}) copy-start(s32[32,256,4]{1,2,0:T(4,128)} %param.13) | copy-start | bytes 393220
  7.4 56.9 %all-to-all-start.2 = ((bf16[16,4,2,16,1024]{4,3,2,1,0:T(8,128)(2,1)}), bf16[16,4,2,16,1024]{4,3,2,1,0:T(8,128)(2,1)}, u32[]{:S(2)}, u32[]{:S(2)}) async-start(bf16[16,4,2,16,1024]{4,3,2,1,0:T(8,128)(2,1)} %shard_map.111), calls=%async_computation.2 | async-start | bytes 8388608 | tf_op jit(solution)/shard_map/all_to_all | solution.py:185
  21.4 47.5 %copy-start.2 = (bf16[256,256]{1,0:T(8,128)(2,1)S(1)}, bf16[256,256]{1,0:T(8,128)(2,1)}, u32[]{:S(2)}) copy-start(bf16[256,256]{1,0:T(8,128)(2,1)} %constant.32.clone) | copy-start | bytes 393220
  21.4 48.4 %copy-start.1 = (bf16[512,512]{1,0:T(8,128)(2,1)S(1)}, bf16[512,512]{1,0:T(8,128)(2,1)}, u32[]{:S(2)}) copy-start(bf16[512,512]{1,0:T(8,128)(2,1)} %constant.27.clone) | copy-start | bytes 1572868
  21.4 48.5 %copy-start.4 = (bf16[256,256]{1,0:T(8,128)(2,1)S(1)}, bf16[256,256]{1,0:T(8,128)(2,1)}, u32[]{:S(2)}) copy-start(bf16[256,256]{1,0:T(8,128)(2,1)} %constant.31.clone) | copy-start | bytes 393220
  21.4 49.6 %copy-start.3 = (bf16[512,512]{1,0:T(8,128)(2,1)S(1)}, bf16[512,512]{1,0:T(8,128)(2,1)}, u32[]{:S(2)}) copy-start(bf16[512,512]{1,0:T(8,128)(2,1)} %constant.26.clone) | copy-start | bytes 1572868
  64.3 54.9 %all-to-all-start = ((bf16[16,4,2,16,1024]{4,3,2,1,0:T(8,128)(2,1)}), bf16[16,4,2,16,1024]{4,3,2,1,0:T(8,128)(2,1)}, u32[]{:S(2)}, u32[]{:S(2)}) async-start(bf16[16,4,2,16,1024]{4,3,2,1,0:T(8,128)(2,1)} %shard_map.109), calls=%async_computation | async-start | bytes 8388608 | tf_op jit(solution)/shard_map/all_to_all | solution.py:185
  119.2 54.9 %all-to-all-start.3 = ((bf16[16,4,2,16,1024]{4,3,2,1,0:T(8,128)(2,1)}), bf16[16,4,2,16,1024]{4,3,2,1,0:T(8,128)(2,1)}, u32[]{:S(2)}, u32[]{:S(2)}) async-start(bf16[16,4,2,16,1024]{4,3,2,1,0:T(8,128)(2,1)} %shard_map.112), calls=%async_computation.3 | async-start | bytes 8388608 | tf_op jit(solution)/shard_map/all_to_all | solution.py:203
  174.2 54.9 %all-to-all-start.1 = ((bf16[16,4,2,16,1024]{4,3,2,1,0:T(8,128)(2,1)}), bf16[16,4,2,16,1024]{4,3,2,1,0:T(8,128)(2,1)}, u32[]{:S(2)}, u32[]{:S(2)}) async-start(bf16[16,4,2,16,1024]{4,3,2,1,0:T(8,128)(2,1)} %shard_map.110), calls=%async_computation.1 | async-start | bytes 8388608 | tf_op jit(solution)/shard_map/all_to_all | solution.py:203

commit v13 on v12

--- a/solution.py
+++ b/solution.py
@@ -58,10 +58,11 @@
 PARAMS = pltpu.CompilerParams(vmem_limit_bytes=60 * 1024 * 1024)
 
 
-def forward_kernel(map_ref, obj_ref, kc_ref, ks_ref, out_ref):
+def forward_kernel(map_ref, obj_ref, k_ref, out_ref):
     depth, rows, width = map_ref.shape
     half = width // 2
-    band = kc_ref.shape[0] // depth
+    band = k_ref.shape[1] // depth
+    lines = depth * band
     maps = map_ref[...].astype(jnp.float32)
     obj = obj_ref[...].astype(jnp.float32)
     m_re, m_im = maps[..., :half], maps[..., half:]
@@ -70,8 +71,8 @@
     for h in range(rows // band):
         part = image[:, h * band : (h + 1) * band, :].reshape(depth * band, width)
         part = part.astype(jnp.bfloat16)
-        direct = dot32(kc_ref[...], part)
-        crossed = dot32(ks_ref[...], part)
+        both = dot32(k_ref[...], part)
+        direct, crossed = both[:lines], both[lines:]
         along_z = turn_add(direct, crossed, half).astype(jnp.bfloat16)
         out_ref[:, :, h * band : (h + 1) * band, :] = along_z.reshape(
             out_ref.shape[:2] + (band, width)
@@ -99,16 +100,17 @@
     out_ref[...] = result.reshape(out_ref.shape)
 
 
-def backward_kernel(first, last, in_ref, map_ref, kc_ref, ks_ref, *refs):
+def backward_kernel(first, last, in_ref, map_ref, k_ref, *refs):
     depth, rows, width = map_ref.shape
     half = width // 2
-    band = kc_ref.shape[0] // depth
+    band = k_ref.shape[1] // depth
+    lines = depth * band
     maps = map_ref[...].astype(jnp.float32)
     pieces = []
     for h in range(rows // band):
         part = in_ref[:, :, h * band : (h + 1) * band, :].reshape(depth * band, width)
-        direct = dot32(kc_ref[...], part)
-        crossed = dot32(ks_ref[...], part)
+        both = dot32(k_ref[...], part)
+        direct, crossed = both[:lines], both[lines:]
         back_x = turn_add(direct, crossed, half).astype(jnp.bfloat16).astype(jnp.float32)
         coil = maps[:, h * band : (h + 1) * band, :].reshape(depth * band, width)
         m_re, m_im = coil[:, :half], coil[:, half:]
@@ -152,8 +154,8 @@
     forward_x = readout_table(cos_x, sin_x)
     inverse_x = readout_table(cos_x, -sin_x)
     band = 8 if rows % 8 == 0 else rows
-    kc_f, ks_f = slice_tables(slices, -1.0, band)
-    kc_i, ks_i = slice_tables(slices, 1.0, band)
+    k_f = jnp.concatenate(slice_tables(slices, -1.0, band), axis=0)
+    k_i = jnp.concatenate(slice_tables(slices, 1.0, band), axis=0)
     cos_y, sin_y = complex_tables(lines)
     wf = block_table(cos_y, sin_y)
     wi = block_table(cos_y, -sin_y)
@@ -173,15 +175,14 @@
             in_specs=[
                 map_spec,
                 pl.BlockSpec((slices, rows, width), const3),
-                pl.BlockSpec((slices * band, slices * band), const2),
-                pl.BlockSpec((slices * band, slices * band), const2),
+                pl.BlockSpec((2 * slices * band, slices * band), const2),
             ],
             out_specs=pl.BlockSpec(
                 (pencils, None, depth, rows, width), lambda c: (0, c, 0, 0, 0)
             ),
             out_shape=jax.ShapeDtypeStruct((pencils, per, depth, rows, width), jnp.bfloat16),
             compiler_params=PARAMS,
-        )(coil_maps, object_image, kc_f, ks_f)
+        )(coil_maps, object_image, k_f)
         gathered = lax.all_to_all(split, "pencil", 0, 0, tiled=True)
         lined = pl.pallas_call(
             line_kernel,
@@ -202,12 +203,11 @@
         )(gathered, mask, forward_x, inverse_x, wf, wi)
         returned = lax.all_to_all(lined, "pencil", 0, 0, tiled=True)
         first, last = start == 0, start + per == coils
-        operands = [returned, coil_maps, kc_i, ks_i]
+        operands = [returned, coil_maps, k_i]
         in_specs = [
             pl.BlockSpec((pencils, None, depth, rows, width), lambda c: (0, c, 0, 0, 0)),
             map_spec,
-            pl.BlockSpec((slices * band, slices * band), const2),
-            pl.BlockSpec((slices * band, slices * band), const2),
+            pl.BlockSpec((2 * slices * band, slices * band), const2),
         ]
         if not first:
             operands.append(acc)

time: 263 us -> 263 us (level)
  no operation moved by 1% of the time
where the time goes in v13:
time: 263 us; the launch traced here: 262 us
  waiting for transfers between devices  136 us (52%)
  Pallas kernels  68.9 us (26%)
  blocking collectives  23.6 us (9%)
  starting transfers between devices  20.3 us (8%)
  other arithmetic  12 us (5%)
    all_to_all x2, waiting for transfers between devices, on_device(): returned = lax.all_to_all(lined, 'pencil', 0, 0, tiled=True)  73.6 us
    all_to_all x2, waiting for transfers between devices, on_device(): gathered = lax.all_to_all(split, 'pencil', 0, 0, tiled=True)  62.6 us
    pallas_call x2, Pallas kernels, on_device(): pl.pallas_call(line_kernel, grid=(per, depth), in_specs=[pl.BlockSpec((pe...  37.8 us
    all_to_all x1, blocking collectives, on_device(): parts = lax.all_to_all(parts, 'coil', 0, 0, tiled=True)  23.6 us
    pallas_call x2, Pallas kernels, on_device(): pl.pallas_call(functools.partial(backward_kernel, first, last), grid=(per...  16.7 us
    pallas_call x2, Pallas kernels, on_device(): pl.pallas_call(forward_kernel, grid=(per,), in_specs=[map_spec, pl.BlockS...  14.4 us
    all_to_all x2, starting transfers between devices, on_device(): gathered = lax.all_to_all(split, 'pencil', 0, 0, tiled=True)  11 us
    concatenate x1, other arithmetic, readout_table(): return jnp.concatenate([upper, lower], axis=0)  9.99 us
  transfers between devices with their start and end apart: 4, of which 4 were waited for; matrix products, arithmetic and copies ran while one was open for 5% of the time, Pallas kernels for 20%

profile of v13, /device:TPU:0, one launch (start us, length us, event | category | flops | bytes accessed | tf_op | source)
XLA Modules:
  0.0 262.0 jit_solution(4020429441091904112)
XLA Ops:
  0.0 0.0 copy-start
  0.0 7.2 %shard_map.111 = bf16[16,4,2,16,1024]{4,3,2,1,0:T(8,128)(2,1)} custom-call(bf16[8,32,16,1024]{3,2,1,0:T(8,128)(2,1)} %map_ref.7, bf16[32,16,1024]{2,1,0:T(8,128)(2,1)} %obj_ref.3, bf16[512,256]{1,0:T(8,128)(2,1)} %constant.33.k_ref), custom_call_target="tpu_custom_call" | custom-call | tf_op jit(solution)/shard_map/pallas_call | solution.py:172
  7.2 6.5 %all-to-all-start.2 = ((bf16[16,4,2,16,1024]{4,3,2,1,0:T(8,128)(2,1)}), bf16[16,4,2,16,1024]{4,3,2,1,0:T(8,128)(2,1)}, u32[]{:S(2)}, u32[]{:S(2)}) async-start(bf16[16,4,2,16,1024]{4,3,2,1,0:T(8,128)(2,1)} %shard_map.111), calls=%async_computation.2 | async-start | bytes 8388608 | tf_op jit(solution)/shard_map/all_to_all | solution.py:186
  13.7 7.2 %shard_map.109 = bf16[16,4,2,16,1024]{4,3,2,1,0:T(8,128)(2,1)} custom-call(bf16[8,32,16,1024]{3,2,1,0:T(8,128)(2,1)} %map_ref.7, bf16[32,16,1024]{2,1,0:T(8,128)(2,1)} %obj_ref.3, bf16[512,256]{1,0:T(8,128)(2,1)} %constant.33.k_ref), custom_call_target="tpu_custom_call" | custom-call | tf_op jit(solution)/shard_map/pallas_call | solution.py:172
  20.9 0.0 copy-start.3
  20.9 43.1 %all-to-all-done.2.in_ref = bf16[16,4,2,16,1024]{4,3,2,1,0:T(8,128)(2,1)} async-done(((bf16[16,4,2,16,1024]{4,3,2,1,0:T(8,128)(2,1)}), bf16[16,4,2,16,1024]{4,3,2,1,0:T(8,128)(2,1)}, u32[]{:S(2)}, u32[]{:S(2)}) %all-to-all-start.2) | async-done | bytes 4194336 | tf_op jit(solution)/shard_map/all_to_all | solution.py:186
  64.1 4.5 %all-to-all-start = ((bf16[16,4,2,16,1024]{4,3,2,1,0:T(8,128)(2,1)}), bf16[16,4,2,16,1024]{4,3,2,1,0:T(8,128)(2,1)}, u32[]{:S(2)}, u32[]{:S(2)}) async-start(bf16[16,4,2,16,1024]{4,3,2,1,0:T(8,128)(2,1)} %shard_map.109), calls=%async_computation | async-start | bytes 8388608 | tf_op jit(solution)/shard_map/all_to_all | solution.py:186
  68.6 0.0 copy-done.2
  68.7 0.0 copy-done
  68.7 0.9 copy.13.mask_ref
  69.6 0.1 neg.4
  69.7 1.0 fusion.3
  70.7 10.0 %fusion.1 = (bf16[1024,1024]{1,0:T(8,128)(2,1)}, bf16[1024,1024]{1,0:T(8,128)(2,1)}) fusion(bf16[512,512]{1,0:T(8,128)(2,1)S(1)} %copy-done.3, bf16[512,512]{1,0:T(8,128)(2,1)S(1)} %copy-done.1, bf16[512,512]{1,0:T(8,128)(2,1)S(1)} %neg.4), kind=kLoop, calls=%fused_computation.5 | loop fusion | flops 14680064 | bytes 5767168 | tf_op jit(solution)/shard_map/concatenate | solution.py:32
  80.7 18.9 %shard_map.112 = bf16[16,4,2,16,1024]{4,3,2,1,0:T(8,128)(2,1)} custom-call(bf16[16,4,2,16,1024]{4,3,2,1,0:T(8,128)(2,1)} %all-to-all-done.2.in_ref, s32[2,256,4]{2,1,0:T(8,128)} %copy.13.mask_ref, bf16[1024,1024]{1,0:T(8,128)(2,1)} %get-tuple-element.14.fx_ref, bf16[1024,1024]{1,0:T(8,128)(2,1)} %get-tuple-element.13.fxi_ref, ...), custom_call_target="tpu_custom_call" | custom-call | tf_op jit(solution)/shard_map/pallas_call | solution.py:187
  99.6 19.4 %all-to-all-done.in_ref = bf16[16,4,2,16,1024]{4,3,2,1,0:T(8,128)(2,1)} async-done(((bf16[16,4,2,16,1024]{4,3,2,1,0:T(8,128)(2,1)}), bf16[16,4,2,16,1024]{4,3,2,1,0:T(8,128)(2,1)}, u32[]{:S(2)}, u32[]{:S(2)}) %all-to-all-start) | async-done | bytes 4194336 | tf_op jit(solution)/shard_map/all_to_all | solution.py:186
  119.0 4.5 %all-to-all-start.3 = ((bf16[16,4,2,16,1024]{4,3,2,1,0:T(8,128)(2,1)}), bf16[16,4,2,16,1024]{4,3,2,1,0:T(8,128)(2,1)}, u32[]{:S(2)}, u32[]{:S(2)}) async-start(bf16[16,4,2,16,1024]{4,3,2,1,0:T(8,128)(2,1)} %shard_map.112), calls=%async_computation.3 | async-start | bytes 8388608 | tf_op jit(solution)/shard_map/all_to_all | solution.py:204
  123.5 18.9 %shard_map.110 = bf16[16,4,2,16,1024]{4,3,2,1,0:T(8,128)(2,1)} custom-call(bf16[16,4,2,16,1024]{4,3,2,1,0:T(8,128)(2,1)} %all-to-all-done.in_ref, s32[2,256,4]{2,1,0:T(8,128)} %copy.13.mask_ref, bf16[1024,1024]{1,0:T(8,128)(2,1)} %get-tuple-element.14.fx_ref, bf16[1024,1024]{1,0:T(8,128)(2,1)} %get-tuple-element.13.fxi_ref, ...), custom_call_target="tpu_custom_call" | custom-call | tf_op jit(solution)/shard_map/pallas_call | solution.py:187
  142.4 31.5 %all-to-all-done.3.in_ref = bf16[16,4,2,16,1024]{4,3,2,1,0:T(8,128)(2,1)} async-done(((bf16[16,4,2,16,1024]{4,3,2,1,0:T(8,128)(2,1)}), bf16[16,4,2,16,1024]{4,3,2,1,0:T(8,128)(2,1)}, u32[]{:S(2)}, u32[]{:S(2)}) %all-to-all-start.3) | async-done | bytes 4194336 | tf_op jit(solution)/shard_map/all_to_all | solution.py:204
  173.9 4.7 %all-to-all-start.1 = ((bf16[16,4,2,16,1024]{4,3,2,1,0:T(8,128)(2,1)}), bf16[16,4,2,16,1024]{4,3,2,1,0:T(8,128)(2,1)}, u32[]{:S(2)}, u32[]{:S(2)}) async-start(bf16[16,4,2,16,1024]{4,3,2,1,0:T(8,128)(2,1)} %shard_map.110), calls=%async_computation.1 | async-start | bytes 8388608 | tf_op jit(solution)/shard_map/all_to_all | solution.py:204
  178.6 8.1 %shard_map.113.refs_0_ = f32[32,16,1024]{2,1,0:T(8,128)} custom-call(bf16[16,4,2,16,1024]{4,3,2,1,0:T(8,128)(2,1)} %all-to-all-done.3.in_ref, bf16[8,32,16,1024]{3,2,1,0:T(8,128)(2,1)} %map_ref.7, bf16[512,256]{1,0:T(8,128)(2,1)} %constant.34.k_ref), custom_call_target="tpu_custom_call" | custom-call | tf_op jit(solution)/shard_map/pallas_call | solution.py:215
  186.7 42.1 %all-to-all-done.1.in_ref = bf16[16,4,2,16,1024]{4,3,2,1,0:T(8,128)(2,1)} async-done(((bf16[16,4,2,16,1024]{4,3,2,1,0:T(8,128)(2,1)}), bf16[16,4,2,16,1024]{4,3,2,1,0:T(8,128)(2,1)}, u32[]{:S(2)}, u32[]{:S(2)}) %all-to-all-start.1) | async-done | bytes 4194336 | tf_op jit(solution)/shard_map/all_to_all | solution.py:204
  228.8 8.6 %shard_map.114 = bf16[32,16,1024]{2,1,0:T(8,128)(2,1)} custom-call(bf16[16,4,2,16,1024]{4,3,2,1,0:T(8,128)(2,1)} %all-to-all-done.1.in_ref, bf16[8,32,16,1024]{3,2,1,0:T(8,128)(2,1)} %map_ref.7, bf16[512,256]{1,0:T(8,128)(2,1)} %constant.34.k_ref, f32[32,16,1024]{2,1,0:T(8,128)} %shard_map.113.refs_0_), custom_call_target="tpu_custom_call" | custom-call | tf_op jit(solution)/shard_map/pallas_call | solution.py:215
  237.4 23.6 %all_to_all.25 = bf16[8,4,16,1024]{3,2,1,0:T(8,128)(2,1)S(1)} all-to-all(bf16[8,4,16,1024]{3,2,1,0:T(8,128)(2,1)} %bitcast.1), channel_id=1, replica_groups=mesh['coil'=8,'pencil'=16] {'coil'}, dimensions={0} | all-to-all | bytes 2097152 | tf_op jit(solution)/shard_map/all_to_all | solution.py:231
  261.1 0.9 convert_reduce_fusion
  (8 shorter events, 0.0 us)
Async XLA Ops:
  0.0 68.7 %copy-start = (s32[32,256,4]{1,2,0:T(4,128)S(1)}, s32[32,256,4]{1,2,0:T(4,128)}, u32[]{:S(2)}) copy-start(s32[32,256,4]{1,2,0:T(4,128)} %param.13) | copy-start | bytes 393220
  7.2 56.9 %all-to-all-start.2 = ((bf16[16,4,2,16,1024]{4,3,2,1,0:T(8,128)(2,1)}), bf16[16,4,2,16,1024]{4,3,2,1,0:T(8,128)(2,1)}, u32[]{:S(2)}, u32[]{:S(2)}) async-start(bf16[16,4,2,16,1024]{4,3,2,1,0:T(8,128)(2,1)} %shard_map.111), calls=%async_computation.2 | async-start | bytes 8388608 | tf_op jit(solution)/shard_map/all_to_all | solution.py:186
  20.9 47.7 %copy-start.2 = (bf16[256,256]{1,0:T(8,128)(2,1)S(1)}, bf16[256,256]{1,0:T(8,128)(2,1)}, u32[]{:S(2)}) copy-start(bf16[256,256]{1,0:T(8,128)(2,1)} %constant.32.clone) | copy-start | bytes 393220
  20.9 48.7 %copy-start.1 = (bf16[512,512]{1,0:T(8,128)(2,1)S(1)}, bf16[512,512]{1,0:T(8,128)(2,1)}, u32[]{:S(2)}) copy-start(bf16[512,512]{1,0:T(8,128)(2,1)} %constant.27.clone) | copy-start | bytes 1572868
  20.9 48.7 %copy-start.4 = (bf16[256,256]{1,0:T(8,128)(2,1)S(1)}, bf16[256,256]{1,0:T(8,128)(2,1)}, u32[]{:S(2)}) copy-start(bf16[256,256]{1,0:T(8,128)(2,1)} %constant.31.clone) | copy-start | bytes 393220
  20.9 49.8 %copy-start.3 = (bf16[512,512]{1,0:T(8,128)(2,1)S(1)}, bf16[512,512]{1,0:T(8,128)(2,1)}, u32[]{:S(2)}) copy-start(bf16[512,512]{1,0:T(8,128)(2,1)} %constant.26.clone) | copy-start | bytes 1572868
  64.1 54.9 %all-to-all-start = ((bf16[16,4,2,16,1024]{4,3,2,1,0:T(8,128)(2,1)}), bf16[16,4,2,16,1024]{4,3,2,1,0:T(8,128)(2,1)}, u32[]{:S(2)}, u32[]{:S(2)}) async-start(bf16[16,4,2,16,1024]{4,3,2,1,0:T(8,128)(2,1)} %shard_map.109), calls=%async_computation | async-start | bytes 8388608 | tf_op jit(solution)/shard_map/all_to_all | solution.py:186
  119.0 54.9 %all-to-all-start.3 = ((bf16[16,4,2,16,1024]{4,3,2,1,0:T(8,128)(2,1)}), bf16[16,4,2,16,1024]{4,3,2,1,0:T(8,128)(2,1)}, u32[]{:S(2)}, u32[]{:S(2)}) async-start(bf16[16,4,2,16,1024]{4,3,2,1,0:T(8,128)(2,1)} %shard_map.112), calls=%async_computation.3 | async-start | bytes 8388608 | tf_op jit(solution)/shard_map/all_to_all | solution.py:204
  173.9 54.9 %all-to-all-start.1 = ((bf16[16,4,2,16,1024]{4,3,2,1,0:T(8,128)(2,1)}), bf16[16,4,2,16,1024]{4,3,2,1,0:T(8,128)(2,1)}, u32[]{:S(2)}, u32[]{:S(2)}) async-start(bf16[16,4,2,16,1024]{4,3,2,1,0:T(8,128)(2,1)} %shard_map.110), calls=%async_computation.1 | async-start | bytes 8388608 | tf_op jit(solution)/shard_map/all_to_all | solution.py:204
